TPU v7x, 32 devices: a whole 2x2x4 slice. The times are simulated.
32 devices in a mesh: grp: 4 (over y, x), blk: 8 (over z, core).
Axes of the slice: x: 2, y: 2, z: 4, core: 2. Of those that a mesh axis runs over, the one named last changes fastest.
Arguments:
- voltages: bfloat16 [4096, 188416], P(('blk', 'grp')), may hold values from -6 to 6
- filter_taps: float32 [8, 8192], replicated, may hold values from -0.0234375 to 0.0234375
- channel_index: int32 [16], replicated, may hold values from 0 to 4095
- antenna_slot_order: int32 [2048], replicated, may hold values from 0 to 2047, each once
Outputs:
- visibilities: bfloat16 [16, 4096, 2, 4096], P('grp', 'blk')
All inputs are finite; a program needn't handle non-finite values.
Results may differ from a plain program's by a relative error of at most 0.0065.
Values sent between devices are 32-bit elements; how exact they have to be, the bound alone decides.
No kernel may reach another device: no remote copies, remote signals or barrier semaphores. Data moves between devices by JAX's collectives and lax.ppermute only.
A program may use at most 192 MiB of HBM per device.

v0:
```python
import math

import jax
import jax.numpy as jnp
from jax import lax
from jax.sharding import PartitionSpec as P


def phase_table(channel_index, fft_length):
    samples_idx = jnp.arange(fft_length, dtype=jnp.int32)
    phase = samples_idx[:, None] * channel_index[None, :] % fft_length
    angle = phase.astype(jnp.float32) * jnp.float32(2.0 * math.pi / fft_length)
    return jnp.concatenate([jnp.cos(angle), -jnp.sin(angle)], axis=1).astype(jnp.bfloat16)


def channelize(voltages, filter_taps, channel_index):
    tap_count, fft_length = filter_taps.shape
    row_count = voltages.shape[0]
    frame_count = voltages.shape[1] // fft_length
    spectra = frame_count - tap_count + 1
    blocked = voltages.reshape(row_count, frame_count, fft_length)
    filtered = jnp.zeros((row_count, spectra, fft_length), jnp.float32)
    for tap_index in range(tap_count):
        filtered = filtered + filter_taps[tap_index][None, None, :] * blocked[
            :, tap_index : tap_index + spectra, :
        ].astype(jnp.float32)
    twiddle = phase_table(channel_index, fft_length)
    spectrum = jnp.dot(
        filtered.astype(jnp.bfloat16).reshape(row_count * spectra, fft_length),
        twiddle,
        preferred_element_type=jnp.float32,
    )
    chan_count = channel_index.shape[0]
    return (
        spectrum.reshape(row_count, spectra, 2, chan_count)
        .transpose(3, 2, 1, 0)
        .reshape(chan_count, 2 * spectra, row_count)
    )


def column_index(antenna_slot_order):
    count = antenna_slot_order.shape[0]
    inverse = (
        jnp.zeros((count,), jnp.int32)
        .at[antenna_slot_order]
        .set(jnp.arange(count, dtype=jnp.int32))
    )
    column_entry = jnp.arange(2 * count, dtype=jnp.int32)
    return 2 * inverse[column_entry // 2] + column_entry % 2


def stacked_rows(block):
    half = block.shape[1] // 2
    turned = jnp.concatenate([block[:, half:], -block[:, :half]], axis=1)
    return jnp.stack([block, turned], axis=1)


def correlate(lhs, cols):
    return jnp.einsum(
        "cpkr,ckn->crpn",
        lhs,
        cols,
        precision=lax.Precision.HIGHEST,
        preferred_element_type=jnp.float32,
    )


def per_device(voltages, filter_taps, channel_index, antenna_slot_order):
    local = channelize(voltages, filter_taps, channel_index)
    scale = jnp.float32(1.0 / (local.shape[1] // 2))
    columns = column_index(antenna_slot_order)
    turned = lax.all_to_all(local, "grp", split_axis=0, concat_axis=2, tiled=True)
    lhs = stacked_rows(turned)
    everything = lax.all_gather(turned, "blk", axis=2, tiled=True)
    ordered = jnp.take(everything, columns, axis=2)
    result = (correlate(lhs, ordered) * scale).astype(jnp.bfloat16)
    return result


def solution(mesh):
    in_specs = (P(("blk", "grp"), None), P(), P(), P())
    out_specs = P("grp", "blk", None, None)
    return jax.shard_map(
        per_device, mesh=mesh, in_specs=in_specs, out_specs=out_specs, check_vma=False
    )
```

profile of v0, /device:TPU:0, one launch (start us, length us, event | category | flops | bytes accessed | tf_op | source)
XLA Modules:
  0.0 413.1 jit_solution(9023769274649659987)
XLA Ops:
  6.5 0.0 all-gather.2.cloned.1.call-start
  6.5 2.3 fusion.25
  8.9 3.2 cosine_convert_fusion
  12.1 62.3 %copy.14 = bf16[128,188416]{0,1:T(8,128)(2,1)} copy(bf16[128,188416]{1,0:T(8,128)(2,1)} %param.4) | data formatting | bytes 96468992 | tf_op args[0]
  74.4 0.0 copy-start
  74.4 91.6 %fusion.4 = f32[16,2,16,128]{3,0,1,2:T(8,128)S(1)} fusion(bf16[2,16,8192,1]{2,1,0,3:T(8,128)(2,1)S(1)} %bitcast.55, bf16[128,23,8192]{0,2,1:T(8,128)(2,1)} %bitcast.49, f32[8192]{0:T(1024)S(1)} %bitcast.65, f32[8192]{0:T(1024)S(1)} %bitcast.66, f32[8192]{0:T(1024)S(1)} %bitcast.60, f32[8192]{0:T(1024)S(1)} %bitcast.61, f32[8192]{0:T(1024)S(1)} %bitcast.62, ...), kind=kOutput, calls=%fused_computation.10 | convolution fusion | flops 1476395008 | bytes 269484032 | tf_op jit(solution)/shard_map/dot_general | solution.py:28
  166.0 0.2 copy.16
  166.2 10.7 %all_to_all.18 = f32[16,32,128]{2,1,0:T(8,128)S(1)} all-to-all(f32[16,32,128]{2,1,0:T(8,128)S(1)} %bitcast.54), channel_id=1, replica_groups=mesh['grp'=4,'blk'=8] {'grp'}, dimensions={0} | all-to-all | bytes 524288 | tf_op jit(solution)/shard_map/all_to_all | solution.py:72
  176.9 0.7 copy.33
  177.6 0.0 all-gather.2.cloned.1.call-update
  177.7 0.0 copy-done
  177.7 8.2 %scatter_custom_fusion = s32[2048]{0:T(1024)S(1)} fusion(s32[2048]{0:T(1024)S(1)} %compare_select_fusion.3, s32[2048]{0:T(1024)S(1)} %iota.16, s32[]{:T(128)} %constant.59.clone.1), kind=kCustom, calls=%fused_computation.49 | custom fusion | bytes 8196 | tf_op jit(solution)/shard_map/scatter | solution.py:46
  186.0 23.0 %gather_fusion = s32[4096]{0:T(1024)S(1)} fusion(s32[2048]{0:T(1024)S(1)} %scatter_custom_fusion, s32[4096]{0:T(1024)S(1)} %broadcast_clamp_fusion.1), kind=kCustom, calls=%fused_computation | custom fusion | bytes 49152 | tf_op jit(solution)/shard_map/gather | solution.py:49
  209.1 0.2 copy.17
  209.3 0.1 stack.9
  209.4 1.0 fusion.24
  210.4 0.0 all-gather.2.cloned.1.call-done
  210.4 7.2 %copy.18 = f32[4,32,4096]{1,0,2:T(4,128)} copy(f32[4,32,4096]{2,1,0:T(8,128)} %all-gather.2.cloned.1.call-done) | data formatting | bytes 4194304 | tf_op jit(solution)/shard_map/all_gather | solution.py:74
  217.6 33.3 %gather_fusion.1 = f32[4096,4,32]{2,1,0:T(4,128)} fusion(f32[4,32,4096]{1,0,2:T(4,128)} %copy.18, s32[4096]{0:T(1024)S(1)} %broadcast_clamp_fusion), kind=kCustom, calls=%fused_computation.1 | custom fusion | bytes 4210688 | tf_op jit(solution)/shard_map/jit(_take)/gather | solution.py:75
  251.0 16.4 %select_bitcast_fusion = f32[4,32,4096,1]{1,0,2,3:T(4,128)S(1)} fusion(f32[4096,4,32]{2,1,0:T(4,128)} %gather_fusion.1, pred[4096]{0:T(1024)(128)(4,1)S(1)} %compare_and_fusion), kind=kLoop, calls=%fused_computation.9 | loop fusion | flops 524288 | bytes 4198400 | tf_op jit(solution)/shard_map/jit(_take)/select_n | solution.py:75
  267.3 57.2 %fusion.2 = bf16[4,512,2,4096]{1,3,2,0:T(8,128)(2,1)} fusion(f32[4,32,4096,1]{1,0,2,3:T(4,128)S(1)} %select_bitcast_fusion, f32[4,1,32,512]{3,2,1,0:T(8,128)S(1)} %maximum_bitcast_fusion, f32[4,1,32,512]{3,2,1,0:T(8,128)S(1)} %stack.9), kind=kOutput, calls=%fused_computation.7 | convolution fusion | flops 6476136448 | bytes 36175872 | tf_op jit(solution)/shard_map/cpkr,ckn->crpn/dot_general | solution.py:59
  324.5 81.8 %copy.21 = bf16[4,512,2,4096]{3,2,1,0:T(2,128)(2,1)} copy(bf16[4,512,2,4096]{1,3,2,0:T(8,128)(2,1)} %fusion.2) | data formatting | bytes 67108864 | tf_op jit(solution)/shard_map/convert_element_type | solution.py:76
  (10 shorter events, 0.1 us)
Async XLA Ops:
  6.5 203.9 %all-gather.2.cloned.1.call-start = ((), (), s32[]{:S(2)}) async-start(), calls=%async_computation.1 | async-start | bytes 2359296 | tf_op jit(solution)/shard_map/all_gather | solution.py:74
  74.4 103.2 %copy-start = (s32[2048]{0:T(1024)S(1)}, s32[2048]{0:T(1024)}, u32[]{:S(2)}) copy-start(s32[2048]{0:T(1024)} %param.7) | copy-start | bytes 24580
Sparse Core Ops, SparseCore 0:
  177.8 28.8 all-gather.1
where the time goes:
time: 417 us; the launch traced here: 413 us
  local copies, waits for them, and re-layouts  219 us (53%)
  matrix products  149 us (36%)
  other arithmetic  20.7 us (5%)
  between operations  13.6 us (3%)
  blocking collectives  10.7 us (3%)
    dot_general x1, matrix products, channelize(): jnp.dot(filtered.astype(jnp.bfloat16).reshape(row_count * spectra, fft_le...  91.6 us
    convert_element_type x1, local copies, waits for them, and re-layouts, per_device(): result = (correlate(lhs, ordered) * scale).astype(jnp.bfloat16)  81.8 us
    unnamed x3, local copies, waits for them, and re-layouts  62.3 us
    dot_general x1, matrix products, correlate(): jnp.einsum('cpkr,ckn->crpn', lhs, cols, precision=lax.Precision.HIGHEST,...  57.2 us
    gather x1, local copies, waits for them, and re-layouts, per_device(): ordered = jnp.take(everything, columns, axis=2)  33.3 us
    gather x1, local copies, waits for them, and re-layouts, column_index(): return 2 * inverse[column_entry // 2] + column_entry % 2  23 us
    select_n x2, other arithmetic, per_device(): ordered = jnp.take(everything, columns, axis=2)  16.4 us
    all_to_all x1, blocking collectives, per_device(): lax.all_to_all(local, 'grp', split_axis=0, concat_axis=2, tiled=True)  10.7 us
  transfers between devices with their start and end apart: 1, of which 0 were waited for; matrix products, arithmetic and copies ran while one was open for 8% of the time, Pallas kernels for 0%

commit v1 on v0

v1 whole, which is shorter than its diff:
```python
import math

import jax
import jax.numpy as jnp
from jax import lax
from jax.experimental import pallas as pl
from jax.experimental.pallas import tpu as pltpu
from jax.sharding import PartitionSpec as P


def phase_table(channel_index, fft_length):
    samples_idx = jnp.arange(fft_length, dtype=jnp.int32)
    phase = samples_idx[:, None] * channel_index[None, :] % fft_length
    angle = phase.astype(jnp.float32) * jnp.float32(2.0 * math.pi / fft_length)
    return jnp.concatenate([jnp.cos(angle), -jnp.sin(angle)], axis=1).astype(jnp.bfloat16)


def _frame_kernel(v_ref, w_ref, o_ref):
    o_ref[0] = jnp.dot(v_ref[...], w_ref[...], preferred_element_type=jnp.float32)


def frame_products(voltages, weights, fft_length):
    rows, samples = voltages.shape
    frames = samples // fft_length
    width = weights.shape[1]
    return pl.pallas_call(
        _frame_kernel,
        grid=(frames,),
        in_specs=[
            pl.BlockSpec((rows, fft_length), lambda f: (0, f)),
            pl.BlockSpec((fft_length, width), lambda f: (0, 0)),
        ],
        out_specs=pl.BlockSpec((1, rows, width), lambda f: (f, 0, 0)),
        out_shape=jax.ShapeDtypeStruct((frames, rows, width), jnp.float32),
        compiler_params=pltpu.CompilerParams(vmem_limit_bytes=48 * 1024 * 1024),
    )(voltages, weights)


def channelize(voltages, filter_taps, channel_index):
    tap_count, fft_length = filter_taps.shape
    frame_count = voltages.shape[1] // fft_length
    spectra = frame_count - tap_count + 1
    twiddle = phase_table(channel_index, fft_length).astype(jnp.float32)
    cols = twiddle.shape[1]
    weights = (filter_taps[:, :, None] * twiddle[None, :, :]).astype(jnp.bfloat16)
    weights = weights.transpose(1, 0, 2).reshape(fft_length, tap_count * cols)
    prod = frame_products(voltages, weights, fft_length)
    spec = prod[0:spectra, :, 0:cols]
    for m in range(1, tap_count):
        spec = spec + prod[m : m + spectra, :, m * cols : (m + 1) * cols]
    return spec


def column_index(antenna_slot_order):
    count = antenna_slot_order.shape[0]
    ids = jnp.arange(count, dtype=jnp.int32)
    inverse = jnp.sum(
        jnp.where(antenna_slot_order[None, :] == ids[:, None], ids[None, :], 0), axis=1
    )
    column_entry = jnp.arange(2 * count, dtype=jnp.int32)
    return 2 * inverse[column_entry // 2] + column_entry % 2


def split2(x):
    hi = x.astype(jnp.bfloat16)
    lo = (x - hi.astype(jnp.float32)).astype(jnp.bfloat16)
    return hi, lo


def _corr_kernel(l0_ref, l1_ref, o_ref, out_ref):
    rhs = o_ref[0]
    r0 = jnp.dot(l0_ref[0], rhs, preferred_element_type=jnp.float32)
    r1 = jnp.dot(l1_ref[0], rhs, preferred_element_type=jnp.float32)
    out_ref[0] = jnp.stack([r0, r1], axis=1).astype(out_ref.dtype)


def correlate(l0, l1, rhs, block_rows):
    chans, slots, width = l0.shape
    cols = rhs.shape[2]
    return pl.pallas_call(
        _corr_kernel,
        grid=(chans, slots // block_rows),
        in_specs=[
            pl.BlockSpec((1, block_rows, width), lambda c, s: (c, s, 0)),
            pl.BlockSpec((1, block_rows, width), lambda c, s: (c, s, 0)),
            pl.BlockSpec((1, width, cols), lambda c, s: (c, 0, 0)),
        ],
        out_specs=pl.BlockSpec((1, block_rows, 2, cols), lambda c, s: (c, s, 0, 0)),
        out_shape=jax.ShapeDtypeStruct((chans, slots, 2, cols), jnp.bfloat16),
        compiler_params=pltpu.CompilerParams(vmem_limit_bytes=48 * 1024 * 1024),
    )(l0, l1, rhs)


def per_device(voltages, filter_taps, channel_index, antenna_slot_order):
    spec = channelize(voltages, filter_taps, channel_index)
    spectra, rows, cols = spec.shape
    chans = cols // 2
    grp = lax.psum(1, "grp")
    local_ch = chans // grp
    x = spec.reshape(spectra, rows, 2, chans).transpose(1, 3, 2, 0)
    x = lax.all_to_all(x, "grp", split_axis=1, concat_axis=0, tiled=True)
    slots_local = x.shape[0]
    x = x.reshape(slots_local, local_ch * 2 * spectra)
    everything = lax.all_gather(x, "blk", axis=0, tiled=True)
    columns = column_index(antenna_slot_order)
    ordered = jnp.take(everything, columns, axis=0)
    ordered = ordered.reshape(-1, local_ch, 2 * spectra).transpose(1, 0, 2)
    scale = jnp.float32(1.0 / spectra)
    xl = x.reshape(slots_local, local_ch, 2, spectra).transpose(1, 0, 2, 3) * scale
    re = xl[:, :, 0, :]
    im = xl[:, :, 1, :]
    row0 = jnp.concatenate([re, im], axis=-1)
    row1 = jnp.concatenate([im, -re], axis=-1)
    r0a, r0b = split2(row0)
    r1a, r1b = split2(row1)
    o1, o2 = split2(ordered)
    l0 = jnp.concatenate([r0a, r0a, r0b], axis=-1)
    l1 = jnp.concatenate([r1a, r1a, r1b], axis=-1)
    rhs = jnp.concatenate([o1, o2, o1], axis=-1).transpose(0, 2, 1)
    result = correlate(l0, l1, rhs, min(128, slots_local))
    return result


def solution(mesh):
    in_specs = (P(("blk", "grp"), None), P(), P(), P())
    out_specs = P("grp", "blk", None, None)
    return jax.shard_map(
        per_device, mesh=mesh, in_specs=in_specs, out_specs=out_specs, check_vma=False
    )
```

time: 417 us -> 185 us (0.44)
  local copies, waits for them, and re-layouts: 219 us -> 50.5 us
  matrix products: 149 us -> 0 us
  Pallas kernels: 0 us -> 95.5 us
  blocking collectives: 10.7 us -> 0 us
  other arithmetic: 20.7 us -> 12.4 us
  waiting for transfers between devices: 0.04 us -> 7.22 us
  starting transfers between devices: 0.01 us -> 5.19 us
    dot_general x2 -> x0, matrix products: 149 us -> none  [the longest x1 91.6 us: channelize(): jnp.dot(filtered.astype(jnp.bfloat16).reshape(row_count * spectra, fft_le...]
    pallas_call x0 -> x2, Pallas kernels: none -> 95.5 us  [the longest x1 65.5 us: correlate(): pl.pallas_call(_corr_kernel, grid=(chans, slots // block_rows), in_specs=...]
    convert_element_type x1 -> x3, local copies, waits for them, and re-layouts: 81.8 us -> 6.92 us  [the longest x1 6.37 us: channelize(): (filter_taps[:, :, None] * twiddle[None, :, :]).astype(jnp.bfloat16)]
    unnamed x3, local copies, waits for them, and re-layouts: 62.3 us -> 0.03 us
    select_n x3 -> x1, other arithmetic: 16.4 us -> 0.03 us  [per_device(): ordered = jnp.take(everything, columns, axis=0)]
    gather x1 -> x2, local copies, waits for them, and re-layouts: 33.3 us -> 17.7 us  [per_device(): ordered = jnp.take(everything, columns, axis=0)]
    all_to_all x1 -> x0, blocking collectives: 10.7 us -> none  [per_device(): lax.all_to_all(local, 'grp', split_axis=0, concat_axis=2, tiled=True)]
    scatter x1 -> x0, local copies, waits for them, and re-layouts: 8.23 us -> none  [column_index(): inverse = jnp.zeros((count,), jnp.int32).at[antenna_slot_order].set(jnp.a...]
  transfers between devices with their start and end apart: 1 -> 2, of which waited for: 0 -> 2; matrix products, arithmetic and copies ran while one was open for 8% -> 15% of each run, Pallas kernels for 0% -> 0%
where the time goes in v1:
time: 185 us; the launch traced here: 184 us
  Pallas kernels  95.5 us (52%)
  local copies, waits for them, and re-layouts  50.5 us (27%)
  between operations  13.6 us (7%)
  other arithmetic  12.4 us (7%)
  waiting for transfers between devices  7.22 us (4%)
  starting transfers between devices  5.19 us (3%)
    pallas_call x1, Pallas kernels, correlate(): pl.pallas_call(_corr_kernel, grid=(chans, slots // block_rows), in_specs=...  65.5 us
    pallas_call x1, Pallas kernels, frame_products(): pl.pallas_call(_frame_kernel, grid=(frames,), in_specs=[pl.BlockSpec((row...  30 us
    gather x1, local copies, waits for them, and re-layouts, column_index(): return 2 * inverse[column_entry // 2] + column_entry % 2  23 us
    gather x2, local copies, waits for them, and re-layouts, per_device(): ordered = jnp.take(everything, columns, axis=0)  17.7 us
    convert_element_type x1, local copies, waits for them, and re-layouts, channelize(): (filter_taps[:, :, None] * twiddle[None, :, :]).astype(jnp.bfloat16)  6.37 us
    all_to_all x1, waiting for transfers between devices, per_device(): x = lax.all_to_all(x, 'grp', split_axis=1, concat_axis=0, tiled=True)  5.34 us
    all_to_all x1, starting transfers between devices, per_device(): x = lax.all_to_all(x, 'grp', split_axis=1, concat_axis=0, tiled=True)  5.18 us
  transfers between devices with their start and end apart: 2, of which 2 were waited for; matrix products, arithmetic and copies ran while one was open for 15% of the time, Pallas kernels for 0%

profile of v1, /device:TPU:0, one launch (start us, length us, event | category | flops | bytes accessed | tf_op | source)
XLA Modules:
  0.0 184.5 jit_solution(13298331509339404599)
XLA Ops:
  6.5 3.1 %cosine_convert_fusion = (bf16[8192,16]{0,1:T(8,128)(2,1)S(1)}, bf16[8192,16]{0,1:T(8,128)(2,1)S(1)}) fusion(s32[16]{0:T(128)} %param.6), kind=kLoop, calls=%fused_computation.28 | loop fusion | flops 2228224 | bytes 524352 | tf_op jit(solution)/shard_map/convert
  9.7 0.1 maximum_convert_fusion
  9.8 3.6 %multiply_convert_fusion = bf16[8192,8,32]{0,2,1:T(8,128)(2,1)} fusion(f32[8192,32]{0,1:T(8,128)S(1)} %maximum_convert_fusion, f32[8192,8]{0,1:T(8,128)} %bitcast.49), kind=kLoop, calls=%fused_computation.4 | loop fusion | flops 4194304 | bytes 5505024 | tf_op jit(solution)/shard_map/convert_element_type | solution.py:45
  13.4 6.4 %copy.50.w_ref = bf16[8192,256]{1,0:T(8,128)(2,1)} copy(bf16[8192,256]{0,1:T(8,128)(2,1)} %bitcast.43) | data formatting | bytes 8388608 | tf_op jit(solution)/shard_map/convert_element_type | solution.py:45
  19.7 30.0 %shard_map.46 = f32[23,128,256]{2,1,0:T(8,128)S(1)} custom-call(bf16[128,188416]{1,0:T(8,128)(2,1)} %v_ref.1, bf16[8192,256]{1,0:T(8,128)(2,1)} %copy.50.w_ref), custom_call_target="tpu_custom_call" | custom-call | tf_op jit(solution)/shard_map/pallas_call | solution.py:26
  49.8 1.7 slice_add_fusion
  51.5 0.0 copy-start
  51.5 0.3 copy.51
  51.8 0.8 copy.52
  52.6 5.2 %all-to-all-start = ((f32[128,16,2,16]{0,2,3,1:T(2,128)}), f32[128,16,2,16]{0,2,3,1:T(2,128)S(1)}, u32[]{:S(2)}, u32[]{:S(2)}) async-start(f32[128,16,2,16]{0,2,3,1:T(2,128)} %copy.52), calls=%async_computation | async-start | bytes 524288 | tf_op jit(solution)/shard_map/all_to_all | solution.py:101
  57.8 0.0 all-gather.2.cloned.1.call-start
  57.8 5.3 %all-to-all-done = f32[128,16,2,16]{0,2,3,1:T(2,128)S(1)} async-done(((f32[128,16,2,16]{0,2,3,1:T(2,128)}), f32[128,16,2,16]{0,2,3,1:T(2,128)S(1)}, u32[]{:S(2)}, u32[]{:S(2)}) %all-to-all-start) | async-done | bytes 262176 | tf_op jit(solution)/shard_map/all_to_all | solution.py:101
  63.2 0.2 copy.63
  63.4 0.8 copy.64
  64.2 0.0 all-gather.2.cloned.1.call-update
  64.3 1.8 select_reduce_fusion
  66.0 23.0 %gather_fusion = s32[4096]{0:T(1024)S(1)} fusion(s32[2048]{0:T(1024)S(1)} %select_reduce_fusion, s32[4096]{0:T(1024)S(1)} %broadcast_clamp_fusion.1), kind=kCustom, calls=%fused_computation | custom fusion | bytes 49152 | tf_op jit(solution)/shard_map/gather | solution.py:61
  89.3 0.3 copy.61
  89.6 0.3 copy.57
  89.8 0.1 pad_maximum_fusion.3
  89.9 0.3 copy.60
  90.2 0.3 copy.56
  90.6 0.1 subtract_convert_fusion
  90.7 0.1 subtract_convert_fusion.1
  90.8 1.0 pad_maximum_fusion
  91.8 1.9 %all-gather.2.cloned.1.call-done = f32[4096,128]{1,0:T(8,128)} async-done(((f32[512,128]{1,0:T(8,128)}), f32[4096,128]{1,0:T(8,128)}) %all-gather.2.cloned.1.call-update) | async-done | bytes 2097168 | tf_op jit(solution)/shard_map/all_gather | solution.py:104
  93.7 15.8 %gather_fusion.1 = f32[4096,128]{1,0:T(8,128)} fusion(f32[4096,128]{1,0:T(8,128)} %all-gather.2.cloned.1.call-done, s32[4096]{0:T(1024)S(1)} %broadcast_clamp_fusion), kind=kCustom, calls=%fused_computation.1 | custom fusion | bytes 4210688 | tf_op jit(solution)/shard_map/jit(_take)/gather | solution.py:106
  109.4 1.9 %copy.65 = f32[4096,128]{0,1:T(8,128)S(1)} copy(f32[4096,128]{1,0:T(8,128)} %gather_fusion.1) | data formatting | bytes 4194304 | tf_op jit(solution)/shard_map/jit(_take)/gather | solution.py:106
  111.4 0.2 fusion
  111.6 0.2 bitcast_convert_fusion
  111.7 0.4 maximum_bitcast_fusion.o_ref
  112.2 65.5 %shard_map.47 = bf16[4,512,2,4096]{3,2,1,0:T(2,128)(2,1)} custom-call(bf16[4,512,96]{2,1,0:T(8,128)(2,1)S(1)} %get-tuple-element.13.l0_ref, bf16[4,512,96]{2,1,0:T(8,128)(2,1)S(1)} %get-tuple-element.14.l1_ref, bf16[4,96,4096]{2,1,0:T(8,128)(2,1)S(1)} %maximum_bitcast_fusion.o_ref), custom_call_target="tpu_custom_call" | custom-call | tf_op jit(solution)/shard_map/pallas_call | solution.py:80
  (13 shorter events, 0.2 us)
Async XLA Ops:
  51.5 12.8 %copy-start = (s32[2048]{0:T(1024)S(1)}, s32[2048]{0:T(1024)}, u32[]{:S(2)}) copy-start(s32[2048]{0:T(1024)} %param.7) | copy-start | bytes 24580
  52.6 10.6 %all-to-all-start = ((f32[128,16,2,16]{0,2,3,1:T(2,128)}), f32[128,16,2,16]{0,2,3,1:T(2,128)S(1)}, u32[]{:S(2)}, u32[]{:S(2)}) async-start(f32[128,16,2,16]{0,2,3,1:T(2,128)} %copy.52), calls=%async_computation | async-start | bytes 524288 | tf_op jit(solution)/shard_map/all_to_all | solution.py:101
  57.8 35.8 %all-gather.2.cloned.1.call-start = ((), (), s32[]{:S(2)}) async-start(), calls=%async_computation.1 | async-start | bytes 2359296 | tf_op jit(solution)/shard_map/all_gather | solution.py:104
Sparse Core Ops, SparseCore 0:
  64.4 29.2 all-gather.1

commit v2 on v1

--- a/solution.py
+++ b/solution.py
@@ -16,23 +16,28 @@
 
 
 def _frame_kernel(v_ref, w_ref, o_ref):
-    o_ref[0] = jnp.dot(v_ref[...], w_ref[...], preferred_element_type=jnp.float32)
+    n = w_ref.shape[0]
+    group = o_ref.shape[0]
+    lhs = jnp.concatenate([v_ref[:, g * n : (g + 1) * n] for g in range(group)], axis=0)
+    res = jnp.dot(lhs, w_ref[...], preferred_element_type=jnp.float32)
+    o_ref[...] = res.reshape(o_ref.shape)
 
 
-def frame_products(voltages, weights, fft_length):
+def frame_products(voltages, weights, fft_length, group):
     rows, samples = voltages.shape
     frames = samples // fft_length
+    steps = -(-frames // group)
     width = weights.shape[1]
     return pl.pallas_call(
         _frame_kernel,
-        grid=(frames,),
+        grid=(steps,),
         in_specs=[
-            pl.BlockSpec((rows, fft_length), lambda f: (0, f)),
+            pl.BlockSpec((rows, group * fft_length), lambda f: (0, f)),
             pl.BlockSpec((fft_length, width), lambda f: (0, 0)),
         ],
-        out_specs=pl.BlockSpec((1, rows, width), lambda f: (f, 0, 0)),
-        out_shape=jax.ShapeDtypeStruct((frames, rows, width), jnp.float32),
-        compiler_params=pltpu.CompilerParams(vmem_limit_bytes=48 * 1024 * 1024),
+        out_specs=pl.BlockSpec((group, rows, width), lambda f: (f, 0, 0)),
+        out_shape=jax.ShapeDtypeStruct((steps * group, rows, width), jnp.float32),
+        compiler_params=pltpu.CompilerParams(vmem_limit_bytes=56 * 1024 * 1024),
     )(voltages, weights)
 
 
@@ -44,7 +49,7 @@
     cols = twiddle.shape[1]
     weights = (filter_taps[:, :, None] * twiddle[None, :, :]).astype(jnp.bfloat16)
     weights = weights.transpose(1, 0, 2).reshape(fft_length, tap_count * cols)
-    prod = frame_products(voltages, weights, fft_length)
+    prod = frame_products(voltages, weights, fft_length, 4)
     spec = prod[0:spectra, :, 0:cols]
     for m in range(1, tap_count):
         spec = spec + prod[m : m + spectra, :, m * cols : (m + 1) * cols]
@@ -57,8 +62,8 @@
     inverse = jnp.sum(
         jnp.where(antenna_slot_order[None, :] == ids[:, None], ids[None, :], 0), axis=1
     )
-    column_entry = jnp.arange(2 * count, dtype=jnp.int32)
-    return 2 * inverse[column_entry // 2] + column_entry % 2
+    pol = jnp.arange(2, dtype=jnp.int32)
+    return (2 * inverse[:, None] + pol[None, :]).reshape(2 * count)
 
 
 def split2(x):
@@ -67,28 +72,26 @@
     return hi, lo
 
 
-def _corr_kernel(l0_ref, l1_ref, o_ref, out_ref):
-    rhs = o_ref[0]
-    r0 = jnp.dot(l0_ref[0], rhs, preferred_element_type=jnp.float32)
-    r1 = jnp.dot(l1_ref[0], rhs, preferred_element_type=jnp.float32)
-    out_ref[0] = jnp.stack([r0, r1], axis=1).astype(out_ref.dtype)
+def _corr_kernel(l_ref, o_ref, out_ref):
+    res = jnp.dot(l_ref[0], o_ref[0], preferred_element_type=jnp.float32)
+    out_ref[0] = res.astype(out_ref.dtype).reshape(out_ref.shape[1:])
 
 
-def correlate(l0, l1, rhs, block_rows):
-    chans, slots, width = l0.shape
+def correlate(lhs, rhs, block_rows):
+    chans, slots, pairs, width = lhs.shape
     cols = rhs.shape[2]
+    lhs = lhs.reshape(chans, slots * pairs, width)
     return pl.pallas_call(
         _corr_kernel,
         grid=(chans, slots // block_rows),
         in_specs=[
-            pl.BlockSpec((1, block_rows, width), lambda c, s: (c, s, 0)),
-            pl.BlockSpec((1, block_rows, width), lambda c, s: (c, s, 0)),
+            pl.BlockSpec((1, block_rows * pairs, width), lambda c, s: (c, s, 0)),
             pl.BlockSpec((1, width, cols), lambda c, s: (c, 0, 0)),
         ],
-        out_specs=pl.BlockSpec((1, block_rows, 2, cols), lambda c, s: (c, s, 0, 0)),
-        out_shape=jax.ShapeDtypeStruct((chans, slots, 2, cols), jnp.bfloat16),
+        out_specs=pl.BlockSpec((1, block_rows, pairs, cols), lambda c, s: (c, s, 0, 0)),
+        out_shape=jax.ShapeDtypeStruct((chans, slots, pairs, cols), jnp.bfloat16),
         compiler_params=pltpu.CompilerParams(vmem_limit_bytes=48 * 1024 * 1024),
-    )(l0, l1, rhs)
+    )(lhs, rhs)
 
 
 def per_device(voltages, filter_taps, channel_index, antenna_slot_order):
@@ -111,13 +114,12 @@
     im = xl[:, :, 1, :]
     row0 = jnp.concatenate([re, im], axis=-1)
     row1 = jnp.concatenate([im, -re], axis=-1)
-    r0a, r0b = split2(row0)
-    r1a, r1b = split2(row1)
+    lhs = jnp.stack([row0, row1], axis=2)
+    la, lb = split2(lhs)
     o1, o2 = split2(ordered)
-    l0 = jnp.concatenate([r0a, r0a, r0b], axis=-1)
-    l1 = jnp.concatenate([r1a, r1a, r1b], axis=-1)
+    lcat = jnp.concatenate([la, la, lb], axis=-1)
     rhs = jnp.concatenate([o1, o2, o1], axis=-1).transpose(0, 2, 1)
-    result = correlate(l0, l1, rhs, min(128, slots_local))
+    result = correlate(lcat, rhs, min(128, slots_local))
     return result
 
 

time: 185 us -> 132 us (0.71)
  Pallas kernels: 95.5 us -> 39.5 us
  local copies, waits for them, and re-layouts: 50.5 us -> 27.7 us
  waiting for transfers between devices: 7.22 us -> 23.3 us
  blocking collectives: 0 us -> 10.7 us
  starting transfers between devices: 5.19 us -> 0.01 us
  other arithmetic: 12.4 us -> 16.5 us
    pallas_call x1, Pallas kernels: 65.5 us -> 17.2 us  [correlate(): pl.pallas_call(_corr_kernel, grid=(chans, slots // block_rows), in_specs=...]
    gather x1 -> x0, local copies, waits for them, and re-layouts: 23 us -> none  [column_index(): return 2 * inverse[column_entry // 2] + column_entry % 2]
    all_gather x1, waiting for transfers between devices: 1.87 us -> 23.2 us  [per_device(): everything = lax.all_gather(x, 'blk', axis=0, tiled=True)]
    all_to_all x0 -> x1, blocking collectives: none -> 10.7 us  [per_device(): x = lax.all_to_all(x, 'grp', split_axis=1, concat_axis=0, tiled=True)]
    pallas_call x1, Pallas kernels: 30 us -> 22.3 us  [frame_products(): pl.pallas_call(_frame_kernel, grid=(steps,), in_specs=[pl.BlockSpec((rows...]
    all_to_all x1 -> x0, waiting for transfers between devices: 5.34 us -> none  [per_device(): x = lax.all_to_all(x, 'grp', split_axis=1, concat_axis=0, tiled=True)]
    all_to_all x1 -> x0, starting transfers between devices: 5.18 us -> none  [per_device(): x = lax.all_to_all(x, 'grp', split_axis=1, concat_axis=0, tiled=True)]
    add x1, other arithmetic: 1.68 us -> 5.38 us  [channelize(): spec = spec + prod[m:m + spectra, :, m * cols:(m + 1) * cols]]
  transfers between devices with their start and end apart: 2 -> 1, of which waited for: 2 -> 1; matrix products, arithmetic and copies ran while one was open for 15% -> 4% of each run, Pallas kernels for 0% -> 0%
where the time goes in v2:
time: 132 us; the launch traced here: 131 us
  Pallas kernels  39.5 us (30%)
  local copies, waits for them, and re-layouts  27.7 us (21%)
  waiting for transfers between devices  23.3 us (18%)
  other arithmetic  16.5 us (12%)
  between operations  13.6 us (10%)
  blocking collectives  10.7 us (8%)
    all_gather x1, waiting for transfers between devices, per_device(): everything = lax.all_gather(x, 'blk', axis=0, tiled=True)  23.2 us
    pallas_call x1, Pallas kernels, frame_products(): pl.pallas_call(_frame_kernel, grid=(steps,), in_specs=[pl.BlockSpec((rows...  22.3 us
    gather x2, local copies, waits for them, and re-layouts, per_device(): ordered = jnp.take(everything, columns, axis=0)  17.7 us
    pallas_call x1, Pallas kernels, correlate(): pl.pallas_call(_corr_kernel, grid=(chans, slots // block_rows), in_specs=...  17.2 us
    all_to_all x1, blocking collectives, per_device(): x = lax.all_to_all(x, 'grp', split_axis=1, concat_axis=0, tiled=True)  10.7 us
    convert_element_type x1, local copies, waits for them, and re-layouts, channelize(): (filter_taps[:, :, None] * twiddle[None, :, :]).astype(jnp.bfloat16)  6.36 us
    add x1, other arithmetic, channelize(): spec = spec + prod[m:m + spectra, :, m * cols:(m + 1) * cols]  5.38 us
    convert_element_type x1, other arithmetic, channelize(): (filter_taps[:, :, None] * twiddle[None, :, :]).astype(jnp.bfloat16)  3.6 us
  transfers between devices with their start and end apart: 1, of which 1 were waited for; matrix products, arithmetic and copies ran while one was open for 4% of the time, Pallas kernels for 0%

profile of v2, /device:TPU:0, one launch (start us, length us, event | category | flops | bytes accessed | tf_op | source)
XLA Modules:
  0.0 131.3 jit_solution(5708797485150738642)
XLA Ops:
  6.5 0.0 all-gather.2.cloned.1.call-start
  6.5 3.1 %cosine_convert_fusion = (bf16[8192,16]{0,1:T(8,128)(2,1)S(1)}, bf16[8192,16]{0,1:T(8,128)(2,1)S(1)}) fusion(s32[16]{0:T(128)} %param.6), kind=kLoop, calls=%fused_computation.27 | loop fusion | flops 2228224 | bytes 524352 | tf_op jit(solution)/shard_map/convert
  9.7 0.1 maximum_convert_fusion
  9.8 3.6 %multiply_convert_fusion = bf16[8192,8,32]{0,2,1:T(8,128)(2,1)} fusion(f32[8192,32]{0,1:T(8,128)S(1)} %maximum_convert_fusion, f32[8192,8]{0,1:T(8,128)} %bitcast.56), kind=kLoop, calls=%fused_computation.3 | loop fusion | flops 4194304 | bytes 5505024 | tf_op jit(solution)/shard_map/convert_element_type | solution.py:50
  13.4 6.4 %copy.36.w_ref = bf16[8192,256]{1,0:T(8,128)(2,1)} copy(bf16[8192,256]{0,1:T(8,128)(2,1)} %bitcast.50) | data formatting | bytes 8388608 | tf_op jit(solution)/shard_map/convert_element_type | solution.py:50
  19.7 22.3 %shard_map.46 = f32[24,128,256]{2,1,0:T(8,128)} custom-call(bf16[128,188416]{1,0:T(8,128)(2,1)} %v_ref.1, bf16[8192,256]{1,0:T(8,128)(2,1)} %copy.36.w_ref), custom_call_target="tpu_custom_call" | custom-call | tf_op jit(solution)/shard_map/pallas_call | solution.py:31
  42.1 5.4 %slice_add_fusion = f32[16,128,32]{2,1,0:T(8,128)S(1)} fusion(f32[24,128,256]{2,1,0:T(8,128)} %shard_map.46), kind=kLoop, calls=%fused_computation.9 | loop fusion | flops 458752 | bytes 2359296 | tf_op jit(solution)/shard_map/add | solution.py:55
  47.4 0.0 copy-start
  47.5 0.3 copy.37
  47.8 0.1 copy.38
  47.9 10.7 %all_to_all.15 = f32[128,16,2,16]{0,2,3,1:T(2,128)S(1)} all-to-all(f32[128,16,2,16]{0,2,3,1:T(2,128)S(1)} %copy.38), channel_id=1, replica_groups=mesh['grp'=4,'blk'=8] {'grp'}, dimensions={1} | all-to-all | bytes 524288 | tf_op jit(solution)/shard_map/all_to_all | solution.py:104
  58.6 0.2 copy.43
  58.8 0.8 copy.44
  59.7 0.0 all-gather.2.cloned.1.call-update
  59.7 0.0 copy-done
  59.7 1.8 %select_reduce_fusion = s32[2048]{0:T(1024)S(1)} fusion(s32[2048]{0:T(1024)S(1)} %copy-done), kind=kLoop, calls=%fused_computation.1 | loop fusion | flops 12580864 | bytes 16384 | tf_op jit(solution)/shard_map/reduce_sum | solution.py:62
  61.5 0.3 iota_add_fusion
  61.8 0.6 add.95
  62.5 0.5 add.92
  63.0 0.1 maximum_bitcast_fusion.1
  63.2 1.0 copy.42
  64.2 0.1 convert_element_type.54
  64.4 0.2 subtract_convert_fusion
  64.5 1.0 pad_maximum_fusion.l_ref
  65.5 23.2 %all-gather.2.cloned.1.call-done = f32[4096,128]{1,0:T(8,128)} async-done(((f32[512,128]{1,0:T(8,128)}), f32[4096,128]{1,0:T(8,128)}) %all-gather.2.cloned.1.call-update) | async-done | bytes 2097168 | tf_op jit(solution)/shard_map/all_gather | solution.py:107
  88.7 15.8 %gather_fusion = f32[4096,128]{1,0:T(8,128)} fusion(f32[4096,128]{1,0:T(8,128)} %all-gather.2.cloned.1.call-done, s32[4096]{0:T(1024)S(1)} %broadcast_clamp_fusion), kind=kCustom, calls=%fused_computation | custom fusion | bytes 4210688 | tf_op jit(solution)/shard_map/jit(_take)/gather | solution.py:109
  104.5 1.9 %copy.45 = f32[4096,128]{0,1:T(8,128)S(1)} copy(f32[4096,128]{1,0:T(8,128)} %gather_fusion) | data formatting | bytes 4194304 | tf_op jit(solution)/shard_map/jit(_take)/gather | solution.py:109
  106.4 0.2 fusion
  106.7 0.2 bitcast_convert_fusion
  106.8 0.4 maximum_bitcast_fusion.o_ref
  107.2 17.2 %shard_map.47 = bf16[4,512,2,4096]{3,2,1,0:T(2,128)(2,1)} custom-call(bf16[4,1024,96]{2,1,0:T(8,128)(2,1)S(1)} %pad_maximum_fusion.l_ref, bf16[4,96,4096]{2,1,0:T(8,128)(2,1)S(1)} %maximum_bitcast_fusion.o_ref), custom_call_target="tpu_custom_call" | custom-call | tf_op jit(solution)/shard_map/pallas_call | solution.py:84
  (10 shorter events, 0.2 us)
Async XLA Ops:
  6.5 82.2 %all-gather.2.cloned.1.call-start = ((), (), s32[]{:S(2)}) async-start(), calls=%async_computation.1 | async-start | bytes 2359296 | tf_op jit(solution)/shard_map/all_gather | solution.py:107
  47.4 12.3 %copy-start = (s32[2048]{0:T(1024)S(1)}, s32[2048]{0:T(1024)}, u32[]{:S(2)}) copy-start(s32[2048]{0:T(1024)} %param.7) | copy-start | bytes 24580
Sparse Core Ops, SparseCore 0:
  59.8 28.8 all-gather.1

commit v3 on v2

--- a/solution.py
+++ b/solution.py
@@ -15,11 +15,20 @@
     return jnp.concatenate([jnp.cos(angle), -jnp.sin(angle)], axis=1).astype(jnp.bfloat16)
 
 
+def phase_table_t(channel_index, fft_length):
+    samples_idx = jnp.arange(fft_length, dtype=jnp.int32)
+    phase = channel_index[:, None] * samples_idx[None, :] % fft_length
+    angle = phase.astype(jnp.float32) * jnp.float32(2.0 * math.pi / fft_length)
+    return jnp.concatenate([jnp.cos(angle), -jnp.sin(angle)], axis=0).astype(jnp.bfloat16)
+
+
 def _frame_kernel(v_ref, w_ref, o_ref):
-    n = w_ref.shape[0]
+    n = w_ref.shape[1]
     group = o_ref.shape[0]
     lhs = jnp.concatenate([v_ref[:, g * n : (g + 1) * n] for g in range(group)], axis=0)
-    res = jnp.dot(lhs, w_ref[...], preferred_element_type=jnp.float32)
+    res = lax.dot_general(
+        lhs, w_ref[...], (((1,), (1,)), ((), ())), preferred_element_type=jnp.float32
+    )
     o_ref[...] = res.reshape(o_ref.shape)
 
 
@@ -27,13 +36,13 @@
     rows, samples = voltages.shape
     frames = samples // fft_length
     steps = -(-frames // group)
-    width = weights.shape[1]
+    width = weights.shape[0]
     return pl.pallas_call(
         _frame_kernel,
         grid=(steps,),
         in_specs=[
             pl.BlockSpec((rows, group * fft_length), lambda f: (0, f)),
-            pl.BlockSpec((fft_length, width), lambda f: (0, 0)),
+            pl.BlockSpec((width, fft_length), lambda f: (0, 0)),
         ],
         out_specs=pl.BlockSpec((group, rows, width), lambda f: (f, 0, 0)),
         out_shape=jax.ShapeDtypeStruct((steps * group, rows, width), jnp.float32),
@@ -45,10 +54,10 @@
     tap_count, fft_length = filter_taps.shape
     frame_count = voltages.shape[1] // fft_length
     spectra = frame_count - tap_count + 1
-    twiddle = phase_table(channel_index, fft_length).astype(jnp.float32)
-    cols = twiddle.shape[1]
-    weights = (filter_taps[:, :, None] * twiddle[None, :, :]).astype(jnp.bfloat16)
-    weights = weights.transpose(1, 0, 2).reshape(fft_length, tap_count * cols)
+    twiddle = phase_table_t(channel_index, fft_length).astype(jnp.float32)
+    cols = twiddle.shape[0]
+    weights = (filter_taps[:, None, :] * twiddle[None, :, :]).astype(jnp.bfloat16)
+    weights = weights.reshape(tap_count * cols, fft_length)
     prod = frame_products(voltages, weights, fft_length, 4)
     spec = prod[0:spectra, :, 0:cols]
     for m in range(1, tap_count):
@@ -56,14 +65,12 @@
     return spec
 
 
-def column_index(antenna_slot_order):
+def slot_index(antenna_slot_order):
     count = antenna_slot_order.shape[0]
     ids = jnp.arange(count, dtype=jnp.int32)
-    inverse = jnp.sum(
+    return jnp.sum(
         jnp.where(antenna_slot_order[None, :] == ids[:, None], ids[None, :], 0), axis=1
     )
-    pol = jnp.arange(2, dtype=jnp.int32)
-    return (2 * inverse[:, None] + pol[None, :]).reshape(2 * count)
 
 
 def split2(x):
@@ -105,8 +112,10 @@
     slots_local = x.shape[0]
     x = x.reshape(slots_local, local_ch * 2 * spectra)
     everything = lax.all_gather(x, "blk", axis=0, tiled=True)
-    columns = column_index(antenna_slot_order)
-    ordered = jnp.take(everything, columns, axis=0)
+    inverse = slot_index(antenna_slot_order)
+    width = everything.shape[1]
+    ordered = jnp.take(everything.reshape(-1, 2 * width), inverse, axis=0)
+    ordered = ordered.reshape(-1, width)
     ordered = ordered.reshape(-1, local_ch, 2 * spectra).transpose(1, 0, 2)
     scale = jnp.float32(1.0 / spectra)
     xl = x.reshape(slots_local, local_ch, 2, spectra).transpose(1, 0, 2, 3) * scale

time: 132 us -> 135 us (1.023)
  local copies, waits for them, and re-layouts: 27.7 us -> 30.8 us
    convert_element_type x1 -> x0, local copies, waits for them, and re-layouts: 6.36 us -> none  [channelize(): (filter_taps[:, :, None] * twiddle[None, :, :]).astype(jnp.bfloat16)]
    gather x2 -> x3, local copies, waits for them, and re-layouts: 17.7 us -> 22.6 us  [per_device(): ordered = jnp.take(everything.reshape(-1, 2 * width), inverse, axis=0)]
    all_gather x0 -> x1, local copies, waits for them, and re-layouts: none -> 2.88 us  [per_device(): everything = lax.all_gather(x, 'blk', axis=0, tiled=True)]
where the time goes in v3:
time: 135 us
  Pallas kernels  39.5 us (29%)
  local copies, waits for them, and re-layouts  30.8 us (23%)
  waiting for transfers between devices  23.7 us (18%)
  other arithmetic  16.2 us (12%)
  between operations  13.6 us (10%)
  blocking collectives  10.7 us (8%)
    all_gather x1, waiting for transfers between devices, per_device(): everything = lax.all_gather(x, 'blk', axis=0, tiled=True)  23.7 us
    gather x3, local copies, waits for them, and re-layouts, per_device(): ordered = jnp.take(everything.reshape(-1, 2 * width), inverse, axis=0)  22.6 us
    pallas_call x1, Pallas kernels, frame_products(): pl.pallas_call(_frame_kernel, grid=(steps,), in_specs=[pl.BlockSpec((rows...  22.3 us
    pallas_call x1, Pallas kernels, correlate(): pl.pallas_call(_corr_kernel, grid=(chans, slots // block_rows), in_specs=...  17.2 us
    all_to_all x1, blocking collectives, per_device(): x = lax.all_to_all(x, 'grp', split_axis=1, concat_axis=0, tiled=True)  10.7 us
    add x1, other arithmetic, channelize(): spec = spec + prod[m:m + spectra, :, m * cols:(m + 1) * cols]  5.45 us
    convert_element_type x1, other arithmetic, channelize(): (filter_taps[:, None, :] * twiddle[None, :, :]).astype(jnp.bfloat16)  3.6 us
    another operation x1, other arithmetic  3.15 us
  transfers between devices with their start and end apart: 1, of which 1 were waited for; matrix products, arithmetic and copies ran while one was open for 4% of the time, Pallas kernels for 0%

profile of v3, /device:TPU:0, one launch (start us, length us, event | category | flops | bytes accessed | tf_op | source)
XLA Modules:
  0.0 134.5 jit_solution(5644321639515826962)
XLA Ops:
  6.5 0.0 all-gather.2.cloned.1.call-start
  6.5 3.1 %cosine_convert_fusion = (bf16[16,8192]{1,0:T(8,128)(2,1)S(1)}, bf16[16,8192]{1,0:T(8,128)(2,1)S(1)}) fusion(s32[16]{0:T(128)} %param.6), kind=kLoop, calls=%fused_computation.26 | loop fusion | flops 2228224 | bytes 524352 | tf_op jit(solution)/shard_map/convert
  9.7 0.1 maximum_convert_fusion
  9.8 3.6 %multiply_convert_fusion = bf16[8,32,8192]{2,1,0:T(8,128)(2,1)} fusion(f32[32,8192]{1,0:T(8,128)S(1)} %maximum_convert_fusion, f32[8,8192]{1,0:T(8,128)} %param.5), kind=kLoop, calls=%fused_computation.3 | loop fusion | flops 4194304 | bytes 5505024 | tf_op jit(solution)/shard_map/convert_element_type | solution.py:59
  13.4 22.3 %shard_map.46 = f32[24,128,256]{2,1,0:T(8,128)} custom-call(bf16[128,188416]{1,0:T(8,128)(2,1)} %v_ref.1, bf16[256,8192]{1,0:T(8,128)(2,1)} %bitcast.47), custom_call_target="tpu_custom_call" | custom-call | tf_op jit(solution)/shard_map/pallas_call | solution.py:40
  35.7 5.4 %slice_add_fusion = f32[16,128,32]{2,1,0:T(8,128)S(1)} fusion(f32[24,128,256]{2,1,0:T(8,128)} %shard_map.46), kind=kLoop, calls=%fused_computation.9 | loop fusion | flops 458752 | bytes 2359296 | tf_op jit(solution)/shard_map/add | solution.py:64
  41.2 0.0 copy-start
  41.2 0.3 copy.31
  41.5 0.1 copy.32
  41.6 10.7 %all_to_all.15 = f32[128,16,2,16]{0,2,3,1:T(2,128)S(1)} all-to-all(f32[128,16,2,16]{0,2,3,1:T(2,128)S(1)} %copy.32), channel_id=1, replica_groups=mesh['grp'=4,'blk'=8] {'grp'}, dimensions={1} | all-to-all | bytes 524288 | tf_op jit(solution)/shard_map/all_to_all | solution.py:111
  52.4 0.2 copy.37
  52.5 0.7 copy.45
  53.3 0.0 all-gather.2.cloned.1.call-update
  53.3 0.0 copy-done
  53.3 1.8 %select_reduce_fusion = s32[2048]{0:T(1024)S(1)} fusion(s32[2048]{0:T(1024)S(1)} %copy-done), kind=kLoop, calls=%fused_computation.1 | loop fusion | flops 12580864 | bytes 16384 | tf_op jit(solution)/shard_map/reduce_sum | solution.py:71
  55.1 0.3 broadcast_in_dim.35
  55.4 0.7 broadcast_in_dim.36
  56.2 0.1 maximum_bitcast_fusion.1
  56.3 1.0 copy.36
  57.3 0.1 convert_element_type.53
  57.5 0.2 subtract_convert_fusion
  57.7 1.0 pad_maximum_fusion.l_ref
  58.6 23.7 %all-gather.2.cloned.1.call-done = f32[4096,128]{0,1:T(8,128)} async-done(((f32[512,128]{0,1:T(8,128)}), f32[4096,128]{0,1:T(8,128)}) %all-gather.2.cloned.1.call-update) | async-done | bytes 2097168 | tf_op jit(solution)/shard_map/all_gather | solution.py:114
  82.3 2.9 %copy.38 = f32[4096,128]{1,0:T(8,128)} copy(f32[4096,128]{0,1:T(8,128)} %all-gather.2.cloned.1.call-done) | data formatting | bytes 4194304 | tf_op jit(solution)/shard_map/all_gather | solution.py:114
  85.2 1.9 %reshape.73 = f32[2048,256]{1,0:T(8,128)S(1)} reshape(f32[4096,128]{1,0:T(8,128)} %copy.38) | data formatting | bytes 4194304 | tf_op jit(solution)/shard_map/reshape | solution.py:117
  87.1 8.6 %gather_fusion = f32[2048,256]{1,0:T(8,128)} fusion(f32[2048,256]{1,0:T(8,128)S(1)} %reshape.73, s32[2048]{0:T(1024)S(1)} %broadcast_clamp_fusion), kind=kCustom, calls=%fused_computation | custom fusion | bytes 4202496 | tf_op jit(solution)/shard_map/jit(_take)/gather | solution.py:117
  95.7 7.3 %gather.7 = f32[4096,4,32]{2,1,0:T(4,128)} reshape(f32[2048,256]{1,0:T(8,128)} %gather_fusion) | data formatting | bytes 4194304 | tf_op jit(solution)/shard_map/jit(_take)/gather | solution.py:117
  103.0 6.7 %copy.39 = f32[4096,4,32]{0,2,1:T(8,128)S(1)} copy(f32[4096,4,32]{2,1,0:T(4,128)} %gather.7) | data formatting | bytes 4194304 | tf_op jit(solution)/shard_map/jit(_take)/gather | solution.py:117
  109.7 0.2 fusion
  109.9 0.2 bitcast_convert_fusion
  110.1 0.4 maximum_bitcast_fusion.o_ref
  110.5 17.2 %shard_map.47 = bf16[4,512,2,4096]{3,2,1,0:T(2,128)(2,1)} custom-call(bf16[4,1024,96]{2,1,0:T(8,128)(2,1)S(1)} %pad_maximum_fusion.l_ref, bf16[4,96,4096]{2,1,0:T(8,128)(2,1)S(1)} %maximum_bitcast_fusion.o_ref), custom_call_target="tpu_custom_call" | custom-call | tf_op jit(solution)/shard_map/pallas_call | solution.py:91
  (8 shorter events, 0.1 us)
Async XLA Ops:
  6.5 75.8 %all-gather.2.cloned.1.call-start = ((), (), s32[]{:S(2)}) async-start(), calls=%async_computation.1 | async-start | bytes 2359296 | tf_op jit(solution)/shard_map/all_gather | solution.py:114
  41.2 12.1 %copy-start = (s32[2048]{0:T(1024)S(1)}, s32[2048]{0:T(1024)}, u32[]{:S(2)}) copy-start(s32[2048]{0:T(1024)} %param.7) | copy-start | bytes 24580
Sparse Core Ops, SparseCore 0:
  53.4 28.8 all-gather.1

commit v4 on v3

--- a/solution.py
+++ b/solution.py
@@ -73,6 +73,29 @@
     )
 
 
+def _perm_kernel(inv_ref, e_ref, o_ref):
+    def body(a, carry):
+        src = inv_ref[a] * 2
+        o_ref[pl.ds(2 * a, 2), :] = e_ref[pl.ds(src, 2), :]
+        return carry
+
+    lax.fori_loop(0, inv_ref.shape[0], body, 0, unroll=8)
+
+
+def permute_pairs(everything, inverse):
+    rows, width = everything.shape
+    return pl.pallas_call(
+        _perm_kernel,
+        grid_spec=pltpu.PrefetchScalarGridSpec(
+            num_scalar_prefetch=1,
+            grid=(1,),
+            in_specs=[pl.BlockSpec((rows, width), lambda i, inv: (0, 0))],
+            out_specs=pl.BlockSpec((rows, width), lambda i, inv: (0, 0)),
+        ),
+        out_shape=jax.ShapeDtypeStruct((rows, width), everything.dtype),
+    )(inverse, everything)
+
+
 def split2(x):
     hi = x.astype(jnp.bfloat16)
     lo = (x - hi.astype(jnp.float32)).astype(jnp.bfloat16)
@@ -113,9 +136,7 @@
     x = x.reshape(slots_local, local_ch * 2 * spectra)
     everything = lax.all_gather(x, "blk", axis=0, tiled=True)
     inverse = slot_index(antenna_slot_order)
-    width = everything.shape[1]
-    ordered = jnp.take(everything.reshape(-1, 2 * width), inverse, axis=0)
-    ordered = ordered.reshape(-1, width)
+    ordered = permute_pairs(everything, inverse)
     ordered = ordered.reshape(-1, local_ch, 2 * spectra).transpose(1, 0, 2)
     scale = jnp.float32(1.0 / spectra)
     xl = x.reshape(slots_local, local_ch, 2, spectra).transpose(1, 0, 2, 3) * scale
@@ -128,7 +149,7 @@
     o1, o2 = split2(ordered)
     lcat = jnp.concatenate([la, la, lb], axis=-1)
     rhs = jnp.concatenate([o1, o2, o1], axis=-1).transpose(0, 2, 1)
-    result = correlate(lcat, rhs, min(128, slots_local))
+    result = correlate(lcat, rhs, min(256, slots_local))
     return result
 
 

time: 135 us -> 114 us (0.84)
  local copies, waits for them, and re-layouts: 30.8 us -> 4.48 us
  Pallas kernels: 39.5 us -> 44.3 us
    gather x3 -> x0, local copies, waits for them, and re-layouts: 22.6 us -> none  [per_device(): ordered = jnp.take(everything.reshape(-1, 2 * width), inverse, axis=0)]
    pallas_call x0 -> x1, Pallas kernels: none -> 7.18 us  [permute_pairs(): pl.pallas_call(_perm_kernel, grid_spec=pltpu.PrefetchScalarGridSpec(num_s...]
    all_gather x1 -> x0, local copies, waits for them, and re-layouts: 2.88 us -> none  [per_device(): everything = lax.all_gather(x, 'blk', axis=0, tiled=True)]
    pallas_call x1, Pallas kernels: 17.2 us -> 14.8 us  [correlate(): pl.pallas_call(_corr_kernel, grid=(chans, slots // block_rows), in_specs=...]
    pallas_call x0 -> x1, local copies, waits for them, and re-layouts: none -> 1.92 us  [permute_pairs(): pl.pallas_call(_perm_kernel, grid_spec=pltpu.PrefetchScalarGridSpec(num_s...]
where the time goes in v4:
time: 114 us
  Pallas kernels  44.3 us (39%)
  waiting for transfers between devices  24.2 us (21%)
  other arithmetic  16.7 us (15%)
  between operations  13.5 us (12%)
  blocking collectives  10.7 us (9%)
  local copies, waits for them, and re-layouts  4.48 us (4%)
    all_gather x1, waiting for transfers between devices, per_device(): everything = lax.all_gather(x, 'blk', axis=0, tiled=True)  24.2 us
    pallas_call x1, Pallas kernels, frame_products(): pl.pallas_call(_frame_kernel, grid=(steps,), in_specs=[pl.BlockSpec((rows...  22.3 us
    pallas_call x1, Pallas kernels, correlate(): pl.pallas_call(_corr_kernel, grid=(chans, slots // block_rows), in_specs=...  14.8 us
    all_to_all x1, blocking collectives, per_device(): x = lax.all_to_all(x, 'grp', split_axis=1, concat_axis=0, tiled=True)  10.7 us
    pallas_call x1, Pallas kernels, permute_pairs(): pl.pallas_call(_perm_kernel, grid_spec=pltpu.PrefetchScalarGridSpec(num_s...  7.18 us
    add x1, other arithmetic, channelize(): spec = spec + prod[m:m + spectra, :, m * cols:(m + 1) * cols]  5.47 us
    convert_element_type x1, other arithmetic, channelize(): (filter_taps[:, None, :] * twiddle[None, :, :]).astype(jnp.bfloat16)  3.6 us
    another operation x1, other arithmetic  3.15 us
  transfers between devices with their start and end apart: 1, of which 1 were waited for; matrix products, arithmetic and copies ran while one was open for 4% of the time, Pallas kernels for 0%

profile of v4, /device:TPU:0, one launch (start us, length us, event | category | flops | bytes accessed | tf_op | source)
XLA Modules:
  0.0 114.0 jit_solution(5756285249193588080)
XLA Ops:
  6.5 0.0 all-gather.2.cloned.1.call-start
  6.5 3.1 %cosine_convert_fusion = (bf16[16,8192]{1,0:T(8,128)(2,1)S(1)}, bf16[16,8192]{1,0:T(8,128)(2,1)S(1)}) fusion(s32[16]{0:T(128)} %param.6), kind=kLoop, calls=%fused_computation.23 | loop fusion | flops 2228224 | bytes 524352 | tf_op jit(solution)/shard_map/convert
  9.7 0.1 maximum_convert_fusion
  9.8 3.6 %multiply_convert_fusion = bf16[8,32,8192]{2,1,0:T(8,128)(2,1)} fusion(f32[32,8192]{1,0:T(8,128)S(1)} %maximum_convert_fusion, f32[8,8192]{1,0:T(8,128)} %param.5), kind=kLoop, calls=%fused_computation.2 | loop fusion | flops 4194304 | bytes 5505024 | tf_op jit(solution)/shard_map/convert_element_type | solution.py:59
  13.4 22.3 %shard_map.46 = f32[24,128,256]{2,1,0:T(8,128)} custom-call(bf16[128,188416]{1,0:T(8,128)(2,1)} %v_ref.1, bf16[256,8192]{1,0:T(8,128)(2,1)} %bitcast.41), custom_call_target="tpu_custom_call" | custom-call | tf_op jit(solution)/shard_map/pallas_call | solution.py:40
  35.7 5.5 %slice_add_fusion = f32[16,128,32]{2,1,0:T(8,128)S(1)} fusion(f32[24,128,256]{2,1,0:T(8,128)} %shard_map.46), kind=kLoop, calls=%fused_computation.6 | loop fusion | flops 458752 | bytes 2359296 | tf_op jit(solution)/shard_map/add | solution.py:64
  41.2 0.0 copy-start
  41.2 0.3 copy.31
  41.5 0.1 copy.32
  41.6 10.7 %all_to_all.15 = f32[128,16,2,16]{0,2,3,1:T(2,128)S(1)} all-to-all(f32[128,16,2,16]{0,2,3,1:T(2,128)S(1)} %copy.32), channel_id=1, replica_groups=mesh['grp'=4,'blk'=8] {'grp'}, dimensions={1} | all-to-all | bytes 524288 | tf_op jit(solution)/shard_map/all_to_all | solution.py:134
  52.4 0.2 copy.37
  52.6 0.8 copy.38
  53.4 0.0 all-gather.2.cloned.1.call-update
  53.4 0.0 copy-done
  53.5 2.3 %select_reduce_fusion.inv_ref = s32[2048]{0:T(1024)} fusion(s32[2048]{0:T(1024)S(1)} %copy-done), kind=kLoop, calls=%fused_computation | loop fusion | flops 12580864 | bytes 16384 | tf_op jit(solution)/shard_map/reduce_sum | solution.py:71
  55.9 0.1 maximum_bitcast_fusion.1
  56.0 1.0 copy.36
  57.0 0.1 convert_element_type.53
  57.2 0.2 subtract_convert_fusion.1
  57.4 1.0 pad_maximum_fusion.l_ref
  58.3 24.2 %all-gather.2.cloned.1.call-done.e_ref = f32[4096,128]{1,0:T(8,128)} async-done(((f32[512,128]{1,0:T(8,128)}), f32[4096,128]{1,0:T(8,128)}) %all-gather.2.cloned.1.call-update) | async-done | bytes 2097168 | tf_op jit(solution)/shard_map/all_gather | solution.py:137
  82.5 7.2 %shard_map.47 = f32[4096,128]{1,0:T(8,128)} custom-call(s32[2048]{0:T(1024)} %select_reduce_fusion.inv_ref, f32[4096,128]{1,0:T(8,128)} %all-gather.2.cloned.1.call-done.e_ref), custom_call_target="tpu_custom_call" | custom-call | tf_op jit(solution)/shard_map/pallas_call | solution.py:87
  89.7 1.9 %copy.39 = f32[4096,128]{0,1:T(8,128)S(1)} copy(f32[4096,128]{1,0:T(8,128)} %shard_map.47) | data formatting | bytes 4194304 | tf_op jit(solution)/shard_map/pallas_call | solution.py:87
  91.6 0.3 subtract_convert_fusion
  91.9 0.4 maximum_bitcast_fusion.o_ref
  92.3 14.8 %shard_map.48 = bf16[4,512,2,4096]{3,2,1,0:T(2,128)(2,1)} custom-call(bf16[4,1024,96]{2,1,0:T(8,128)(2,1)S(1)} %pad_maximum_fusion.l_ref, bf16[4,96,4096]{2,1,0:T(8,128)(2,1)S(1)} %maximum_bitcast_fusion.o_ref), custom_call_target="tpu_custom_call" | custom-call | tf_op jit(solution)/shard_map/pallas_call | solution.py:114
  (6 shorter events, 0.1 us)
Async XLA Ops:
  6.5 75.9 %all-gather.2.cloned.1.call-start = ((), (), s32[]{:S(2)}) async-start(), calls=%async_computation.1 | async-start | bytes 2359296 | tf_op jit(solution)/shard_map/all_gather | solution.py:137
  41.2 12.3 %copy-start = (s32[2048]{0:T(1024)S(1)}, s32[2048]{0:T(1024)}, u32[]{:S(2)}) copy-start(s32[2048]{0:T(1024)} %param.7) | copy-start | bytes 24580
Sparse Core Ops, SparseCore 0:
  53.6 28.8 all-gather.1

commit v5 on v4

--- a/solution.py
+++ b/solution.py
@@ -22,21 +22,32 @@
     return jnp.concatenate([jnp.cos(angle), -jnp.sin(angle)], axis=0).astype(jnp.bfloat16)
 
 
-def _frame_kernel(v_ref, w_ref, o_ref):
+def _frame_kernel(v_ref, w_ref, o_ref, p_ref):
+    i = pl.program_id(0)
     n = w_ref.shape[1]
-    group = o_ref.shape[0]
+    spectra, rows, cols = o_ref.shape
+    group = p_ref.shape[0] // pl.num_programs(0)
     lhs = jnp.concatenate([v_ref[:, g * n : (g + 1) * n] for g in range(group)], axis=0)
     res = lax.dot_general(
         lhs, w_ref[...], (((1,), (1,)), ((), ())), preferred_element_type=jnp.float32
     )
-    o_ref[...] = res.reshape(o_ref.shape)
+    p_ref[pl.ds(i * group, group)] = res.reshape(group, rows, res.shape[1])
+
+    @pl.when(i == pl.num_programs(0) - 1)
+    def _():
+        taps = res.shape[1] // cols
+        acc = p_ref[0:spectra, :, 0:cols]
+        for m in range(1, taps):
+            acc = acc + p_ref[m : m + spectra, :, m * cols : (m + 1) * cols]
+        o_ref[...] = acc
 
 
-def frame_products(voltages, weights, fft_length, group):
+def frame_products(voltages, weights, fft_length, group, spectra):
     rows, samples = voltages.shape
     frames = samples // fft_length
     steps = -(-frames // group)
-    width = weights.shape[0]
+    width, _ = weights.shape
+    cols = width // (frames - spectra + 1)
     return pl.pallas_call(
         _frame_kernel,
         grid=(steps,),
@@ -44,8 +55,9 @@
             pl.BlockSpec((rows, group * fft_length), lambda f: (0, f)),
             pl.BlockSpec((width, fft_length), lambda f: (0, 0)),
         ],
-        out_specs=pl.BlockSpec((group, rows, width), lambda f: (f, 0, 0)),
-        out_shape=jax.ShapeDtypeStruct((steps * group, rows, width), jnp.float32),
+        out_specs=pl.BlockSpec((spectra, rows, cols), lambda f: (0, 0, 0)),
+        out_shape=jax.ShapeDtypeStruct((spectra, rows, cols), jnp.float32),
+        scratch_shapes=[pltpu.VMEM((steps * group, rows, width), jnp.float32)],
         compiler_params=pltpu.CompilerParams(vmem_limit_bytes=56 * 1024 * 1024),
     )(voltages, weights)
 
@@ -58,11 +70,7 @@
     cols = twiddle.shape[0]
     weights = (filter_taps[:, None, :] * twiddle[None, :, :]).astype(jnp.bfloat16)
     weights = weights.reshape(tap_count * cols, fft_length)
-    prod = frame_products(voltages, weights, fft_length, 4)
-    spec = prod[0:spectra, :, 0:cols]
-    for m in range(1, tap_count):
-        spec = spec + prod[m : m + spectra, :, m * cols : (m + 1) * cols]
-    return spec
+    return frame_products(voltages, weights, fft_length, 4, spectra)
 
 
 def slot_index(antenna_slot_order):
@@ -124,6 +132,20 @@
     )(lhs, rhs)
 
 
+def exchange_channels(x, grp, local_ch):
+    me = lax.axis_index("grp")
+    got = []
+    for d in range(grp):
+        part = lax.dynamic_slice_in_dim(x, ((me + d) % grp) * local_ch, local_ch, axis=1)
+        if d:
+            part = lax.ppermute(part, "grp", [(j, (j + d) % grp) for j in range(grp)])
+        got.append(part)
+    stacked = jnp.stack(got, axis=0)
+    order = (me - jnp.arange(grp, dtype=jnp.int32)) % grp
+    stacked = jnp.take(stacked, order, axis=0)
+    return stacked.reshape((grp * x.shape[0],) + stacked.shape[2:])
+
+
 def per_device(voltages, filter_taps, channel_index, antenna_slot_order):
     spec = channelize(voltages, filter_taps, channel_index)
     spectra, rows, cols = spec.shape
@@ -131,7 +153,7 @@
     grp = lax.psum(1, "grp")
     local_ch = chans // grp
     x = spec.reshape(spectra, rows, 2, chans).transpose(1, 3, 2, 0)
-    x = lax.all_to_all(x, "grp", split_axis=1, concat_axis=0, tiled=True)
+    x = exchange_channels(x, grp, local_ch)
     slots_local = x.shape[0]
     x = x.reshape(slots_local, local_ch * 2 * spectra)
     everything = lax.all_gather(x, "blk", axis=0, tiled=True)

time: 114 us -> 112 us (0.982)
  blocking collectives: 10.7 us -> 0 us
  starting transfers between devices: 0.01 us -> 5.18 us
  waiting for transfers between devices: 24.2 us -> 29.2 us
  other arithmetic: 16.7 us -> 12.1 us
  Pallas kernels: 44.3 us -> 45.7 us
    all_to_all x1 -> x0, blocking collectives: 10.7 us -> none  [per_device(): x = lax.all_to_all(x, 'grp', split_axis=1, concat_axis=0, tiled=True)]
    add x1 -> x0, other arithmetic: 5.47 us -> none  [channelize(): spec = spec + prod[m:m + spectra, :, m * cols:(m + 1) * cols]]
    ppermute x0 -> x3, starting transfers between devices: none -> 5.18 us  [exchange_channels(): part = lax.ppermute(part, 'grp', [(j, (j + d) % grp) for j in range(grp)])]
    ppermute x0 -> x3, waiting for transfers between devices: none -> 3.85 us  [exchange_channels(): part = lax.ppermute(part, 'grp', [(j, (j + d) % grp) for j in range(grp)])]
    pallas_call x0 -> x1, local copies, waits for them, and re-layouts: none -> 1.53 us  [frame_products(): pl.pallas_call(_frame_kernel, grid=(steps,), in_specs=[pl.BlockSpec((rows...]
    pallas_call x1, Pallas kernels: 22.3 us -> 23.7 us  [frame_products(): pl.pallas_call(_frame_kernel, grid=(steps,), in_specs=[pl.BlockSpec((rows...]
    all_gather x1, waiting for transfers between devices: 24.2 us -> 25.3 us  [per_device(): everything = lax.all_gather(x, 'blk', axis=0, tiled=True)]
    another operation x1 -> x2, other arithmetic: 3.15 us -> 3.16 us
  transfers between devices with their start and end apart: 1 -> 4, of which waited for: 1 -> 3; matrix products, arithmetic and copies ran while one was open for 4% -> 4% of each run, Pallas kernels for 0% -> 0%
where the time goes in v5:
time: 112 us; the launch traced here: 111 us
  Pallas kernels  45.7 us (41%)
  waiting for transfers between devices  29.2 us (26%)
  between operations  13.6 us (12%)
  other arithmetic  12.1 us (11%)
  local copies, waits for them, and re-layouts  5.6 us (5%)
  starting transfers between devices  5.18 us (5%)
    all_gather x1, waiting for transfers between devices, per_device(): everything = lax.all_gather(x, 'blk', axis=0, tiled=True)  25.3 us
    pallas_call x1, Pallas kernels, frame_products(): pl.pallas_call(_frame_kernel, grid=(steps,), in_specs=[pl.BlockSpec((rows...  23.7 us
    pallas_call x1, Pallas kernels, correlate(): pl.pallas_call(_corr_kernel, grid=(chans, slots // block_rows), in_specs=...  14.8 us
    pallas_call x1, Pallas kernels, permute_pairs(): pl.pallas_call(_perm_kernel, grid_spec=pltpu.PrefetchScalarGridSpec(num_s...  7.18 us
    ppermute x3, starting transfers between devices, exchange_channels(): part = lax.ppermute(part, 'grp', [(j, (j + d) % grp) for j in range(grp)])  5.18 us
    ppermute x3, waiting for transfers between devices, exchange_channels(): part = lax.ppermute(part, 'grp', [(j, (j + d) % grp) for j in range(grp)])  3.85 us
    convert_element_type x1, other arithmetic, channelize(): (filter_taps[:, None, :] * twiddle[None, :, :]).astype(jnp.bfloat16)  3.6 us
    another operation x1, other arithmetic  3.15 us
  transfers between devices with their start and end apart: 4, of which 3 were waited for; matrix products, arithmetic and copies ran while one was open for 4% of the time, Pallas kernels for 0%

profile of v5, /device:TPU:0, one launch (start us, length us, event | category | flops | bytes accessed | tf_op | source)
XLA Modules:
  0.0 111.5 jit_solution(12738187400068596329)
XLA Ops:
  6.5 0.0 all-gather.2.cloned.1.call-start
  6.5 3.1 %cosine_convert_fusion = (bf16[16,8192]{1,0:T(8,128)(2,1)S(1)}, bf16[16,8192]{1,0:T(8,128)(2,1)S(1)}) fusion(s32[16]{0:T(128)} %param.6), kind=kLoop, calls=%fused_computation.17 | loop fusion | flops 2228224 | bytes 524352 | tf_op jit(solution)/shard_map/convert
  9.7 0.1 maximum_convert_fusion
  9.8 3.6 %multiply_convert_fusion = bf16[8,32,8192]{2,1,0:T(8,128)(2,1)} fusion(f32[32,8192]{1,0:T(8,128)S(1)} %maximum_convert_fusion, f32[8,8192]{1,0:T(8,128)} %param.5), kind=kLoop, calls=%fused_computation.3 | loop fusion | flops 4194304 | bytes 5505024 | tf_op jit(solution)/shard_map/convert_element_type | solution.py:71
  13.4 23.7 %shard_map.46 = f32[16,128,32]{2,1,0:T(8,128)} custom-call(bf16[128,188416]{1,0:T(8,128)(2,1)} %v_ref.1, bf16[256,8192]{1,0:T(8,128)(2,1)} %bitcast.61), custom_call_target="tpu_custom_call" | custom-call | tf_op jit(solution)/shard_map/pallas_call | solution.py:51
  37.1 1.5 %copy.28 = f32[16,128,32]{1,2,0:T(8,128)S(1)} copy(f32[16,128,32]{2,1,0:T(8,128)} %shard_map.46) | data formatting | bytes 524288 | tf_op jit(solution)/shard_map/pallas_call | solution.py:51
  38.6 0.1 constant_dynamic-slice_fusion.3
  38.7 4.0 %collective-permute-start.2 = (f32[128,4,2,16]{0,3,2,1:T(8,128)S(1)}, f32[128,4,2,16]{0,3,2,1:T(8,128)S(1)}, u32[]{:S(2)}, u32[]{:S(2)}) collective-permute-start(f32[128,4,2,16]{0,3,2,1:T(8,128)S(1)} %bitcast.67), channel_id=1, source_target_pairs={{0,24},{8,0},{16,8},{24,16},{1,25},{9,1},{17,9},{25,17},{2,26},{10... | collective-permute-start | bytes 196616 | tf_op jit(solution)/shard_map/ppermute | solution.py:141
  42.7 0.1 collective-permute-start
  42.8 1.1 %collective-permute-start.1 = (f32[128,4,2,16]{0,3,2,1:T(8,128)S(1)}, f32[128,4,2,16]{0,3,2,1:T(8,128)S(1)}, u32[]{:S(2)}, u32[]{:S(2)}) collective-permute-start(f32[128,4,2,16]{0,3,2,1:T(8,128)S(1)} %bitcast.69), channel_id=1, source_target_pairs={{0,16},{8,24},{16,0},{24,8},{1,17},{9,25},{17,1},{25,9},{2,18},{10... | collective-permute-start | bytes 196616 | tf_op jit(solution)/shard_map/ppermute | solution.py:141
  44.0 0.1 broadcast_bitcast_fusion
  44.1 0.7 collective-permute-done.2
  44.8 3.2 %collective-permute-done = f32[128,4,2,16]{0,3,2,1:T(8,128)S(1)} collective-permute-done((f32[128,4,2,16]{0,3,2,1:T(8,128)S(1)}, f32[128,4,2,16]{0,3,2,1:T(8,128)S(1)}, u32[]{:S(2)}, u32[]{:S(2)}) %collective-permute-start) | collective-permute-done | bytes 65568 | tf_op jit(solution)/shard_map/ppermute | solution.py:141
  47.9 0.0 collective-permute-done.1
  48.0 0.0 copy-start
  48.0 0.6 gather_fusion
  48.6 0.2 copy.33
  48.8 0.1 copy.37
  48.9 0.8 broadcast_select_fusion
  49.7 0.0 all-gather.2.cloned.1.call-update
  49.8 2.3 %select_reduce_fusion.inv_ref = s32[2048]{0:T(1024)} fusion(s32[2048]{0:T(1024)S(1)} %copy-done), kind=kLoop, calls=%fused_computation.1 | loop fusion | flops 12580864 | bytes 16384 | tf_op jit(solution)/shard_map/reduce_sum | solution.py:79
  52.2 0.1 maximum_bitcast_fusion.1
  52.3 1.0 copy.35
  53.3 0.1 convert_element_type.53
  53.5 0.2 subtract_convert_fusion.1
  53.7 1.0 pad_maximum_fusion.l_ref
  54.6 25.3 %all-gather.2.cloned.1.call-done.e_ref = f32[4096,128]{1,0:T(8,128)} async-done(((f32[512,128]{1,0:T(8,128)}), f32[4096,128]{1,0:T(8,128)}) %all-gather.2.cloned.1.call-update) | async-done | bytes 2097168 | tf_op jit(solution)/shard_map/all_gather | solution.py:159
  80.0 7.2 %shard_map.47 = f32[4096,128]{1,0:T(8,128)} custom-call(s32[2048]{0:T(1024)} %select_reduce_fusion.inv_ref, f32[4096,128]{1,0:T(8,128)} %all-gather.2.cloned.1.call-done.e_ref), custom_call_target="tpu_custom_call" | custom-call | tf_op jit(solution)/shard_map/pallas_call | solution.py:95
  87.2 1.9 %copy.38 = f32[4096,128]{0,1:T(8,128)S(1)} copy(f32[4096,128]{1,0:T(8,128)} %shard_map.47) | data formatting | bytes 4194304 | tf_op jit(solution)/shard_map/pallas_call | solution.py:95
  89.1 0.3 subtract_convert_fusion
  89.4 0.4 maximum_bitcast_fusion.o_ref
  89.8 14.8 %shard_map.48 = bf16[4,512,2,4096]{3,2,1,0:T(2,128)(2,1)} custom-call(bf16[4,1024,96]{2,1,0:T(8,128)(2,1)S(1)} %pad_maximum_fusion.l_ref, bf16[4,96,4096]{2,1,0:T(8,128)(2,1)S(1)} %maximum_bitcast_fusion.o_ref), custom_call_target="tpu_custom_call" | custom-call | tf_op jit(solution)/shard_map/pallas_call | solution.py:122
  (14 shorter events, 0.2 us)
Async XLA Ops:
  6.5 73.4 %all-gather.2.cloned.1.call-start = ((), (), s32[]{:S(2)}) async-start(), calls=%async_computation | async-start | bytes 2359296 | tf_op jit(solution)/shard_map/all_gather | solution.py:159
  38.7 6.0 %collective-permute-start.2 = (f32[128,4,2,16]{0,3,2,1:T(8,128)S(1)}, f32[128,4,2,16]{0,3,2,1:T(8,128)S(1)}, u32[]{:S(2)}, u32[]{:S(2)}) collective-permute-start(f32[128,4,2,16]{0,3,2,1:T(8,128)S(1)} %bitcast.67), channel_id=1, source_target_pairs={{0,24},{8,0},{16,8},{24,16},{1,25},{9,1},{17,9},{25,17},{2,26},{10... | collective-permute-start | bytes 196616 | tf_op jit(solution)/shard_map/ppermute | solution.py:141
  42.7 5.2 %collective-permute-start = (f32[128,4,2,16]{0,3,2,1:T(8,128)S(1)}, f32[128,4,2,16]{0,3,2,1:T(8,128)S(1)}, u32[]{:S(2)}, u32[]{:S(2)}) collective-permute-start(f32[128,4,2,16]{0,3,2,1:T(8,128)S(1)} %bitcast.68), channel_id=1, source_target_pairs={{0,8},{8,16},{16,24},{24,0},{1,9},{9,17},{17,25},{25,1},{2,10},{10... | collective-permute-start | bytes 196616 | tf_op jit(solution)/shard_map/ppermute | solution.py:141
  42.8 5.1 %collective-permute-start.1 = (f32[128,4,2,16]{0,3,2,1:T(8,128)S(1)}, f32[128,4,2,16]{0,3,2,1:T(8,128)S(1)}, u32[]{:S(2)}, u32[]{:S(2)}) collective-permute-start(f32[128,4,2,16]{0,3,2,1:T(8,128)S(1)} %bitcast.69), channel_id=1, source_target_pairs={{0,16},{8,24},{16,0},{24,8},{1,17},{9,25},{17,1},{25,9},{2,18},{10... | collective-permute-start | bytes 196616 | tf_op jit(solution)/shard_map/ppermute | solution.py:141
  48.0 1.8 %copy-start = (s32[2048]{0:T(1024)S(1)}, s32[2048]{0:T(1024)}, u32[]{:S(2)}) copy-start(s32[2048]{0:T(1024)} %param.7) | copy-start | bytes 24580
Sparse Core Ops, SparseCore 0:
  49.9 30.0 all-gather.1

commit v6 on v5

--- a/solution.py
+++ b/solution.py
@@ -1,3 +1,4 @@
+import functools
 import math
 
 import jax
@@ -42,8 +43,9 @@
         o_ref[...] = acc
 
 
-def frame_products(voltages, weights, fft_length, group, spectra):
+def frame_products(voltages, weights, fft_length, group, spectra, part, parts):
     rows, samples = voltages.shape
+    rows = rows // parts
     frames = samples // fft_length
     steps = -(-frames // group)
     width, _ = weights.shape
@@ -52,7 +54,7 @@
         _frame_kernel,
         grid=(steps,),
         in_specs=[
-            pl.BlockSpec((rows, group * fft_length), lambda f: (0, f)),
+            pl.BlockSpec((rows, group * fft_length), lambda f: (part, f)),
             pl.BlockSpec((width, fft_length), lambda f: (0, 0)),
         ],
         out_specs=pl.BlockSpec((spectra, rows, cols), lambda f: (0, 0, 0)),
@@ -62,15 +64,12 @@
     )(voltages, weights)
 
 
-def channelize(voltages, filter_taps, channel_index):
+def tap_weights(filter_taps, channel_index):
     tap_count, fft_length = filter_taps.shape
-    frame_count = voltages.shape[1] // fft_length
-    spectra = frame_count - tap_count + 1
     twiddle = phase_table_t(channel_index, fft_length).astype(jnp.float32)
     cols = twiddle.shape[0]
     weights = (filter_taps[:, None, :] * twiddle[None, :, :]).astype(jnp.bfloat16)
-    weights = weights.reshape(tap_count * cols, fft_length)
-    return frame_products(voltages, weights, fft_length, 4, spectra)
+    return weights.reshape(tap_count * cols, fft_length)
 
 
 def slot_index(antenna_slot_order):
@@ -81,27 +80,37 @@
     )
 
 
-def _perm_kernel(inv_ref, e_ref, o_ref):
+def _perm_kernel(part_rows, inv_ref, *refs):
+    srcs, o_ref = refs[:-1], refs[-1]
+    parts = len(srcs)
+
     def body(a, carry):
-        src = inv_ref[a] * 2
-        o_ref[pl.ds(2 * a, 2), :] = e_ref[pl.ds(src, 2), :]
+        u = inv_ref[a] * 2
+        h = (u // part_rows) % parts
+        row = (u // (parts * part_rows)) * part_rows + u % part_rows
+        val = srcs[0][pl.ds(row, 2), :]
+        for k in range(1, parts):
+            val = jnp.where(h == k, srcs[k][pl.ds(row, 2), :], val)
+        o_ref[pl.ds(2 * a, 2), :] = val
         return carry
 
     lax.fori_loop(0, inv_ref.shape[0], body, 0, unroll=8)
 
 
-def permute_pairs(everything, inverse):
-    rows, width = everything.shape
+def permute_pairs(parts_list, inverse, part_rows):
+    rows, width = parts_list[0].shape
+    total = rows * len(parts_list)
+    spec = pl.BlockSpec((rows, width), lambda i, inv: (0, 0))
     return pl.pallas_call(
-        _perm_kernel,
+        functools.partial(_perm_kernel, part_rows),
         grid_spec=pltpu.PrefetchScalarGridSpec(
             num_scalar_prefetch=1,
             grid=(1,),
-            in_specs=[pl.BlockSpec((rows, width), lambda i, inv: (0, 0))],
-            out_specs=pl.BlockSpec((rows, width), lambda i, inv: (0, 0)),
+            in_specs=[spec] * len(parts_list),
+            out_specs=pl.BlockSpec((total, width), lambda i, inv: (0, 0)),
         ),
-        out_shape=jax.ShapeDtypeStruct((rows, width), everything.dtype),
-    )(inverse, everything)
+        out_shape=jax.ShapeDtypeStruct((total, width), parts_list[0].dtype),
+    )(inverse, *parts_list)
 
 
 def split2(x):
@@ -147,18 +156,30 @@
 
 
 def per_device(voltages, filter_taps, channel_index, antenna_slot_order):
-    spec = channelize(voltages, filter_taps, channel_index)
-    spectra, rows, cols = spec.shape
-    chans = cols // 2
+    rows = voltages.shape[0]
+    parts = 2 if rows % 32 == 0 else 1
+    weights = tap_weights(filter_taps, channel_index)
+    tap_count, fft_length = filter_taps.shape
+    spectra = voltages.shape[1] // fft_length - tap_count + 1
     grp = lax.psum(1, "grp")
-    local_ch = chans // grp
-    x = spec.reshape(spectra, rows, 2, chans).transpose(1, 3, 2, 0)
-    x = exchange_channels(x, grp, local_ch)
-    slots_local = x.shape[0]
+    locals_, gathered = [], []
+    for h in range(parts):
+        spec = frame_products(voltages, weights, fft_length, 4, spectra, h, parts)
+        _, part_rows, cols = spec.shape
+        chans = cols // 2
+        local_ch = chans // grp
+        x = spec.reshape(spectra, part_rows, 2, chans).transpose(1, 3, 2, 0)
+        x = exchange_channels(x, grp, local_ch)
+        x = x.reshape(grp, part_rows, local_ch * 2 * spectra)
+        locals_.append(x)
+        send = x.reshape(grp * part_rows, -1)
+        voltages, send = lax.optimization_barrier((voltages, send))
+        gathered.append(lax.all_gather(send, "blk", axis=0, tiled=True))
+    x = jnp.stack(locals_, axis=1)
+    slots_local = grp * parts * part_rows
     x = x.reshape(slots_local, local_ch * 2 * spectra)
-    everything = lax.all_gather(x, "blk", axis=0, tiled=True)
     inverse = slot_index(antenna_slot_order)
-    ordered = permute_pairs(everything, inverse)
+    ordered = permute_pairs(gathered, inverse, part_rows)
     ordered = ordered.reshape(-1, local_ch, 2 * spectra).transpose(1, 0, 2)
     scale = jnp.float32(1.0 / spectra)
     xl = x.reshape(slots_local, local_ch, 2, spectra).transpose(1, 0, 2, 3) * scale

time: 112 us -> 145 us (1.29)
  Pallas kernels: 45.7 us -> 75.4 us
  local copies, waits for them, and re-layouts: 5.6 us -> 10.2 us
  waiting for transfers between devices: 29.2 us -> 25.4 us
  starting transfers between devices: 5.18 us -> 8.29 us
    pallas_call x1, Pallas kernels: 7.18 us -> 30.8 us  [permute_pairs(): pl.pallas_call(functools.partial(_perm_kernel, part_rows), grid_spec=pltp...]
    all_gather x1 -> x2, waiting for transfers between devices: 25.3 us -> 17.2 us  [per_device(): gathered.append(lax.all_gather(send, 'blk', axis=0, tiled=True))]
    pallas_call x1 -> x2, Pallas kernels: 23.7 us -> 29.7 us  [frame_products(): pl.pallas_call(_frame_kernel, grid=(steps,), in_specs=[pl.BlockSpec((rows...]
    ppermute x3 -> x6, waiting for transfers between devices: 3.85 us -> 8.16 us  [exchange_channels(): part = lax.ppermute(part, 'grp', [(j, (j + d) % grp) for j in range(grp)])]
    ppermute x3 -> x6, starting transfers between devices: 5.18 us -> 8.25 us  [exchange_channels(): part = lax.ppermute(part, 'grp', [(j, (j + d) % grp) for j in range(grp)])]
    optimization_barrier x0 -> x2, local copies, waits for them, and re-layouts: none -> 1.51 us  [per_device(): voltages, send = lax.optimization_barrier((voltages, send))]
  transfers between devices with their start and end apart: 4 -> 8, of which waited for: 3 -> 5; matrix products, arithmetic and copies ran while one was open for 4% -> 6% of each run, Pallas kernels for 0% -> 10%
where the time goes in v6:
time: 145 us; the launch traced here: 144 us
  Pallas kernels  75.4 us (52%)
  waiting for transfers between devices  25.4 us (18%)
  between operations  13.7 us (9%)
  other arithmetic  11.4 us (8%)
  local copies, waits for them, and re-layouts  10.2 us (7%)
  starting transfers between devices  8.29 us (6%)
    pallas_call x1, Pallas kernels, permute_pairs(): pl.pallas_call(functools.partial(_perm_kernel, part_rows), grid_spec=pltp...  30.8 us
    pallas_call x2, Pallas kernels, frame_products(): pl.pallas_call(_frame_kernel, grid=(steps,), in_specs=[pl.BlockSpec((rows...  29.7 us
    all_gather x2, waiting for transfers between devices, per_device(): gathered.append(lax.all_gather(send, 'blk', axis=0, tiled=True))  17.2 us
    pallas_call x1, Pallas kernels, correlate(): pl.pallas_call(_corr_kernel, grid=(chans, slots // block_rows), in_specs=...  14.8 us
    ppermute x6, starting transfers between devices, exchange_channels(): part = lax.ppermute(part, 'grp', [(j, (j + d) % grp) for j in range(grp)])  8.25 us
    ppermute x6, waiting for transfers between devices, exchange_channels(): part = lax.ppermute(part, 'grp', [(j, (j + d) % grp) for j in range(grp)])  8.16 us
    convert_element_type x1, other arithmetic, tap_weights(): (filter_taps[:, None, :] * twiddle[None, :, :]).astype(jnp.bfloat16)  3.6 us
    another operation x1, other arithmetic  3.15 us
  transfers between devices with their start and end apart: 8, of which 5 were waited for; matrix products, arithmetic and copies ran while one was open for 6% of the time, Pallas kernels for 10%

profile of v6, /device:TPU:0, one launch (start us, length us, event | category | flops | bytes accessed | tf_op | source)
XLA Modules:
  0.0 144.4 jit_solution(3700363381165882675)
XLA Ops:
  6.5 3.1 %cosine_convert_fusion = (bf16[16,8192]{1,0:T(8,128)(2,1)S(1)}, bf16[16,8192]{1,0:T(8,128)(2,1)S(1)}) fusion(s32[16]{0:T(128)} %param.8), kind=kLoop, calls=%fused_computation.18 | loop fusion | flops 2228224 | bytes 524352 | tf_op jit(solution)/shard_map/convert
  9.8 3.6 %multiply_convert_fusion = bf16[8,32,8192]{2,1,0:T(8,128)(2,1)} fusion(f32[32,8192]{1,0:T(8,128)S(1)} %maximum_convert_fusion, f32[8,8192]{1,0:T(8,128)} %param.7), kind=kLoop, calls=%fused_computation.4 | loop fusion | flops 4194304 | bytes 5505024 | tf_op jit(solution)/shard_map/convert_element_type | solution.py:71
  13.4 14.8 %shard_map.46 = f32[16,64,32]{2,1,0:T(8,128)} custom-call(bf16[128,188416]{1,0:T(8,128)(2,1)} %v_ref.2, bf16[256,8192]{1,0:T(8,128)(2,1)} %bitcast.64), custom_call_target="tpu_custom_call" | custom-call | tf_op jit(solution)/shard_map/pallas_call | solution.py:53
  28.2 1.2 copy.43
  29.5 4.0 %collective-permute-start.2 = (f32[64,4,2,16]{0,3,2,1:T(8,128)S(1)}, f32[64,4,2,16]{0,3,2,1:T(8,128)S(1)}, u32[]{:S(2)}, u32[]{:S(2)}) collective-permute-start(f32[64,4,2,16]{0,3,2,1:T(8,128)S(1)} %bitcast.78), channel_id=1, source_target_pairs={{0,24},{8,0},{16,8},{24,16},{1,25},{9,1},{17,9},{25,17},{2,26},{10... | collective-permute-start | bytes 98312 | tf_op jit(solution)/shard_map/ppermute | solution.py:150
  33.6 1.1 collective-permute-start.1
  34.8 0.7 collective-permute-done.2
  35.6 3.2 %collective-permute-done = f32[64,4,2,16]{0,3,2,1:T(8,128)S(1)} collective-permute-done((f32[64,4,2,16]{0,3,2,1:T(8,128)S(1)}, f32[64,4,2,16]{0,3,2,1:T(8,128)S(1)}, u32[]{:S(2)}, u32[]{:S(2)}) %collective-permute-start) | collective-permute-done | bytes 32800 | tf_op jit(solution)/shard_map/ppermute | solution.py:150
  38.8 0.6 gather_fusion
  39.5 0.2 copy.48
  39.6 0.2 reshape_reshape_reshape.6
  39.8 0.8 copy.59
  40.7 14.9 %shard_map.47 = f32[16,64,32]{2,1,0:T(8,128)} custom-call(bf16[128,188416]{1,0:T(8,128)(2,1)} %v_ref.2, bf16[256,8192]{1,0:T(8,128)(2,1)} %bitcast.65), custom_call_target="tpu_custom_call" | custom-call | tf_op jit(solution)/shard_map/pallas_call | solution.py:53
  55.6 1.2 copy.49
  57.0 2.2 %collective-permute-start.5 = (f32[64,4,2,16]{0,3,2,1:T(8,128)S(1)}, f32[64,4,2,16]{0,3,2,1:T(8,128)S(1)}, u32[]{:S(2)}, u32[]{:S(2)}) collective-permute-start(f32[64,4,2,16]{0,3,2,1:T(8,128)S(1)} %bitcast.82), channel_id=1, source_target_pairs={{0,24},{8,0},{16,8},{24,16},{1,25},{9,1},{17,9},{25,17},{2,26},{10... | collective-permute-start | bytes 98312 | tf_op jit(solution)/shard_map/ppermute | solution.py:150
  59.2 0.9 collective-permute-start.4
  60.1 1.7 %collective-permute-done.5 = f32[64,4,2,16]{0,3,2,1:T(8,128)S(1)} collective-permute-done((f32[64,4,2,16]{0,3,2,1:T(8,128)S(1)}, f32[64,4,2,16]{0,3,2,1:T(8,128)S(1)}, u32[]{:S(2)}, u32[]{:S(2)}) %collective-permute-start.5) | collective-permute-done | bytes 32800 | tf_op jit(solution)/shard_map/ppermute | solution.py:150
  61.7 2.6 %collective-permute-done.3 = f32[64,4,2,16]{0,3,2,1:T(8,128)S(1)} collective-permute-done((f32[64,4,2,16]{0,3,2,1:T(8,128)S(1)}, f32[64,4,2,16]{0,3,2,1:T(8,128)S(1)}, u32[]{:S(2)}, u32[]{:S(2)}) %collective-permute-start.3) | collective-permute-done | bytes 32800 | tf_op jit(solution)/shard_map/ppermute | solution.py:150
  64.3 0.6 gather_fusion.1
  65.2 0.2 reshape_reshape_reshape.7
  65.4 0.8 copy.61
  66.2 2.3 %select_reduce_fusion.inv_ref = s32[2048]{0:T(1024)} fusion(s32[2048]{0:T(1024)S(1)} %copy-done), kind=kLoop, calls=%fused_computation.2 | loop fusion | flops 12580864 | bytes 16384 | tf_op jit(solution)/shard_map/reduce_sum | solution.py:78
  68.8 0.3 copy.56
  69.2 0.5 mul.84
  69.8 1.0 copy.58
  71.2 1.0 pad_maximum_fusion.l_ref
  72.1 17.2 %all-gather.5.cloned.1.call-done.refs_1_ = f32[2048,128]{1,0:T(8,128)} async-done(((f32[256,128]{1,0:T(8,128)}), f32[2048,128]{1,0:T(8,128)}) %all-gather.5.cloned.1.call-update) | async-done | bytes 1048592 | tf_op jit(solution)/shard_map/all_gather | solution.py:177
  89.4 30.8 %shard_map.48 = f32[4096,128]{1,0:T(8,128)} custom-call(s32[2048]{0:T(1024)} %select_reduce_fusion.inv_ref, f32[2048,128]{1,0:T(8,128)} %all-gather.3.cloned.1.call-done.refs_0_, f32[2048,128]{1,0:T(8,128)} %all-gather.5.cloned.1.call-done.refs_1_), custom_call_target="tpu_custom_call" | custom-call | tf_op jit(solution)/shard_map/pallas_call | solution.py:104
  120.2 1.9 %copy.62 = f32[4096,128]{0,1:T(8,128)S(1)} copy(f32[4096,128]{1,0:T(8,128)} %shard_map.48) | data formatting | bytes 4194304 | tf_op jit(solution)/shard_map/pallas_call | solution.py:104
  122.1 0.3 subtract_convert_fusion
  122.4 0.3 maximum_bitcast_fusion.o_ref
  122.7 14.8 %shard_map.49 = bf16[4,512,2,4096]{3,2,1,0:T(2,128)(2,1)} custom-call(bf16[4,1024,96]{2,1,0:T(8,128)(2,1)S(1)} %pad_maximum_fusion.l_ref, bf16[4,96,4096]{2,1,0:T(8,128)(2,1)S(1)} %maximum_bitcast_fusion.o_ref), custom_call_target="tpu_custom_call" | custom-call | tf_op jit(solution)/shard_map/pallas_call | solution.py:131
  (39 shorter events, 1.6 us)
Async XLA Ops:
  6.5 65.6 %all-gather.3.cloned.1.call-start = ((), (), s32[]{:S(2)}) async-start(), calls=%async_computation | async-start | bytes 1179648 | tf_op jit(solution)/shard_map/all_gather | solution.py:177
  29.5 6.0 %collective-permute-start.2 = (f32[64,4,2,16]{0,3,2,1:T(8,128)S(1)}, f32[64,4,2,16]{0,3,2,1:T(8,128)S(1)}, u32[]{:S(2)}, u32[]{:S(2)}) collective-permute-start(f32[64,4,2,16]{0,3,2,1:T(8,128)S(1)} %bitcast.78), channel_id=1, source_target_pairs={{0,24},{8,0},{16,8},{24,16},{1,25},{9,1},{17,9},{25,17},{2,26},{10... | collective-permute-start | bytes 98312 | tf_op jit(solution)/shard_map/ppermute | solution.py:150
  33.5 5.2 %collective-permute-start = (f32[64,4,2,16]{0,3,2,1:T(8,128)S(1)}, f32[64,4,2,16]{0,3,2,1:T(8,128)S(1)}, u32[]{:S(2)}, u32[]{:S(2)}) collective-permute-start(f32[64,4,2,16]{0,3,2,1:T(8,128)S(1)} %bitcast.79), channel_id=1, source_target_pairs={{0,8},{8,16},{16,24},{24,0},{1,9},{9,17},{17,25},{25,1},{2,10},{10... | collective-permute-start | bytes 98312 | tf_op jit(solution)/shard_map/ppermute | solution.py:150
  33.6 5.1 %collective-permute-start.1 = (f32[64,4,2,16]{0,3,2,1:T(8,128)S(1)}, f32[64,4,2,16]{0,3,2,1:T(8,128)S(1)}, u32[]{:S(2)}, u32[]{:S(2)}) collective-permute-start(f32[64,4,2,16]{0,3,2,1:T(8,128)S(1)} %bitcast.81), channel_id=1, source_target_pairs={{0,16},{8,24},{16,0},{24,8},{1,17},{9,25},{17,1},{25,9},{2,18},{10... | collective-permute-start | bytes 98312 | tf_op jit(solution)/shard_map/ppermute | solution.py:150
  40.6 48.8 %all-gather.5.cloned.1.call-start = ((), (), s32[]{:S(2)}) async-start(), calls=%async_computation.1 | async-start | bytes 1179648 | tf_op jit(solution)/shard_map/all_gather | solution.py:177
  55.6 10.6 %copy-start = (s32[2048]{0:T(1024)S(1)}, s32[2048]{0:T(1024)}, u32[]{:S(2)}) copy-start(s32[2048]{0:T(1024)} %param.9) | copy-start | bytes 24580
  57.0 4.7 %collective-permute-start.5 = (f32[64,4,2,16]{0,3,2,1:T(8,128)S(1)}, f32[64,4,2,16]{0,3,2,1:T(8,128)S(1)}, u32[]{:S(2)}, u32[]{:S(2)}) collective-permute-start(f32[64,4,2,16]{0,3,2,1:T(8,128)S(1)} %bitcast.82), channel_id=1, source_target_pairs={{0,24},{8,0},{16,8},{24,16},{1,25},{9,1},{17,9},{25,17},{2,26},{10... | collective-permute-start | bytes 98312 | tf_op jit(solution)/shard_map/ppermute | solution.py:150
  59.2 5.2 %collective-permute-start.3 = (f32[64,4,2,16]{0,3,2,1:T(8,128)S(1)}, f32[64,4,2,16]{0,3,2,1:T(8,128)S(1)}, u32[]{:S(2)}, u32[]{:S(2)}) collective-permute-start(f32[64,4,2,16]{0,3,2,1:T(8,128)S(1)} %bitcast.80), channel_id=1, source_target_pairs={{0,8},{8,16},{16,24},{24,0},{1,9},{9,17},{17,25},{25,1},{2,10},{10... | collective-permute-start | bytes 98312 | tf_op jit(solution)/shard_map/ppermute | solution.py:150
  59.2 5.2 %collective-permute-start.4 = (f32[64,4,2,16]{0,3,2,1:T(8,128)S(1)}, f32[64,4,2,16]{0,3,2,1:T(8,128)S(1)}, u32[]{:S(2)}, u32[]{:S(2)}) collective-permute-start(f32[64,4,2,16]{0,3,2,1:T(8,128)S(1)} %bitcast.77), channel_id=1, source_target_pairs={{0,16},{8,24},{16,0},{24,8},{1,17},{9,25},{17,1},{25,9},{2,18},{10... | collective-permute-start | bytes 98312 | tf_op jit(solution)/shard_map/ppermute | solution.py:150
Sparse Core Ops, SparseCore 0:
  40.7 23.1 all-gather.2
  66.3 23.0 all-gather.4

commit v7 on v5

--- a/solution.py
+++ b/solution.py
@@ -1,3 +1,4 @@
+import functools
 import math
 
 import jax
@@ -22,43 +23,74 @@
     return jnp.concatenate([jnp.cos(angle), -jnp.sin(angle)], axis=0).astype(jnp.bfloat16)
 
 
-def _frame_kernel(v_ref, w_ref, o_ref, p_ref):
-    i = pl.program_id(0)
-    n = w_ref.shape[1]
+def _frame_kernel(chunk, v_hbm, w_ref, o_ref, buf, acc, sem):
     spectra, rows, cols = o_ref.shape
-    group = p_ref.shape[0] // pl.num_programs(0)
-    lhs = jnp.concatenate([v_ref[:, g * n : (g + 1) * n] for g in range(group)], axis=0)
-    res = lax.dot_general(
-        lhs, w_ref[...], (((1,), (1,)), ((), ())), preferred_element_type=jnp.float32
-    )
-    p_ref[pl.ds(i * group, group)] = res.reshape(group, rows, res.shape[1])
-
-    @pl.when(i == pl.num_programs(0) - 1)
-    def _():
-        taps = res.shape[1] // cols
-        acc = p_ref[0:spectra, :, 0:cols]
-        for m in range(1, taps):
-            acc = acc + p_ref[m : m + spectra, :, m * cols : (m + 1) * cols]
-        o_ref[...] = acc
-
-
-def frame_products(voltages, weights, fft_length, group, spectra):
+    width, n = w_ref.shape
+    frames = buf.shape[1] // rows
+    chunks = n // chunk
+
+    def copies(k, slot):
+        return [
+            pltpu.make_async_copy(
+                v_hbm.at[:, pl.ds(f * n + k * chunk, chunk)],
+                buf.at[slot, pl.ds(f * rows, rows), :],
+                sem.at[slot, f],
+            )
+            for f in range(frames)
+        ]
+
+    for c in copies(0, 0):
+        c.start()
+    acc[...] = jnp.zeros(acc.shape, acc.dtype)
+
+    def step(k, carry):
+        slot = k % 2
+
+        @pl.when(k + 1 < chunks)
+        def _():
+            for c in copies(k + 1, 1 - slot):
+                c.start()
+
+        for c in copies(k, slot):
+            c.wait()
+        start = pl.multiple_of(k * chunk, chunk)
+        acc[...] += lax.dot_general(
+            buf[slot],
+            w_ref[:, pl.ds(start, chunk)],
+            (((1,), (1,)), ((), ())),
+            preferred_element_type=jnp.float32,
+        )
+        return carry
+
+    lax.fori_loop(0, chunks, step, 0)
+    taps = width // cols
+    total = acc[...].reshape(frames, rows, width)
+    out = total[0:spectra, :, 0:cols]
+    for m in range(1, taps):
+        out = out + total[m : m + spectra, :, m * cols : (m + 1) * cols]
+    o_ref[...] = out
+
+
+def frame_products(voltages, weights, fft_length, spectra):
     rows, samples = voltages.shape
     frames = samples // fft_length
-    steps = -(-frames // group)
     width, _ = weights.shape
     cols = width // (frames - spectra + 1)
+    chunk = 1024
     return pl.pallas_call(
-        _frame_kernel,
-        grid=(steps,),
+        functools.partial(_frame_kernel, chunk),
         in_specs=[
-            pl.BlockSpec((rows, group * fft_length), lambda f: (0, f)),
-            pl.BlockSpec((width, fft_length), lambda f: (0, 0)),
+            pl.BlockSpec(memory_space=pl.ANY),
+            pl.BlockSpec(memory_space=pltpu.VMEM),
         ],
-        out_specs=pl.BlockSpec((spectra, rows, cols), lambda f: (0, 0, 0)),
+        out_specs=pl.BlockSpec(memory_space=pltpu.VMEM),
         out_shape=jax.ShapeDtypeStruct((spectra, rows, cols), jnp.float32),
-        scratch_shapes=[pltpu.VMEM((steps * group, rows, width), jnp.float32)],
-        compiler_params=pltpu.CompilerParams(vmem_limit_bytes=56 * 1024 * 1024),
+        scratch_shapes=[
+            pltpu.VMEM((2, frames * rows, chunk), voltages.dtype),
+            pltpu.VMEM((frames * rows, width), jnp.float32),
+            pltpu.SemaphoreType.DMA((2, frames)),
+        ],
+        compiler_params=pltpu.CompilerParams(vmem_limit_bytes=60 * 1024 * 1024),
     )(voltages, weights)
 
 
@@ -70,7 +102,7 @@
     cols = twiddle.shape[0]
     weights = (filter_taps[:, None, :] * twiddle[None, :, :]).astype(jnp.bfloat16)
     weights = weights.reshape(tap_count * cols, fft_length)
-    return frame_products(voltages, weights, fft_length, 4, spectra)
+    return frame_products(voltages, weights, fft_length, spectra)
 
 
 def slot_index(antenna_slot_order):

time: 112 us -> 113 us (level)
  Pallas kernels: 45.7 us -> 47.4 us
    pallas_call x1, Pallas kernels: 23.7 us -> 25.4 us  [frame_products(): pl.pallas_call(functools.partial(_frame_kernel, chunk), in_specs=[pl.Bloc...]
where the time goes in v7:
time: 113 us
  Pallas kernels  47.4 us (42%)
  waiting for transfers between devices  29.2 us (26%)
  between operations  13.6 us (12%)
  other arithmetic  12.1 us (11%)
  local copies, waits for them, and re-layouts  5.6 us (5%)
  starting transfers between devices  5.17 us (5%)
    pallas_call x1, Pallas kernels, frame_products(): pl.pallas_call(functools.partial(_frame_kernel, chunk), in_specs=[pl.Bloc...  25.4 us
    all_gather x1, waiting for transfers between devices, per_device(): everything = lax.all_gather(x, 'blk', axis=0, tiled=True)  25.3 us
    pallas_call x1, Pallas kernels, correlate(): pl.pallas_call(_corr_kernel, grid=(chans, slots // block_rows), in_specs=...  14.8 us
    pallas_call x1, Pallas kernels, permute_pairs(): pl.pallas_call(_perm_kernel, grid_spec=pltpu.PrefetchScalarGridSpec(num_s...  7.18 us
    ppermute x3, starting transfers between devices, exchange_channels(): part = lax.ppermute(part, 'grp', [(j, (j + d) % grp) for j in range(grp)])  5.16 us
    ppermute x3, waiting for transfers between devices, exchange_channels(): part = lax.ppermute(part, 'grp', [(j, (j + d) % grp) for j in range(grp)])  3.86 us
    convert_element_type x1, other arithmetic, channelize(): (filter_taps[:, None, :] * twiddle[None, :, :]).astype(jnp.bfloat16)  3.6 us
    another operation x1, other arithmetic  3.15 us
  transfers between devices with their start and end apart: 4, of which 3 were waited for; matrix products, arithmetic and copies ran while one was open for 4% of the time, Pallas kernels for 0%

profile of v7, /device:TPU:0, one launch (start us, length us, event | category | flops | bytes accessed | tf_op | source)
XLA Modules:
  0.0 113.1 jit_solution(6639589979008460223)
XLA Ops:
  6.5 0.0 all-gather.2.cloned.1.call-start
  6.5 3.1 %cosine_convert_fusion = (bf16[16,8192]{1,0:T(8,128)(2,1)S(1)}, bf16[16,8192]{1,0:T(8,128)(2,1)S(1)}) fusion(s32[16]{0:T(128)} %param.6), kind=kLoop, calls=%fused_computation.17 | loop fusion | flops 2228224 | bytes 524352 | tf_op jit(solution)/shard_map/convert
  9.7 0.1 maximum_convert_fusion
  9.8 3.6 %multiply_convert_fusion = bf16[8,32,8192]{2,1,0:T(8,128)(2,1)} fusion(f32[32,8192]{1,0:T(8,128)S(1)} %maximum_convert_fusion, f32[8,8192]{1,0:T(8,128)} %param.5), kind=kLoop, calls=%fused_computation.3 | loop fusion | flops 4194304 | bytes 5505024 | tf_op jit(solution)/shard_map/convert_element_type | solution.py:103
  13.4 25.4 %shard_map.46 = f32[16,128,32]{2,1,0:T(8,128)} custom-call(bf16[128,188416]{1,0:T(8,128)(2,1)} %v_hbm.1, bf16[256,8192]{1,0:T(8,128)(2,1)} %bitcast.61), custom_call_target="tpu_custom_call" | custom-call | tf_op jit(solution)/shard_map/pallas_call | solution.py:80
  38.8 1.5 %copy.28 = f32[16,128,32]{1,2,0:T(8,128)S(1)} copy(f32[16,128,32]{2,1,0:T(8,128)} %shard_map.46) | data formatting | bytes 524288 | tf_op jit(solution)/shard_map/pallas_call | solution.py:80
  40.3 0.1 constant_dynamic-slice_fusion.3
  40.4 4.0 %collective-permute-start.2 = (f32[128,4,2,16]{0,3,2,1:T(8,128)S(1)}, f32[128,4,2,16]{0,3,2,1:T(8,128)S(1)}, u32[]{:S(2)}, u32[]{:S(2)}) collective-permute-start(f32[128,4,2,16]{0,3,2,1:T(8,128)S(1)} %bitcast.67), channel_id=1, source_target_pairs={{0,24},{8,0},{16,8},{24,16},{1,25},{9,1},{17,9},{25,17},{2,26},{10... | collective-permute-start | bytes 196616 | tf_op jit(solution)/shard_map/ppermute | solution.py:173
  44.4 0.1 collective-permute-start
  44.5 1.1 %collective-permute-start.1 = (f32[128,4,2,16]{0,3,2,1:T(8,128)S(1)}, f32[128,4,2,16]{0,3,2,1:T(8,128)S(1)}, u32[]{:S(2)}, u32[]{:S(2)}) collective-permute-start(f32[128,4,2,16]{0,3,2,1:T(8,128)S(1)} %bitcast.69), channel_id=1, source_target_pairs={{0,16},{8,24},{16,0},{24,8},{1,17},{9,25},{17,1},{25,9},{2,18},{10... | collective-permute-start | bytes 196616 | tf_op jit(solution)/shard_map/ppermute | solution.py:173
  45.7 0.1 broadcast_bitcast_fusion
  45.8 0.7 collective-permute-done.2
  46.4 3.2 %collective-permute-done = f32[128,4,2,16]{0,3,2,1:T(8,128)S(1)} collective-permute-done((f32[128,4,2,16]{0,3,2,1:T(8,128)S(1)}, f32[128,4,2,16]{0,3,2,1:T(8,128)S(1)}, u32[]{:S(2)}, u32[]{:S(2)}) %collective-permute-start) | collective-permute-done | bytes 65568 | tf_op jit(solution)/shard_map/ppermute | solution.py:173
  49.6 0.0 collective-permute-done.1
  49.6 0.0 copy-start
  49.7 0.6 gather_fusion
  50.2 0.2 copy.33
  50.4 0.1 copy.37
  50.6 0.8 broadcast_select_fusion
  51.4 0.0 all-gather.2.cloned.1.call-update
  51.4 2.3 %select_reduce_fusion.inv_ref = s32[2048]{0:T(1024)} fusion(s32[2048]{0:T(1024)S(1)} %copy-done), kind=kLoop, calls=%fused_computation.1 | loop fusion | flops 12580864 | bytes 16384 | tf_op jit(solution)/shard_map/reduce_sum | solution.py:111
  53.9 0.1 maximum_bitcast_fusion.1
  54.0 1.0 copy.35
  55.0 0.1 convert_element_type.53
  55.2 0.2 subtract_convert_fusion.1
  55.4 1.0 pad_maximum_fusion.l_ref
  56.3 25.3 %all-gather.2.cloned.1.call-done.e_ref = f32[4096,128]{1,0:T(8,128)} async-done(((f32[512,128]{1,0:T(8,128)}), f32[4096,128]{1,0:T(8,128)}) %all-gather.2.cloned.1.call-update) | async-done | bytes 2097168 | tf_op jit(solution)/shard_map/all_gather | solution.py:191
  81.6 7.2 %shard_map.47 = f32[4096,128]{1,0:T(8,128)} custom-call(s32[2048]{0:T(1024)} %select_reduce_fusion.inv_ref, f32[4096,128]{1,0:T(8,128)} %all-gather.2.cloned.1.call-done.e_ref), custom_call_target="tpu_custom_call" | custom-call | tf_op jit(solution)/shard_map/pallas_call | solution.py:127
  88.8 1.9 %copy.38 = f32[4096,128]{0,1:T(8,128)S(1)} copy(f32[4096,128]{1,0:T(8,128)} %shard_map.47) | data formatting | bytes 4194304 | tf_op jit(solution)/shard_map/pallas_call | solution.py:127
  90.8 0.3 subtract_convert_fusion
  91.1 0.4 maximum_bitcast_fusion.o_ref
  91.5 14.8 %shard_map.48 = bf16[4,512,2,4096]{3,2,1,0:T(2,128)(2,1)} custom-call(bf16[4,1024,96]{2,1,0:T(8,128)(2,1)S(1)} %pad_maximum_fusion.l_ref, bf16[4,96,4096]{2,1,0:T(8,128)(2,1)S(1)} %maximum_bitcast_fusion.o_ref), custom_call_target="tpu_custom_call" | custom-call | tf_op jit(solution)/shard_map/pallas_call | solution.py:154
  (14 shorter events, 0.2 us)
Async XLA Ops:
  6.5 75.1 %all-gather.2.cloned.1.call-start = ((), (), s32[]{:S(2)}) async-start(), calls=%async_computation | async-start | bytes 2359296 | tf_op jit(solution)/shard_map/all_gather | solution.py:191
  40.4 6.0 %collective-permute-start.2 = (f32[128,4,2,16]{0,3,2,1:T(8,128)S(1)}, f32[128,4,2,16]{0,3,2,1:T(8,128)S(1)}, u32[]{:S(2)}, u32[]{:S(2)}) collective-permute-start(f32[128,4,2,16]{0,3,2,1:T(8,128)S(1)} %bitcast.67), channel_id=1, source_target_pairs={{0,24},{8,0},{16,8},{24,16},{1,25},{9,1},{17,9},{25,17},{2,26},{10... | collective-permute-start | bytes 196616 | tf_op jit(solution)/shard_map/ppermute | solution.py:173
  44.4 5.2 %collective-permute-start = (f32[128,4,2,16]{0,3,2,1:T(8,128)S(1)}, f32[128,4,2,16]{0,3,2,1:T(8,128)S(1)}, u32[]{:S(2)}, u32[]{:S(2)}) collective-permute-start(f32[128,4,2,16]{0,3,2,1:T(8,128)S(1)} %bitcast.68), channel_id=1, source_target_pairs={{0,8},{8,16},{16,24},{24,0},{1,9},{9,17},{17,25},{25,1},{2,10},{10... | collective-permute-start | bytes 196616 | tf_op jit(solution)/shard_map/ppermute | solution.py:173
  44.5 5.1 %collective-permute-start.1 = (f32[128,4,2,16]{0,3,2,1:T(8,128)S(1)}, f32[128,4,2,16]{0,3,2,1:T(8,128)S(1)}, u32[]{:S(2)}, u32[]{:S(2)}) collective-permute-start(f32[128,4,2,16]{0,3,2,1:T(8,128)S(1)} %bitcast.69), channel_id=1, source_target_pairs={{0,16},{8,24},{16,0},{24,8},{1,17},{9,25},{17,1},{25,9},{2,18},{10... | collective-permute-start | bytes 196616 | tf_op jit(solution)/shard_map/ppermute | solution.py:173
  49.6 1.8 %copy-start = (s32[2048]{0:T(1024)S(1)}, s32[2048]{0:T(1024)}, u32[]{:S(2)}) copy-start(s32[2048]{0:T(1024)} %param.7) | copy-start | bytes 24580
Sparse Core Ops, SparseCore 0:
  51.6 30.0 all-gather.1

commit v8 on v5

--- a/solution.py
+++ b/solution.py
@@ -146,6 +146,30 @@
     return stacked.reshape((grp * x.shape[0],) + stacked.shape[2:])
 
 
+def gather_blocks(x):
+    count = lax.psum(1, "blk")
+    line = count // 2
+    me = lax.axis_index("blk")
+    pos, core = me // 2, me % 2
+    right = [(z * 2 + c, (z + 1) * 2 + c) for z in range(line - 1) for c in range(2)]
+    left = [(z * 2 + c, (z - 1) * 2 + c) for z in range(1, line) for c in range(2)]
+    got_r, got_l = [], []
+    r = x
+    l = x
+    for _ in range(1, line):
+        r = lax.ppermute(r, "blk", right)
+        l = lax.ppermute(l, "blk", left)
+        got_r.append(r)
+        got_l.append(l)
+    cands = jnp.stack([x] + got_r + got_l, axis=0)
+    zs = jnp.arange(line, dtype=jnp.int32)
+    idx = jnp.where(zs == pos, 0, jnp.where(zs < pos, pos - zs, line - 1 + zs - pos))
+    mine = jnp.take(cands, idx, axis=0)
+    other = lax.ppermute(mine, "blk", [(b, b ^ 1) for b in range(count)])
+    pair = jnp.where(core == 0, jnp.stack([mine, other], 1), jnp.stack([other, mine], 1))
+    return pair.reshape((count * x.shape[0],) + x.shape[1:])
+
+
 def per_device(voltages, filter_taps, channel_index, antenna_slot_order):
     spec = channelize(voltages, filter_taps, channel_index)
     spectra, rows, cols = spec.shape
@@ -156,7 +180,7 @@
     x = exchange_channels(x, grp, local_ch)
     slots_local = x.shape[0]
     x = x.reshape(slots_local, local_ch * 2 * spectra)
-    everything = lax.all_gather(x, "blk", axis=0, tiled=True)
+    everything = gather_blocks(x)
     inverse = slot_index(antenna_slot_order)
     ordered = permute_pairs(everything, inverse)
     ordered = ordered.reshape(-1, local_ch, 2 * spectra).transpose(1, 0, 2)

time: 112 us -> 109 us (0.973)
  waiting for transfers between devices: 29.2 us -> 10.1 us
  starting transfers between devices: 5.18 us -> 21.4 us
  between operations: 13.6 us -> 0.3 us
  local copies, waits for them, and re-layouts: 5.6 us -> 15.5 us
  other arithmetic: 12.1 us -> 15.4 us
    all_gather x1 -> x0, waiting for transfers between devices: 25.3 us -> none  [per_device(): everything = lax.all_gather(x, 'blk', axis=0, tiled=True)]
    ppermute x0 -> x7, starting transfers between devices: none -> 16.3 us  [the longest x3 12.3 us: gather_blocks(): r = lax.ppermute(r, 'blk', right)]
    ppermute x0 -> x7, waiting for transfers between devices: none -> 7.99 us  [the longest x3 5.01 us: gather_blocks(): r = lax.ppermute(r, 'blk', right)]
    unnamed x7 -> x9, local copies, waits for them, and re-layouts: 0.08 us -> 3.62 us
    select_n x0 -> x4, other arithmetic: none -> 3.37 us  [the longest x1 1.97 us: gather_blocks(): jnp.where(core == 0, jnp.stack([mine, other], 1), jnp.stack([other, mine]...]
    gather x0 -> x1, local copies, waits for them, and re-layouts: none -> 2.11 us  [gather_blocks(): mine = jnp.take(cands, idx, axis=0)]
    select_n x0 -> x1, local copies, waits for them, and re-layouts: none -> 1.81 us  [gather_blocks(): jnp.where(core == 0, jnp.stack([mine, other], 1), jnp.stack([other, mine]...]
    ppermute x3, waiting for transfers between devices: 3.85 us -> 2.07 us  [exchange_channels(): part = lax.ppermute(part, 'grp', [(j, (j + d) % grp) for j in range(grp)])]
  transfers between devices with their start and end apart: 4 -> 10, of which waited for: 3 -> 6; matrix products, arithmetic and copies ran while one was open for 4% -> 11% of each run, Pallas kernels for 0% -> 0%
where the time goes in v8:
time: 109 us; the launch traced here: 108 us
  Pallas kernels  45.8 us (42%)
  starting transfers between devices  21.4 us (20%)
  local copies, waits for them, and re-layouts  15.5 us (14%)
  other arithmetic  15.4 us (14%)
  waiting for transfers between devices  10.1 us (9%)
    pallas_call x1, Pallas kernels, frame_products(): pl.pallas_call(_frame_kernel, grid=(steps,), in_specs=[pl.BlockSpec((rows...  23.7 us
    pallas_call x1, Pallas kernels, correlate(): pl.pallas_call(_corr_kernel, grid=(chans, slots // block_rows), in_specs=...  14.8 us
    ppermute x3, starting transfers between devices, gather_blocks(): r = lax.ppermute(r, 'blk', right)  12.3 us
    pallas_call x1, Pallas kernels, permute_pairs(): pl.pallas_call(_perm_kernel, grid_spec=pltpu.PrefetchScalarGridSpec(num_s...  7.2 us
    ppermute x3, starting transfers between devices, exchange_channels(): part = lax.ppermute(part, 'grp', [(j, (j + d) % grp) for j in range(grp)])  5.07 us
    ppermute x3, waiting for transfers between devices, gather_blocks(): r = lax.ppermute(r, 'blk', right)  5.01 us
    ppermute x3, starting transfers between devices, gather_blocks(): l = lax.ppermute(l, 'blk', left)  4.03 us
    unnamed x9, local copies, waits for them, and re-layouts  3.62 us
  transfers between devices with their start and end apart: 10, of which 6 were waited for; matrix products, arithmetic and copies ran while one was open for 11% of the time, Pallas kernels for 0%

profile of v8, /device:TPU:0, one launch (start us, length us, event | category | flops | bytes accessed | tf_op | source)
XLA Modules:
  0.0 108.5 jit_solution(15064077910219747429)
XLA Ops:
  0.0 3.2 %cosine_convert_fusion = (bf16[16,8192]{1,0:T(8,128)(2,1)S(1)}, bf16[16,8192]{1,0:T(8,128)(2,1)S(1)}) fusion(s32[16]{0:T(128)} %param.6), kind=kLoop, calls=%fused_computation.21 | loop fusion | flops 2228224 | bytes 524352 | tf_op jit(solution)/shard_map/convert
  3.3 2.7 %multiply_convert_fusion = bf16[8,32,8192]{2,1,0:T(8,128)(2,1)} fusion(f32[32,8192]{1,0:T(8,128)S(1)} %maximum_convert_fusion, f32[8,8192]{1,0:T(8,128)S(1)} %copy-done), kind=kLoop, calls=%fused_computation.4 | loop fusion | flops 4194304 | bytes 5505024 | tf_op jit(solution)/shard_map/convert_element_type | solution.py:71
  5.9 23.7 %shard_map.46 = f32[16,128,32]{2,1,0:T(8,128)} custom-call(bf16[128,188416]{1,0:T(8,128)(2,1)} %v_ref.1, bf16[256,8192]{1,0:T(8,128)(2,1)} %bitcast.69), custom_call_target="tpu_custom_call" | custom-call | tf_op jit(solution)/shard_map/pallas_call | solution.py:51
  29.7 1.5 %copy.23 = f32[16,128,32]{1,2,0:T(8,128)S(1)} copy(f32[16,128,32]{2,1,0:T(8,128)} %shard_map.46) | data formatting | bytes 524288 | tf_op jit(solution)/shard_map/pallas_call | solution.py:51
  31.3 4.0 %collective-permute-start.2 = (f32[128,4,2,16]{0,1,2,3:T(4,128)S(1)}, f32[128,4,2,16]{0,1,2,3:T(4,128)S(1)}, u32[]{:S(2)}, u32[]{:S(2)}) collective-permute-start(f32[128,4,2,16]{0,1,2,3:T(4,128)S(1)} %get-tuple-element.10), channel_id=1, source_target_pairs={{0,24},{8,0},{16,8},{24,16},{1,25},{9,1},{17,9},{25,17},{2,26},{10... | collective-permute-start | bytes 196616 | tf_op jit(solution)/shard_map/ppermute | solution.py:141
  36.5 2.3 %select_reduce_fusion.inv_ref = s32[2048]{0:T(1024)} fusion(s32[2048]{0:T(1024)S(1)} %copy-done.1), kind=kLoop, calls=%fused_computation.2 | loop fusion | flops 12580864 | bytes 16384 | tf_op jit(solution)/shard_map/reduce_sum | solution.py:79
  38.9 1.1 collective-permute-done.1
  40.0 1.0 collective-permute-done
  41.9 3.5 %collective-permute-start.3 = (f32[512,128]{0,1:T(8,128)S(1)}, f32[512,128]{0,1:T(8,128)S(1)}, u32[]{:S(2)}, u32[]{:S(2)}) collective-permute-start(f32[512,128]{0,1:T(8,128)S(1)} %bitcast_select_fusion.1), channel_id=1, source_target_pairs={{0,2},{1,3},{2,4},{3,5},{4,6},{5,7},{8,10},{9,11},{10,12},{11,13},... | collective-permute-start | bytes 786440 | tf_op jit(solution)/shard_map/ppermute | solution.py:160
  45.6 1.3 %collective-permute-start.6 = (f32[512,128]{0,1:T(8,128)S(1)}, f32[512,128]{0,1:T(8,128)S(1)}, u32[]{:S(2)}, u32[]{:S(2)}) collective-permute-start(f32[512,128]{0,1:T(8,128)S(1)} %bitcast_select_fusion.1), channel_id=1, source_target_pairs={{2,0},{3,1},{4,2},{5,3},{6,4},{7,5},{10,8},{11,9},{12,10},{13,11},... | collective-permute-start | bytes 786440 | tf_op jit(solution)/shard_map/ppermute | solution.py:161
  47.0 2.3 %collective-permute-done.3 = f32[512,128]{0,1:T(8,128)S(1)} collective-permute-done((f32[512,128]{0,1:T(8,128)S(1)}, f32[512,128]{0,1:T(8,128)S(1)}, u32[]{:S(2)}, u32[]{:S(2)}) %collective-permute-start.3) | collective-permute-done | bytes 262176 | tf_op jit(solution)/shard_map/ppermute | solution.py:160
  49.3 4.4 %collective-permute-start.4 = (f32[512,128]{0,1:T(8,128)S(1)}, f32[512,128]{0,1:T(8,128)S(1)}, u32[]{:S(2)}, u32[]{:S(2)}) collective-permute-start(f32[512,128]{0,1:T(8,128)S(1)} %collective-permute-done.3), channel_id=1, source_target_pairs={{0,2},{1,3},{2,4},{3,5},{4,6},{5,7},{8,10},{9,11},{10,12},{11,13},... | collective-permute-start | bytes 786440 | tf_op jit(solution)/shard_map/ppermute | solution.py:160
  53.7 0.7 select_dynamic-update-slice_fusion
  54.4 1.3 %collective-permute-start.7 = (f32[512,128]{0,1:T(8,128)S(1)}, f32[512,128]{0,1:T(8,128)S(1)}, u32[]{:S(2)}, u32[]{:S(2)}) collective-permute-start(f32[512,128]{0,1:T(8,128)S(1)} %collective-permute-done.6), channel_id=1, source_target_pairs={{2,0},{3,1},{4,2},{5,3},{6,4},{7,5},{10,8},{11,9},{12,10},{13,11},... | collective-permute-start | bytes 786440 | tf_op jit(solution)/shard_map/ppermute | solution.py:161
  55.8 1.8 %collective-permute-done.4 = f32[512,128]{0,1:T(8,128)S(1)} collective-permute-done((f32[512,128]{0,1:T(8,128)S(1)}, f32[512,128]{0,1:T(8,128)S(1)}, u32[]{:S(2)}, u32[]{:S(2)}) %collective-permute-start.4) | collective-permute-done | bytes 262176 | tf_op jit(solution)/shard_map/ppermute | solution.py:160
  57.6 4.4 %collective-permute-start.5 = (f32[512,128]{0,1:T(8,128)S(1)}, f32[512,128]{0,1:T(8,128)S(1)}, u32[]{:S(2)}, u32[]{:S(2)}) collective-permute-start(f32[512,128]{0,1:T(8,128)S(1)} %collective-permute-done.4), channel_id=1, source_target_pairs={{0,2},{1,3},{2,4},{3,5},{4,6},{5,7},{8,10},{9,11},{10,12},{11,13},... | collective-permute-start | bytes 786440 | tf_op jit(solution)/shard_map/ppermute | solution.py:160
  62.0 0.7 bitcast_dynamic-update-slice_fusion.5
  62.7 1.5 %collective-permute-start.8 = (f32[512,128]{0,1:T(8,128)S(1)}, f32[512,128]{0,1:T(8,128)S(1)}, u32[]{:S(2)}, u32[]{:S(2)}) collective-permute-start(f32[512,128]{0,1:T(8,128)S(1)} %collective-permute-done.7), channel_id=1, source_target_pairs={{2,0},{3,1},{4,2},{5,3},{6,4},{7,5},{10,8},{11,9},{12,10},{13,11},... | collective-permute-start | bytes 786440 | tf_op jit(solution)/shard_map/ppermute | solution.py:161
  64.2 0.7 bitcast_dynamic-update-slice_fusion.4
  64.9 0.9 collective-permute-done.5
  68.0 3.0 %collective-permute-done.8 = f32[512,128]{0,1:T(8,128)S(1)} collective-permute-done((f32[512,128]{0,1:T(8,128)S(1)}, f32[512,128]{0,1:T(8,128)S(1)}, u32[]{:S(2)}, u32[]{:S(2)}) %collective-permute-start.8) | collective-permute-done | bytes 262176 | tf_op jit(solution)/shard_map/ppermute | solution.py:161
  70.9 0.7 bitcast_dynamic-update-slice_fusion
  71.7 2.1 %gather_fusion.1 = f32[4,512,128]{1,2,0:T(8,128)S(1)} fusion(f32[7,512,128]{1,2,0:T(8,128)} %bitcast_dynamic-update-slice_fusion, s32[1024]{0:T(1024)S(1)} %pad_clamp_fusion), kind=kCustom, calls=%fused_computation.1 | custom fusion | bytes 2097168 | tf_op jit(solution)/shard_map/jit(_take)/gather | solution.py:167
  73.8 1.2 %broadcast_select_fusion = f32[4,512,128]{1,2,0:T(8,128)} fusion(f32[4,512,128]{1,2,0:T(8,128)S(1)} %gather_fusion.1, pred[4]{0:T(512)(128)(4,1)S(1)} %compare_and_fusion), kind=kLoop, calls=%fused_computation.19 | loop fusion | flops 262144 | bytes 2097156 | tf_op jit(solution)/shard_map/jit(_take)/select_n | solution.py:167
  75.1 0.9 pad_maximum_fusion.1
  76.0 2.6 %copy.26 = f32[4,512,2,32]{3,2,1,0:T(2,128)S(1)} copy(f32[4,512,2,32]{1,3,0,2:T(8,128)} %pad_maximum_fusion.1) | data formatting | bytes 1048576 | tf_op jit(solution)/shard_map/stack | solution.py:193
  78.9 1.0 pad_maximum_fusion.l_ref
  80.0 2.0 %maximum_select_fusion = f32[4,2,512,128]{2,3,0,1:T(8,128)S(1)} fusion(f32[4,1,512,128]{2,3,0,1:T(8,128)} %bitcast.26, f32[4,1,512,128]{2,3,0,1:T(8,128)S(1)} %bitcast_select_fusion, pred[]{:T(512)S(6)} %eq.48), kind=kLoop, calls=%fused_computation.6 | loop fusion | flops 1572864 | bytes 4194305 | tf_op jit(solution)/shard_map/jit(_where)/select_n | solution.py:169
  82.0 1.8 %copy.29 = f32[4,2,512,128]{3,2,1,0:T(8,128)} copy(f32[4,2,512,128]{2,3,0,1:T(8,128)S(1)} %maximum_select_fusion) | data formatting | bytes 4194304 | tf_op jit(solution)/shard_map/jit(_where)/select_n | solution.py:169
  83.8 7.2 %shard_map.47 = f32[4096,128]{1,0:T(8,128)} custom-call(s32[2048]{0:T(1024)} %select_reduce_fusion.inv_ref, f32[4096,128]{1,0:T(8,128)} %bitcast.71), custom_call_target="tpu_custom_call" | custom-call | tf_op jit(solution)/shard_map/pallas_call | solution.py:95
  91.0 1.9 %copy.30 = f32[4096,128]{0,1:T(8,128)S(1)} copy(f32[4096,128]{1,0:T(8,128)} %shard_map.47) | data formatting | bytes 4194304 | tf_op jit(solution)/shard_map/pallas_call | solution.py:95
  93.7 14.8 %shard_map.48 = bf16[4,512,2,4096]{3,2,1,0:T(2,128)(2,1)} custom-call(bf16[4,1024,96]{2,1,0:T(8,128)(2,1)S(1)} %pad_maximum_fusion.l_ref, bf16[4,96,4096]{2,1,0:T(8,128)(2,1)S(1)} %maximum_bitcast_fusion.o_ref), custom_call_target="tpu_custom_call" | custom-call | tf_op jit(solution)/shard_map/pallas_call | solution.py:122
  (38 shorter events, 6.0 us)
Async XLA Ops:
  0.0 3.3 %copy-start = (f32[8,8192]{1,0:T(8,128)S(1)}, f32[8,8192]{1,0:T(8,128)}, u32[]{:S(2)}) copy-start(f32[8,8192]{1,0:T(8,128)} %param.5) | copy-start | bytes 786436
  5.9 30.6 %copy-start.1 = (s32[2048]{0:T(1024)S(1)}, s32[2048]{0:T(1024)}, u32[]{:S(2)}) copy-start(s32[2048]{0:T(1024)} %param.7) | copy-start | bytes 24580
  31.3 7.6 %collective-permute-start.2 = (f32[128,4,2,16]{0,1,2,3:T(4,128)S(1)}, f32[128,4,2,16]{0,1,2,3:T(4,128)S(1)}, u32[]{:S(2)}, u32[]{:S(2)}) collective-permute-start(f32[128,4,2,16]{0,1,2,3:T(4,128)S(1)} %get-tuple-element.10), channel_id=1, source_target_pairs={{0,24},{8,0},{16,8},{24,16},{1,25},{9,1},{17,9},{25,17},{2,26},{10... | collective-permute-start | bytes 196616 | tf_op jit(solution)/shard_map/ppermute | solution.py:141
  35.3 4.7 %collective-permute-start.1 = (f32[128,4,2,16]{0,1,2,3:T(4,128)S(1)}, f32[128,4,2,16]{0,1,2,3:T(4,128)S(1)}, u32[]{:S(2)}, u32[]{:S(2)}) collective-permute-start(f32[128,4,2,16]{0,1,2,3:T(4,128)S(1)} %get-tuple-element.11), channel_id=1, source_target_pairs={{0,16},{8,24},{16,0},{24,8},{1,17},{9,25},{17,1},{25,9},{2,18},{10... | collective-permute-start | bytes 196616 | tf_op jit(solution)/shard_map/ppermute | solution.py:141
  35.8 5.2 %collective-permute-start = (f32[128,4,2,16]{0,1,2,3:T(4,128)S(1)}, f32[128,4,2,16]{0,1,2,3:T(4,128)S(1)}, u32[]{:S(2)}, u32[]{:S(2)}) collective-permute-start(f32[128,4,2,16]{0,1,2,3:T(4,128)S(1)} %get-tuple-element.12), channel_id=1, source_target_pairs={{0,8},{8,16},{16,24},{24,0},{1,9},{9,17},{17,25},{25,1},{2,10},{10... | collective-permute-start | bytes 196616 | tf_op jit(solution)/shard_map/ppermute | solution.py:141
  41.9 7.4 %collective-permute-start.3 = (f32[512,128]{0,1:T(8,128)S(1)}, f32[512,128]{0,1:T(8,128)S(1)}, u32[]{:S(2)}, u32[]{:S(2)}) collective-permute-start(f32[512,128]{0,1:T(8,128)S(1)} %bitcast_select_fusion.1), channel_id=1, source_target_pairs={{0,2},{1,3},{2,4},{3,5},{4,6},{5,7},{8,10},{9,11},{10,12},{11,13},... | collective-permute-start | bytes 786440 | tf_op jit(solution)/shard_map/ppermute | solution.py:160
  45.6 8.9 %collective-permute-start.6 = (f32[512,128]{0,1:T(8,128)S(1)}, f32[512,128]{0,1:T(8,128)S(1)}, u32[]{:S(2)}, u32[]{:S(2)}) collective-permute-start(f32[512,128]{0,1:T(8,128)S(1)} %bitcast_select_fusion.1), channel_id=1, source_target_pairs={{2,0},{3,1},{4,2},{5,3},{6,4},{7,5},{10,8},{11,9},{12,10},{13,11},... | collective-permute-start | bytes 786440 | tf_op jit(solution)/shard_map/ppermute | solution.py:161
  49.3 8.3 %collective-permute-start.4 = (f32[512,128]{0,1:T(8,128)S(1)}, f32[512,128]{0,1:T(8,128)S(1)}, u32[]{:S(2)}, u32[]{:S(2)}) collective-permute-start(f32[512,128]{0,1:T(8,128)S(1)} %collective-permute-done.3), channel_id=1, source_target_pairs={{0,2},{1,3},{2,4},{3,5},{4,6},{5,7},{8,10},{9,11},{10,12},{11,13},... | collective-permute-start | bytes 786440 | tf_op jit(solution)/shard_map/ppermute | solution.py:160
  54.4 8.3 %collective-permute-start.7 = (f32[512,128]{0,1:T(8,128)S(1)}, f32[512,128]{0,1:T(8,128)S(1)}, u32[]{:S(2)}, u32[]{:S(2)}) collective-permute-start(f32[512,128]{0,1:T(8,128)S(1)} %collective-permute-done.6), channel_id=1, source_target_pairs={{2,0},{3,1},{4,2},{5,3},{6,4},{7,5},{10,8},{11,9},{12,10},{13,11},... | collective-permute-start | bytes 786440 | tf_op jit(solution)/shard_map/ppermute | solution.py:161
  57.6 8.3 %collective-permute-start.5 = (f32[512,128]{0,1:T(8,128)S(1)}, f32[512,128]{0,1:T(8,128)S(1)}, u32[]{:S(2)}, u32[]{:S(2)}) collective-permute-start(f32[512,128]{0,1:T(8,128)S(1)} %collective-permute-done.4), channel_id=1, source_target_pairs={{0,2},{1,3},{2,4},{3,5},{4,6},{5,7},{8,10},{9,11},{10,12},{11,13},... | collective-permute-start | bytes 786440 | tf_op jit(solution)/shard_map/ppermute | solution.py:160
  62.7 8.3 %collective-permute-start.8 = (f32[512,128]{0,1:T(8,128)S(1)}, f32[512,128]{0,1:T(8,128)S(1)}, u32[]{:S(2)}, u32[]{:S(2)}) collective-permute-start(f32[512,128]{0,1:T(8,128)S(1)} %collective-permute-done.7), channel_id=1, source_target_pairs={{2,0},{3,1},{4,2},{5,3},{6,4},{7,5},{10,8},{11,9},{12,10},{13,11},... | collective-permute-start | bytes 786440 | tf_op jit(solution)/shard_map/ppermute | solution.py:161
  75.0 5.0 %collective-permute-start.9 = (f32[4,512,128]{1,2,0:T(8,128)}, f32[4,512,128]{1,2,0:T(8,128)}, u32[]{:S(2)}, u32[]{:S(2)}) collective-permute-start(f32[4,512,128]{1,2,0:T(8,128)} %broadcast_select_fusion), channel_id=1, source_target_pairs={{0,1},{1,0},{2,3},{3,2},{4,5},{5,4},{6,7},{7,6},{8,9},{9,8},{10,11... | collective-permute-start | bytes 3145736 | tf_op jit(solution)/shard_map/ppermute | solution.py:168

commit v9 on v8

--- a/solution.py
+++ b/solution.py
@@ -81,7 +81,40 @@
     )
 
 
-def _perm_kernel(inv_ref, e_ref, o_ref):
+def _perm_kernel(inv_ref, mine_hbm, other_hbm, o_ref, e_ref, sem):
+    pieces, block, _ = mine_hbm.shape
+    line = (pieces + 1) // 2
+    me = lax.axis_index("blk")
+    pos, core = me // 2, me % 2
+
+    def place(j):
+        if j == 0:
+            return pos
+        if j < line:
+            return pos - j
+        return pos + (j - line + 1)
+
+    copies = []
+    for j in range(pieces):
+        z = place(j)
+        ok = jnp.logical_and(z >= 0, z < line)
+        zc = jnp.clip(z, 0, line - 1)
+        for k, (src, c) in enumerate(((mine_hbm, core), (other_hbm, 1 - core))):
+            copy = pltpu.make_async_copy(
+                src.at[j], e_ref.at[pl.ds((zc * 2 + c) * block, block)], sem.at[j, k]
+            )
+            copies.append((ok, copy))
+
+            @pl.when(ok)
+            def _():
+                copy.start()
+
+    for ok, copy in copies:
+
+        @pl.when(ok)
+        def _():
+            copy.wait()
+
     def body(a, carry):
         src = inv_ref[a] * 2
         o_ref[pl.ds(2 * a, 2), :] = e_ref[pl.ds(src, 2), :]
@@ -90,18 +123,23 @@
     lax.fori_loop(0, inv_ref.shape[0], body, 0, unroll=8)
 
 
-def permute_pairs(everything, inverse):
-    rows, width = everything.shape
+def permute_pairs(mine, other, inverse):
+    pieces, block, width = mine.shape
+    rows = (pieces + 1) * block
     return pl.pallas_call(
         _perm_kernel,
         grid_spec=pltpu.PrefetchScalarGridSpec(
             num_scalar_prefetch=1,
             grid=(1,),
-            in_specs=[pl.BlockSpec((rows, width), lambda i, inv: (0, 0))],
+            in_specs=[pl.BlockSpec(memory_space=pl.ANY), pl.BlockSpec(memory_space=pl.ANY)],
             out_specs=pl.BlockSpec((rows, width), lambda i, inv: (0, 0)),
+            scratch_shapes=[
+                pltpu.VMEM((rows, width), mine.dtype),
+                pltpu.SemaphoreType.DMA((pieces, 2)),
+            ],
         ),
-        out_shape=jax.ShapeDtypeStruct((rows, width), everything.dtype),
-    )(inverse, everything)
+        out_shape=jax.ShapeDtypeStruct((rows, width), mine.dtype),
+    )(inverse, mine, other)
 
 
 def split2(x):
@@ -162,12 +200,8 @@
         got_r.append(r)
         got_l.append(l)
     cands = jnp.stack([x] + got_r + got_l, axis=0)
-    zs = jnp.arange(line, dtype=jnp.int32)
-    idx = jnp.where(zs == pos, 0, jnp.where(zs < pos, pos - zs, line - 1 + zs - pos))
-    mine = jnp.take(cands, idx, axis=0)
-    other = lax.ppermute(mine, "blk", [(b, b ^ 1) for b in range(count)])
-    pair = jnp.where(core == 0, jnp.stack([mine, other], 1), jnp.stack([other, mine], 1))
-    return pair.reshape((count * x.shape[0],) + x.shape[1:])
+    other = lax.ppermute(cands, "blk", [(b, b ^ 1) for b in range(count)])
+    return cands, other
 
 
 def per_device(voltages, filter_taps, channel_index, antenna_slot_order):
@@ -180,9 +214,9 @@
     x = exchange_channels(x, grp, local_ch)
     slots_local = x.shape[0]
     x = x.reshape(slots_local, local_ch * 2 * spectra)
-    everything = gather_blocks(x)
+    cands, other = gather_blocks(x)
     inverse = slot_index(antenna_slot_order)
-    ordered = permute_pairs(everything, inverse)
+    ordered = permute_pairs(cands, other, inverse)
     ordered = ordered.reshape(-1, local_ch, 2 * spectra).transpose(1, 0, 2)
     scale = jnp.float32(1.0 / spectra)
     xl = x.reshape(slots_local, local_ch, 2, spectra).transpose(1, 0, 2, 3) * scale

time: 109 us -> 102 us (0.936)
  local copies, waits for them, and re-layouts: 15.5 us -> 10.2 us
  other arithmetic: 15.4 us -> 11.4 us
  waiting for transfers between devices: 10.1 us -> 12 us
    select_n x4 -> x0, other arithmetic: 3.37 us -> none  [the longest x1 1.97 us: gather_blocks(): jnp.where(core == 0, jnp.stack([mine, other], 1), jnp.stack([other, mine]...]
    gather x1 -> x0, local copies, waits for them, and re-layouts: 2.11 us -> none  [gather_blocks(): mine = jnp.take(cands, idx, axis=0)]
    select_n x1 -> x0, local copies, waits for them, and re-layouts: 1.81 us -> none  [gather_blocks(): jnp.where(core == 0, jnp.stack([mine, other], 1), jnp.stack([other, mine]...]
    ppermute x3, waiting for transfers between devices: 2.07 us -> 3.85 us  [exchange_channels(): part = lax.ppermute(part, 'grp', [(j, (j + d) % grp) for j in range(grp)])]
    another operation x1, local copies, waits for them, and re-layouts: 2.57 us -> 1.04 us  [per_device(): lhs = jnp.stack([row0, row1], axis=2)]
    unnamed x9 -> x14, local copies, waits for them, and re-layouts: 3.62 us -> 3.71 us
  transfers between devices with their start and end apart: 10 -> 10, of which waited for: 6 -> 6; matrix products, arithmetic and copies ran while one was open for 11% -> 10% of each run, Pallas kernels for 0% -> 0%
where the time goes in v9:
time: 102 us; the launch traced here: 101 us
  Pallas kernels  45.8 us (45%)
  starting transfers between devices  21.5 us (21%)
  waiting for transfers between devices  12 us (12%)
  other arithmetic  11.4 us (11%)
  local copies, waits for them, and re-layouts  10.2 us (10%)
    pallas_call x1, Pallas kernels, frame_products(): pl.pallas_call(_frame_kernel, grid=(steps,), in_specs=[pl.BlockSpec((rows...  23.7 us
    pallas_call x1, Pallas kernels, correlate(): pl.pallas_call(_corr_kernel, grid=(chans, slots // block_rows), in_specs=...  14.8 us
    ppermute x3, starting transfers between devices, gather_blocks(): r = lax.ppermute(r, 'blk', right)  12.3 us
    pallas_call x1, Pallas kernels, permute_pairs(): pl.pallas_call(_perm_kernel, grid_spec=pltpu.PrefetchScalarGridSpec(num_s...  7.24 us
    ppermute x3, starting transfers between devices, exchange_channels(): part = lax.ppermute(part, 'grp', [(j, (j + d) % grp) for j in range(grp)])  5.18 us
    ppermute x3, waiting for transfers between devices, gather_blocks(): r = lax.ppermute(r, 'blk', right)  5.17 us
    ppermute x3, starting transfers between devices, gather_blocks(): l = lax.ppermute(l, 'blk', left)  4.05 us
    ppermute x3, waiting for transfers between devices, exchange_channels(): part = lax.ppermute(part, 'grp', [(j, (j + d) % grp) for j in range(grp)])  3.85 us
  transfers between devices with their start and end apart: 10, of which 6 were waited for; matrix products, arithmetic and copies ran while one was open for 10% of the time, Pallas kernels for 0%

profile of v9, /device:TPU:0, one launch (start us, length us, event | category | flops | bytes accessed | tf_op | source)
XLA Modules:
  0.0 101.2 jit_solution(7983473436353148536)
XLA Ops:
  0.0 3.2 %cosine_convert_fusion = (bf16[16,8192]{1,0:T(8,128)(2,1)S(1)}, bf16[16,8192]{1,0:T(8,128)(2,1)S(1)}) fusion(s32[16]{0:T(128)} %param.6), kind=kLoop, calls=%fused_computation.17 | loop fusion | flops 2228224 | bytes 524352 | tf_op jit(solution)/shard_map/convert
  3.3 2.7 %multiply_convert_fusion = bf16[8,32,8192]{2,1,0:T(8,128)(2,1)} fusion(f32[32,8192]{1,0:T(8,128)S(1)} %maximum_convert_fusion, f32[8,8192]{1,0:T(8,128)S(1)} %copy-done), kind=kLoop, calls=%fused_computation.3 | loop fusion | flops 4194304 | bytes 5505024 | tf_op jit(solution)/shard_map/convert_element_type | solution.py:71
  5.9 23.7 %shard_map.46 = f32[16,128,32]{2,1,0:T(8,128)} custom-call(bf16[128,188416]{1,0:T(8,128)(2,1)} %v_ref.1, bf16[256,8192]{1,0:T(8,128)(2,1)} %bitcast.75), custom_call_target="tpu_custom_call" | custom-call | tf_op jit(solution)/shard_map/pallas_call | solution.py:51
  29.7 1.5 %copy.32 = f32[16,128,32]{1,2,0:T(8,128)S(1)} copy(f32[16,128,32]{2,1,0:T(8,128)} %shard_map.46) | data formatting | bytes 524288 | tf_op jit(solution)/shard_map/pallas_call | solution.py:51
  31.3 4.0 %collective-permute-start.2 = (f32[128,4,2,16]{0,3,2,1:T(8,128)S(1)}, f32[128,4,2,16]{0,3,2,1:T(8,128)S(1)}, u32[]{:S(2)}, u32[]{:S(2)}) collective-permute-start(f32[128,4,2,16]{0,3,2,1:T(8,128)S(1)} %bitcast.81), channel_id=1, source_target_pairs={{0,24},{8,0},{16,8},{24,16},{1,25},{9,1},{17,9},{25,17},{2,26},{10... | collective-permute-start | bytes 196616 | tf_op jit(solution)/shard_map/ppermute | solution.py:179
  35.4 1.1 %collective-permute-start.1 = (f32[128,4,2,16]{0,3,2,1:T(8,128)S(1)}, f32[128,4,2,16]{0,3,2,1:T(8,128)S(1)}, u32[]{:S(2)}, u32[]{:S(2)}) collective-permute-start(f32[128,4,2,16]{0,3,2,1:T(8,128)S(1)} %bitcast.83), channel_id=1, source_target_pairs={{0,16},{8,24},{16,0},{24,8},{1,17},{9,25},{17,1},{25,9},{2,18},{10... | collective-permute-start | bytes 196616 | tf_op jit(solution)/shard_map/ppermute | solution.py:179
  36.7 0.7 collective-permute-done.2
  37.3 3.2 %collective-permute-done = f32[128,4,2,16]{0,3,2,1:T(8,128)S(1)} collective-permute-done((f32[128,4,2,16]{0,3,2,1:T(8,128)S(1)}, f32[128,4,2,16]{0,3,2,1:T(8,128)S(1)}, u32[]{:S(2)}, u32[]{:S(2)}) %collective-permute-start) | collective-permute-done | bytes 65568 | tf_op jit(solution)/shard_map/ppermute | solution.py:179
  40.6 0.6 gather_fusion
  41.6 3.5 %collective-permute-start.3 = (f32[512,128]{1,0:T(8,128)S(1)}, f32[512,128]{1,0:T(8,128)S(1)}, u32[]{:S(2)}, u32[]{:S(2)}) collective-permute-start(f32[512,128]{1,0:T(8,128)S(1)} %broadcast_select_fusion), channel_id=1, source_target_pairs={{0,2},{1,3},{2,4},{3,5},{4,6},{5,7},{8,10},{9,11},{10,12},{11,13},... | collective-permute-start | bytes 786440 | tf_op jit(solution)/shard_map/ppermute | solution.py:198
  45.1 1.3 %collective-permute-start.6 = (f32[512,128]{1,0:T(8,128)S(1)}, f32[512,128]{1,0:T(8,128)S(1)}, u32[]{:S(2)}, u32[]{:S(2)}) collective-permute-start(f32[512,128]{1,0:T(8,128)S(1)} %broadcast_select_fusion), channel_id=1, source_target_pairs={{2,0},{3,1},{4,2},{5,3},{6,4},{7,5},{10,8},{11,9},{12,10},{13,11},... | collective-permute-start | bytes 786440 | tf_op jit(solution)/shard_map/ppermute | solution.py:199
  46.4 2.8 %collective-permute-done.3 = f32[512,128]{1,0:T(8,128)S(1)} collective-permute-done((f32[512,128]{1,0:T(8,128)S(1)}, f32[512,128]{1,0:T(8,128)S(1)}, u32[]{:S(2)}, u32[]{:S(2)}) %collective-permute-start.3) | collective-permute-done | bytes 262176 | tf_op jit(solution)/shard_map/ppermute | solution.py:198
  49.2 4.4 %collective-permute-start.4 = (f32[512,128]{1,0:T(8,128)S(1)}, f32[512,128]{1,0:T(8,128)S(1)}, u32[]{:S(2)}, u32[]{:S(2)}) collective-permute-start(f32[512,128]{1,0:T(8,128)S(1)} %collective-permute-done.3), channel_id=1, source_target_pairs={{0,2},{1,3},{2,4},{3,5},{4,6},{5,7},{8,10},{9,11},{10,12},{11,13},... | collective-permute-start | bytes 786440 | tf_op jit(solution)/shard_map/ppermute | solution.py:198
  53.9 1.3 %collective-permute-start.7 = (f32[512,128]{1,0:T(8,128)S(1)}, f32[512,128]{1,0:T(8,128)S(1)}, u32[]{:S(2)}, u32[]{:S(2)}) collective-permute-start(f32[512,128]{1,0:T(8,128)S(1)} %collective-permute-done.6), channel_id=1, source_target_pairs={{2,0},{3,1},{4,2},{5,3},{6,4},{7,5},{10,8},{11,9},{12,10},{13,11},... | collective-permute-start | bytes 786440 | tf_op jit(solution)/shard_map/ppermute | solution.py:199
  55.2 0.9 select_dynamic-update-slice_fusion
  56.0 1.4 %collective-permute-done.4 = f32[512,128]{1,0:T(8,128)S(1)} collective-permute-done((f32[512,128]{1,0:T(8,128)S(1)}, f32[512,128]{1,0:T(8,128)S(1)}, u32[]{:S(2)}, u32[]{:S(2)}) %collective-permute-start.4) | collective-permute-done | bytes 262176 | tf_op jit(solution)/shard_map/ppermute | solution.py:198
  57.5 4.4 %collective-permute-start.5 = (f32[512,128]{1,0:T(8,128)S(1)}, f32[512,128]{1,0:T(8,128)S(1)}, u32[]{:S(2)}, u32[]{:S(2)}) collective-permute-start(f32[512,128]{1,0:T(8,128)S(1)} %collective-permute-done.4), channel_id=1, source_target_pairs={{0,2},{1,3},{2,4},{3,5},{4,6},{5,7},{8,10},{9,11},{10,12},{11,13},... | collective-permute-start | bytes 786440 | tf_op jit(solution)/shard_map/ppermute | solution.py:198
  61.9 0.7 bitcast_dynamic-update-slice_fusion.5
  62.6 1.5 %collective-permute-start.8 = (f32[512,128]{1,0:T(8,128)S(1)}, f32[512,128]{1,0:T(8,128)S(1)}, u32[]{:S(2)}, u32[]{:S(2)}) collective-permute-start(f32[512,128]{1,0:T(8,128)S(1)} %collective-permute-done.7), channel_id=1, source_target_pairs={{2,0},{3,1},{4,2},{5,3},{6,4},{7,5},{10,8},{11,9},{12,10},{13,11},... | collective-permute-start | bytes 786440 | tf_op jit(solution)/shard_map/ppermute | solution.py:199
  64.1 0.7 bitcast_dynamic-update-slice_fusion.4
  64.8 0.9 collective-permute-done.5
  65.7 0.7 bitcast_dynamic-update-slice_fusion.3
  66.5 0.7 bitcast_dynamic-update-slice_fusion.2
  67.2 0.7 bitcast_dynamic-update-slice_fusion.1
  67.9 3.0 %collective-permute-done.8 = f32[512,128]{1,0:T(8,128)S(1)} collective-permute-done((f32[512,128]{1,0:T(8,128)S(1)}, f32[512,128]{1,0:T(8,128)S(1)}, u32[]{:S(2)}, u32[]{:S(2)}) %collective-permute-start.8) | collective-permute-done | bytes 262176 | tf_op jit(solution)/shard_map/ppermute | solution.py:199
  70.9 0.7 bitcast_dynamic-update-slice_fusion.mine_hbm
  71.6 2.3 %select_reduce_fusion.inv_ref = s32[2048]{0:T(1024)} fusion(s32[2048]{0:T(1024)S(1)} %copy-done.1), kind=kLoop, calls=%fused_computation.1 | loop fusion | flops 12580864 | bytes 16384 | tf_op jit(solution)/shard_map/reduce_sum | solution.py:79
  74.1 1.0 %copy.39 = f32[4,512,2,32]{3,2,1,0:T(2,128)S(1)} copy(f32[4,512,2,32]{1,3,0,2:T(8,128)S(1)} %pad_maximum_fusion.1) | data formatting | bytes 1048576 | tf_op jit(solution)/shard_map/stack | solution.py:227
  75.5 1.0 pad_maximum_fusion.l_ref
  76.5 7.2 %shard_map.47 = f32[4096,128]{1,0:T(8,128)} custom-call(s32[2048]{0:T(1024)} %select_reduce_fusion.inv_ref, f32[7,512,128]{2,1,0:T(8,128)} %bitcast_dynamic-update-slice_fusion.mine_hbm, f32[7,512,128]{2,1,0:T(8,128)} %collective-permute-done.9.other_hbm), custom_call_target="tpu_custom_call" | custom-call | tf_op jit(solution)/shard_map/pallas_call | solution.py:129
  83.7 1.9 %copy.44 = f32[4096,128]{0,1:T(8,128)S(1)} copy(f32[4096,128]{1,0:T(8,128)} %shard_map.47) | data formatting | bytes 4194304 | tf_op jit(solution)/shard_map/pallas_call | solution.py:129
  86.4 14.8 %shard_map.48 = bf16[4,512,2,4096]{3,2,1,0:T(2,128)(2,1)} custom-call(bf16[4,1024,96]{2,1,0:T(8,128)(2,1)S(1)} %pad_maximum_fusion.l_ref, bf16[4,96,4096]{2,1,0:T(8,128)(2,1)S(1)} %maximum_bitcast_fusion.o_ref), custom_call_target="tpu_custom_call" | custom-call | tf_op jit(solution)/shard_map/pallas_call | solution.py:160
  (36 shorter events, 2.2 us)
Async XLA Ops:
  0.0 3.3 %copy-start = (f32[8,8192]{1,0:T(8,128)S(1)}, f32[8,8192]{1,0:T(8,128)}, u32[]{:S(2)}) copy-start(f32[8,8192]{1,0:T(8,128)} %param.5) | copy-start | bytes 786436
  31.3 6.0 %collective-permute-start.2 = (f32[128,4,2,16]{0,3,2,1:T(8,128)S(1)}, f32[128,4,2,16]{0,3,2,1:T(8,128)S(1)}, u32[]{:S(2)}, u32[]{:S(2)}) collective-permute-start(f32[128,4,2,16]{0,3,2,1:T(8,128)S(1)} %bitcast.81), channel_id=1, source_target_pairs={{0,24},{8,0},{16,8},{24,16},{1,25},{9,1},{17,9},{25,17},{2,26},{10... | collective-permute-start | bytes 196616 | tf_op jit(solution)/shard_map/ppermute | solution.py:179
  35.3 5.2 %collective-permute-start = (f32[128,4,2,16]{0,3,2,1:T(8,128)S(1)}, f32[128,4,2,16]{0,3,2,1:T(8,128)S(1)}, u32[]{:S(2)}, u32[]{:S(2)}) collective-permute-start(f32[128,4,2,16]{0,3,2,1:T(8,128)S(1)} %bitcast.82), channel_id=1, source_target_pairs={{0,8},{8,16},{16,24},{24,0},{1,9},{9,17},{17,25},{25,1},{2,10},{10... | collective-permute-start | bytes 196616 | tf_op jit(solution)/shard_map/ppermute | solution.py:179
  35.4 5.1 %collective-permute-start.1 = (f32[128,4,2,16]{0,3,2,1:T(8,128)S(1)}, f32[128,4,2,16]{0,3,2,1:T(8,128)S(1)}, u32[]{:S(2)}, u32[]{:S(2)}) collective-permute-start(f32[128,4,2,16]{0,3,2,1:T(8,128)S(1)} %bitcast.83), channel_id=1, source_target_pairs={{0,16},{8,24},{16,0},{24,8},{1,17},{9,25},{17,1},{25,9},{2,18},{10... | collective-permute-start | bytes 196616 | tf_op jit(solution)/shard_map/ppermute | solution.py:179
  41.6 7.6 %collective-permute-start.3 = (f32[512,128]{1,0:T(8,128)S(1)}, f32[512,128]{1,0:T(8,128)S(1)}, u32[]{:S(2)}, u32[]{:S(2)}) collective-permute-start(f32[512,128]{1,0:T(8,128)S(1)} %broadcast_select_fusion), channel_id=1, source_target_pairs={{0,2},{1,3},{2,4},{3,5},{4,6},{5,7},{8,10},{9,11},{10,12},{11,13},... | collective-permute-start | bytes 786440 | tf_op jit(solution)/shard_map/ppermute | solution.py:198
  45.1 8.8 %collective-permute-start.6 = (f32[512,128]{1,0:T(8,128)S(1)}, f32[512,128]{1,0:T(8,128)S(1)}, u32[]{:S(2)}, u32[]{:S(2)}) collective-permute-start(f32[512,128]{1,0:T(8,128)S(1)} %broadcast_select_fusion), channel_id=1, source_target_pairs={{2,0},{3,1},{4,2},{5,3},{6,4},{7,5},{10,8},{11,9},{12,10},{13,11},... | collective-permute-start | bytes 786440 | tf_op jit(solution)/shard_map/ppermute | solution.py:199
  49.2 8.3 %collective-permute-start.4 = (f32[512,128]{1,0:T(8,128)S(1)}, f32[512,128]{1,0:T(8,128)S(1)}, u32[]{:S(2)}, u32[]{:S(2)}) collective-permute-start(f32[512,128]{1,0:T(8,128)S(1)} %collective-permute-done.3), channel_id=1, source_target_pairs={{0,2},{1,3},{2,4},{3,5},{4,6},{5,7},{8,10},{9,11},{10,12},{11,13},... | collective-permute-start | bytes 786440 | tf_op jit(solution)/shard_map/ppermute | solution.py:198
  53.7 17.9 %copy-start.1 = (s32[2048]{0:T(1024)S(1)}, s32[2048]{0:T(1024)}, u32[]{:S(2)}) copy-start(s32[2048]{0:T(1024)} %param.7) | copy-start | bytes 24580
  53.9 8.7 %collective-permute-start.7 = (f32[512,128]{1,0:T(8,128)S(1)}, f32[512,128]{1,0:T(8,128)S(1)}, u32[]{:S(2)}, u32[]{:S(2)}) collective-permute-start(f32[512,128]{1,0:T(8,128)S(1)} %collective-permute-done.6), channel_id=1, source_target_pairs={{2,0},{3,1},{4,2},{5,3},{6,4},{7,5},{10,8},{11,9},{12,10},{13,11},... | collective-permute-start | bytes 786440 | tf_op jit(solution)/shard_map/ppermute | solution.py:199
  57.5 8.3 %collective-permute-start.5 = (f32[512,128]{1,0:T(8,128)S(1)}, f32[512,128]{1,0:T(8,128)S(1)}, u32[]{:S(2)}, u32[]{:S(2)}) collective-permute-start(f32[512,128]{1,0:T(8,128)S(1)} %collective-permute-done.4), channel_id=1, source_target_pairs={{0,2},{1,3},{2,4},{3,5},{4,6},{5,7},{8,10},{9,11},{10,12},{11,13},... | collective-permute-start | bytes 786440 | tf_op jit(solution)/shard_map/ppermute | solution.py:198
  62.6 8.3 %collective-permute-start.8 = (f32[512,128]{1,0:T(8,128)S(1)}, f32[512,128]{1,0:T(8,128)S(1)}, u32[]{:S(2)}, u32[]{:S(2)}) collective-permute-start(f32[512,128]{1,0:T(8,128)S(1)} %collective-permute-done.7), channel_id=1, source_target_pairs={{2,0},{3,1},{4,2},{5,3},{6,4},{7,5},{10,8},{11,9},{12,10},{13,11},... | collective-permute-start | bytes 786440 | tf_op jit(solution)/shard_map/ppermute | solution.py:199
  71.6 4.9 %collective-permute-start.9 = (f32[7,512,128]{2,1,0:T(8,128)}, f32[7,512,128]{2,1,0:T(8,128)}, u32[]{:S(2)}, u32[]{:S(2)}) collective-permute-start(f32[7,512,128]{2,1,0:T(8,128)} %bitcast_dynamic-update-slice_fusion.mine_hbm), channel_id=1, source_target_pairs={{0,1},{1,0},{2,3},{3,2},{4,5},{5,4},{6,7},{7,6},{8,9},{9,8},{10,11... | collective-permute-start | bytes 5505032 | tf_op jit(solution)/shard_map/ppermute | solution.py:203

commit v10 on v9

--- a/solution.py
+++ b/solution.py
@@ -189,16 +189,12 @@
     line = count // 2
     me = lax.axis_index("blk")
     pos, core = me // 2, me % 2
-    right = [(z * 2 + c, (z + 1) * 2 + c) for z in range(line - 1) for c in range(2)]
-    left = [(z * 2 + c, (z - 1) * 2 + c) for z in range(1, line) for c in range(2)]
     got_r, got_l = [], []
-    r = x
-    l = x
-    for _ in range(1, line):
-        r = lax.ppermute(r, "blk", right)
-        l = lax.ppermute(l, "blk", left)
-        got_r.append(r)
-        got_l.append(l)
+    for s in range(1, line):
+        right = [(z * 2 + c, (z + s) * 2 + c) for z in range(line - s) for c in range(2)]
+        left = [(z * 2 + c, (z - s) * 2 + c) for z in range(s, line) for c in range(2)]
+        got_r.append(lax.ppermute(x, "blk", right))
+        got_l.append(lax.ppermute(x, "blk", left))
     cands = jnp.stack([x] + got_r + got_l, axis=0)
     other = lax.ppermute(cands, "blk", [(b, b ^ 1) for b in range(count)])
     return cands, other

time: 102 us -> 104 us (1.020)
  the two profiles are of different devices: /device:TPU:0 before, /device:TPU:27 now
where the time goes in v10:
time: 104 us; the launch traced here: 103 us
  Pallas kernels  45.8 us (44%)
  waiting for transfers between devices  20 us (19%)
  starting transfers between devices  15.6 us (15%)
  other arithmetic  11.4 us (11%)
  local copies, waits for them, and re-layouts  10.2 us (10%)
    pallas_call x1, Pallas kernels, frame_products(): pl.pallas_call(_frame_kernel, grid=(steps,), in_specs=[pl.BlockSpec((rows...  23.7 us
    ppermute x3, waiting for transfers between devices, gather_blocks(): got_r.append(lax.ppermute(x, 'blk', right))  17.5 us
    pallas_call x1, Pallas kernels, correlate(): pl.pallas_call(_corr_kernel, grid=(chans, slots // block_rows), in_specs=...  14.8 us
    ppermute x3, starting transfers between devices, gather_blocks(): got_l.append(lax.ppermute(x, 'blk', left))  7.28 us
    pallas_call x1, Pallas kernels, permute_pairs(): pl.pallas_call(_perm_kernel, grid_spec=pltpu.PrefetchScalarGridSpec(num_s...  7.24 us
    ppermute x3, starting transfers between devices, gather_blocks(): got_r.append(lax.ppermute(x, 'blk', right))  4.05 us
    ppermute x3, starting transfers between devices, exchange_channels(): part = lax.ppermute(part, 'grp', [(j, (j + d) % grp) for j in range(grp)])  3.77 us
    unnamed x14, local copies, waits for them, and re-layouts  3.71 us
  transfers between devices with their start and end apart: 10, of which 4 were waited for; matrix products, arithmetic and copies ran while one was open for 9% of the time, Pallas kernels for 0%

profile of v10, /device:TPU:27, one launch (start us, length us, event | category | flops | bytes accessed | tf_op | source)
XLA Modules:
  0.0 103.3 jit_solution(14762295414757371115)
XLA Ops:
  0.0 3.2 %cosine_convert_fusion = (bf16[16,8192]{1,0:T(8,128)(2,1)S(1)}, bf16[16,8192]{1,0:T(8,128)(2,1)S(1)}) fusion(s32[16]{0:T(128)} %param.6), kind=kLoop, calls=%fused_computation.17 | loop fusion | flops 2228224 | bytes 524352 | tf_op jit(solution)/shard_map/convert
  3.3 2.7 %multiply_convert_fusion = bf16[8,32,8192]{2,1,0:T(8,128)(2,1)} fusion(f32[32,8192]{1,0:T(8,128)S(1)} %maximum_convert_fusion, f32[8,8192]{1,0:T(8,128)S(1)} %copy-done), kind=kLoop, calls=%fused_computation.3 | loop fusion | flops 4194304 | bytes 5505024 | tf_op jit(solution)/shard_map/convert_element_type | solution.py:71
  5.9 23.7 %shard_map.46 = f32[16,128,32]{2,1,0:T(8,128)} custom-call(bf16[128,188416]{1,0:T(8,128)(2,1)} %v_ref.1, bf16[256,8192]{1,0:T(8,128)(2,1)} %bitcast.75), custom_call_target="tpu_custom_call" | custom-call | tf_op jit(solution)/shard_map/pallas_call | solution.py:51
  29.7 1.5 %copy.32 = f32[16,128,32]{1,2,0:T(8,128)S(1)} copy(f32[16,128,32]{2,1,0:T(8,128)} %shard_map.46) | data formatting | bytes 524288 | tf_op jit(solution)/shard_map/pallas_call | solution.py:51
  31.3 0.3 collective-permute-start.2
  31.6 2.2 %collective-permute-start = (f32[128,4,2,16]{0,3,2,1:T(8,128)S(1)}, f32[128,4,2,16]{0,3,2,1:T(8,128)S(1)}, u32[]{:S(2)}, u32[]{:S(2)}) collective-permute-start(f32[128,4,2,16]{0,3,2,1:T(8,128)S(1)} %bitcast.82), channel_id=1, source_target_pairs={{0,8},{8,16},{16,24},{24,0},{1,9},{9,17},{17,25},{25,1},{2,10},{10... | collective-permute-start | bytes 196616 | tf_op jit(solution)/shard_map/ppermute | solution.py:179
  33.8 1.3 %collective-permute-start.1 = (f32[128,4,2,16]{0,3,2,1:T(8,128)S(1)}, f32[128,4,2,16]{0,3,2,1:T(8,128)S(1)}, u32[]{:S(2)}, u32[]{:S(2)}) collective-permute-start(f32[128,4,2,16]{0,3,2,1:T(8,128)S(1)} %bitcast.83), channel_id=1, source_target_pairs={{0,16},{8,24},{16,0},{24,8},{1,17},{9,25},{17,1},{25,9},{2,18},{10... | collective-permute-start | bytes 196616 | tf_op jit(solution)/shard_map/ppermute | solution.py:179
  35.4 1.3 %collective-permute-done = f32[128,4,2,16]{0,3,2,1:T(8,128)S(1)} collective-permute-done((f32[128,4,2,16]{0,3,2,1:T(8,128)S(1)}, f32[128,4,2,16]{0,3,2,1:T(8,128)S(1)}, u32[]{:S(2)}, u32[]{:S(2)}) %collective-permute-start) | collective-permute-done | bytes 65568 | tf_op jit(solution)/shard_map/ppermute | solution.py:179
  36.7 1.1 %collective-permute-done.1 = f32[128,4,2,16]{0,3,2,1:T(8,128)S(1)} collective-permute-done((f32[128,4,2,16]{0,3,2,1:T(8,128)S(1)}, f32[128,4,2,16]{0,3,2,1:T(8,128)S(1)}, u32[]{:S(2)}, u32[]{:S(2)}) %collective-permute-start.1) | collective-permute-done | bytes 65568 | tf_op jit(solution)/shard_map/ppermute | solution.py:179
  37.8 0.6 gather_fusion
  38.8 1.3 %collective-permute-start.3 = (f32[512,128]{1,0:T(8,128)S(1)}, f32[512,128]{1,0:T(8,128)S(1)}, u32[]{:S(2)}, u32[]{:S(2)}) collective-permute-start(f32[512,128]{1,0:T(8,128)S(1)} %broadcast_select_fusion), channel_id=1, source_target_pairs={{0,2},{1,3},{2,4},{3,5},{4,6},{5,7},{8,10},{9,11},{10,12},{11,13},... | collective-permute-start | bytes 786440 | tf_op jit(solution)/shard_map/ppermute | solution.py:196
  40.3 3.8 %collective-permute-start.8 = (f32[512,128]{1,0:T(8,128)S(1)}, f32[512,128]{1,0:T(8,128)S(1)}, u32[]{:S(2)}, u32[]{:S(2)}) collective-permute-start(f32[512,128]{1,0:T(8,128)S(1)} %broadcast_select_fusion), channel_id=1, source_target_pairs={{6,0},{7,1},{14,8},{15,9},{22,16},{23,17},{30,24},{31,25}} | collective-permute-start | bytes 786440 | tf_op jit(solution)/shard_map/ppermute | solution.py:197
  44.1 1.3 %collective-permute-start.7 = (f32[512,128]{1,0:T(8,128)S(1)}, f32[512,128]{1,0:T(8,128)S(1)}, u32[]{:S(2)}, u32[]{:S(2)}) collective-permute-start(f32[512,128]{1,0:T(8,128)S(1)} %broadcast_select_fusion), channel_id=1, source_target_pairs={{4,0},{5,1},{6,2},{7,3},{12,8},{13,9},{14,10},{15,11},{20,16},{21,... | collective-permute-start | bytes 786440 | tf_op jit(solution)/shard_map/ppermute | solution.py:197
  45.4 2.2 %collective-permute-start.6 = (f32[512,128]{1,0:T(8,128)S(1)}, f32[512,128]{1,0:T(8,128)S(1)}, u32[]{:S(2)}, u32[]{:S(2)}) collective-permute-start(f32[512,128]{1,0:T(8,128)S(1)} %broadcast_select_fusion), channel_id=1, source_target_pairs={{2,0},{3,1},{4,2},{5,3},{6,4},{7,5},{10,8},{11,9},{12,10},{13,11},... | collective-permute-start | bytes 786440 | tf_op jit(solution)/shard_map/ppermute | solution.py:197
  47.6 1.3 %collective-permute-start.4 = (f32[512,128]{1,0:T(8,128)S(1)}, f32[512,128]{1,0:T(8,128)S(1)}, u32[]{:S(2)}, u32[]{:S(2)}) collective-permute-start(f32[512,128]{1,0:T(8,128)S(1)} %broadcast_select_fusion), channel_id=1, source_target_pairs={{0,4},{1,5},{2,6},{3,7},{8,12},{9,13},{10,14},{11,15},{16,20},{17,... | collective-permute-start | bytes 786440 | tf_op jit(solution)/shard_map/ppermute | solution.py:196
  49.0 0.9 select_dynamic-update-slice_fusion
  49.9 1.5 %collective-permute-start.5 = (f32[512,128]{1,0:T(8,128)S(1)}, f32[512,128]{1,0:T(8,128)S(1)}, u32[]{:S(2)}, u32[]{:S(2)}) collective-permute-start(f32[512,128]{1,0:T(8,128)S(1)} %broadcast_select_fusion), channel_id=1, source_target_pairs={{0,6},{1,7},{8,14},{9,15},{16,22},{17,23},{24,30},{25,31}} | collective-permute-start | bytes 786440 | tf_op jit(solution)/shard_map/ppermute | solution.py:196
  51.3 0.7 bitcast_dynamic-update-slice_fusion.5
  52.1 17.5 %collective-permute-done.4 = f32[512,128]{1,0:T(8,128)S(1)} collective-permute-done((f32[512,128]{1,0:T(8,128)S(1)}, f32[512,128]{1,0:T(8,128)S(1)}, u32[]{:S(2)}, u32[]{:S(2)}) %collective-permute-start.4) | collective-permute-done | bytes 262176 | tf_op jit(solution)/shard_map/ppermute | solution.py:196
  69.5 0.7 bitcast_dynamic-update-slice_fusion.4
  70.3 0.7 bitcast_dynamic-update-slice_fusion.3
  71.0 0.7 bitcast_dynamic-update-slice_fusion.2
  71.7 0.7 bitcast_dynamic-update-slice_fusion.1
  72.5 0.7 bitcast_dynamic-update-slice_fusion.mine_hbm
  73.2 0.5 collective-permute-start.9
  73.7 2.3 %select_reduce_fusion.inv_ref = s32[2048]{0:T(1024)} fusion(s32[2048]{0:T(1024)S(1)} %copy-done.1), kind=kLoop, calls=%fused_computation.1 | loop fusion | flops 12580864 | bytes 16384 | tf_op jit(solution)/shard_map/reduce_sum | solution.py:79
  76.2 1.0 %copy.39 = f32[4,512,2,32]{3,2,1,0:T(2,128)S(1)} copy(f32[4,512,2,32]{1,3,0,2:T(8,128)S(1)} %pad_maximum_fusion.1) | data formatting | bytes 1048576 | tf_op jit(solution)/shard_map/stack | solution.py:223
  77.6 1.0 pad_maximum_fusion.l_ref
  78.5 7.2 %shard_map.47 = f32[4096,128]{1,0:T(8,128)} custom-call(s32[2048]{0:T(1024)} %select_reduce_fusion.inv_ref, f32[7,512,128]{2,1,0:T(8,128)} %bitcast_dynamic-update-slice_fusion.mine_hbm, f32[7,512,128]{2,1,0:T(8,128)} %collective-permute-done.9.other_hbm), custom_call_target="tpu_custom_call" | custom-call | tf_op jit(solution)/shard_map/pallas_call | solution.py:129
  85.8 1.9 %copy.44 = f32[4096,128]{0,1:T(8,128)S(1)} copy(f32[4096,128]{1,0:T(8,128)} %shard_map.47) | data formatting | bytes 4194304 | tf_op jit(solution)/shard_map/pallas_call | solution.py:129
  88.0 0.4 maximum_bitcast_fusion.o_ref
  88.4 14.8 %shard_map.48 = bf16[4,512,2,4096]{3,2,1,0:T(2,128)(2,1)} custom-call(bf16[4,1024,96]{2,1,0:T(8,128)(2,1)S(1)} %pad_maximum_fusion.l_ref, bf16[4,96,4096]{2,1,0:T(8,128)(2,1)S(1)} %maximum_bitcast_fusion.o_ref), custom_call_target="tpu_custom_call" | custom-call | tf_op jit(solution)/shard_map/pallas_call | solution.py:160
  (36 shorter events, 1.9 us)
Async XLA Ops:
  0.0 3.3 %copy-start = (f32[8,8192]{1,0:T(8,128)S(1)}, f32[8,8192]{1,0:T(8,128)}, u32[]{:S(2)}) copy-start(f32[8,8192]{1,0:T(8,128)} %param.5) | copy-start | bytes 786436
  31.3 4.1 %collective-permute-start.2 = (f32[128,4,2,16]{0,3,2,1:T(8,128)S(1)}, f32[128,4,2,16]{0,3,2,1:T(8,128)S(1)}, u32[]{:S(2)}, u32[]{:S(2)}) collective-permute-start(f32[128,4,2,16]{0,3,2,1:T(8,128)S(1)} %bitcast.81), channel_id=1, source_target_pairs={{0,24},{8,0},{16,8},{24,16},{1,25},{9,1},{17,9},{25,17},{2,26},{10... | collective-permute-start | bytes 196616 | tf_op jit(solution)/shard_map/ppermute | solution.py:179
  31.6 5.1 %collective-permute-start = (f32[128,4,2,16]{0,3,2,1:T(8,128)S(1)}, f32[128,4,2,16]{0,3,2,1:T(8,128)S(1)}, u32[]{:S(2)}, u32[]{:S(2)}) collective-permute-start(f32[128,4,2,16]{0,3,2,1:T(8,128)S(1)} %bitcast.82), channel_id=1, source_target_pairs={{0,8},{8,16},{16,24},{24,0},{1,9},{9,17},{17,25},{25,1},{2,10},{10... | collective-permute-start | bytes 196616 | tf_op jit(solution)/shard_map/ppermute | solution.py:179
  33.8 3.9 %collective-permute-start.1 = (f32[128,4,2,16]{0,3,2,1:T(8,128)S(1)}, f32[128,4,2,16]{0,3,2,1:T(8,128)S(1)}, u32[]{:S(2)}, u32[]{:S(2)}) collective-permute-start(f32[128,4,2,16]{0,3,2,1:T(8,128)S(1)} %bitcast.83), channel_id=1, source_target_pairs={{0,16},{8,24},{16,0},{24,8},{1,17},{9,25},{17,1},{25,9},{2,18},{10... | collective-permute-start | bytes 196616 | tf_op jit(solution)/shard_map/ppermute | solution.py:179
  38.8 11.0 %collective-permute-start.3 = (f32[512,128]{1,0:T(8,128)S(1)}, f32[512,128]{1,0:T(8,128)S(1)}, u32[]{:S(2)}, u32[]{:S(2)}) collective-permute-start(f32[512,128]{1,0:T(8,128)S(1)} %broadcast_select_fusion), channel_id=1, source_target_pairs={{0,2},{1,3},{2,4},{3,5},{4,6},{5,7},{8,10},{9,11},{10,12},{11,13},... | collective-permute-start | bytes 786440 | tf_op jit(solution)/shard_map/ppermute | solution.py:196
  40.2 33.4 %copy-start.1 = (s32[2048]{0:T(1024)S(1)}, s32[2048]{0:T(1024)}, u32[]{:S(2)}) copy-start(s32[2048]{0:T(1024)} %param.7) | copy-start | bytes 24580
  40.3 32.2 %collective-permute-start.8 = (f32[512,128]{1,0:T(8,128)S(1)}, f32[512,128]{1,0:T(8,128)S(1)}, u32[]{:S(2)}, u32[]{:S(2)}) collective-permute-start(f32[512,128]{1,0:T(8,128)S(1)} %broadcast_select_fusion), channel_id=1, source_target_pairs={{6,0},{7,1},{14,8},{15,9},{22,16},{23,17},{30,24},{31,25}} | collective-permute-start | bytes 786440 | tf_op jit(solution)/shard_map/ppermute | solution.py:197
  44.1 27.7 %collective-permute-start.7 = (f32[512,128]{1,0:T(8,128)S(1)}, f32[512,128]{1,0:T(8,128)S(1)}, u32[]{:S(2)}, u32[]{:S(2)}) collective-permute-start(f32[512,128]{1,0:T(8,128)S(1)} %broadcast_select_fusion), channel_id=1, source_target_pairs={{4,0},{5,1},{6,2},{7,3},{12,8},{13,9},{14,10},{15,11},{20,16},{21,... | collective-permute-start | bytes 786440 | tf_op jit(solution)/shard_map/ppermute | solution.py:197
  45.4 25.6 %collective-permute-start.6 = (f32[512,128]{1,0:T(8,128)S(1)}, f32[512,128]{1,0:T(8,128)S(1)}, u32[]{:S(2)}, u32[]{:S(2)}) collective-permute-start(f32[512,128]{1,0:T(8,128)S(1)} %broadcast_select_fusion), channel_id=1, source_target_pairs={{2,0},{3,1},{4,2},{5,3},{6,4},{7,5},{10,8},{11,9},{12,10},{13,11},... | collective-permute-start | bytes 786440 | tf_op jit(solution)/shard_map/ppermute | solution.py:197
  47.6 22.0 %collective-permute-start.4 = (f32[512,128]{1,0:T(8,128)S(1)}, f32[512,128]{1,0:T(8,128)S(1)}, u32[]{:S(2)}, u32[]{:S(2)}) collective-permute-start(f32[512,128]{1,0:T(8,128)S(1)} %broadcast_select_fusion), channel_id=1, source_target_pairs={{0,4},{1,5},{2,6},{3,7},{8,12},{9,13},{10,14},{11,15},{16,20},{17,... | collective-permute-start | bytes 786440 | tf_op jit(solution)/shard_map/ppermute | solution.py:196
  49.9 20.4 %collective-permute-start.5 = (f32[512,128]{1,0:T(8,128)S(1)}, f32[512,128]{1,0:T(8,128)S(1)}, u32[]{:S(2)}, u32[]{:S(2)}) collective-permute-start(f32[512,128]{1,0:T(8,128)S(1)} %broadcast_select_fusion), channel_id=1, source_target_pairs={{0,6},{1,7},{8,14},{9,15},{16,22},{17,23},{24,30},{25,31}} | collective-permute-start | bytes 786440 | tf_op jit(solution)/shard_map/ppermute | solution.py:196
  73.2 5.4 %collective-permute-start.9 = (f32[7,512,128]{2,1,0:T(8,128)}, f32[7,512,128]{2,1,0:T(8,128)}, u32[]{:S(2)}, u32[]{:S(2)}) collective-permute-start(f32[7,512,128]{2,1,0:T(8,128)} %bitcast_dynamic-update-slice_fusion.mine_hbm), channel_id=1, source_target_pairs={{0,1},{1,0},{2,3},{3,2},{4,5},{5,4},{6,7},{7,6},{8,9},{9,8},{10,11... | collective-permute-start | bytes 5505032 | tf_op jit(solution)/shard_map/ppermute | solution.py:199

commit v11 on v9

--- a/solution.py
+++ b/solution.py
@@ -120,7 +120,7 @@
         o_ref[pl.ds(2 * a, 2), :] = e_ref[pl.ds(src, 2), :]
         return carry
 
-    lax.fori_loop(0, inv_ref.shape[0], body, 0, unroll=8)
+    lax.fori_loop(0, inv_ref.shape[0], body, 0, unroll=16)
 
 
 def permute_pairs(mine, other, inverse):
@@ -229,7 +229,7 @@
     o1, o2 = split2(ordered)
     lcat = jnp.concatenate([la, la, lb], axis=-1)
     rhs = jnp.concatenate([o1, o2, o1], axis=-1).transpose(0, 2, 1)
-    result = correlate(lcat, rhs, min(256, slots_local))
+    result = correlate(lcat, rhs, min(512, slots_local))
     return result
 
 

time: 102 us -> 101 us (level)
  no operation moved by 1% of the time
where the time goes in v11:
time: 101 us; the launch traced here: 100 us
  Pallas kernels  44.9 us (44%)
  starting transfers between devices  21.5 us (21%)
  waiting for transfers between devices  12 us (12%)
  other arithmetic  11.4 us (11%)
  local copies, waits for them, and re-layouts  10.2 us (10%)
    pallas_call x1, Pallas kernels, frame_products(): pl.pallas_call(_frame_kernel, grid=(steps,), in_specs=[pl.BlockSpec((rows...  23.7 us
    pallas_call x1, Pallas kernels, correlate(): pl.pallas_call(_corr_kernel, grid=(chans, slots // block_rows), in_specs=...  14.7 us
    ppermute x3, starting transfers between devices, gather_blocks(): r = lax.ppermute(r, 'blk', right)  12.3 us
    pallas_call x1, Pallas kernels, permute_pairs(): pl.pallas_call(_perm_kernel, grid_spec=pltpu.PrefetchScalarGridSpec(num_s...  6.51 us
    ppermute x3, starting transfers between devices, exchange_channels(): part = lax.ppermute(part, 'grp', [(j, (j + d) % grp) for j in range(grp)])  5.18 us
    ppermute x3, waiting for transfers between devices, gather_blocks(): r = lax.ppermute(r, 'blk', right)  5.17 us
    ppermute x3, starting transfers between devices, gather_blocks(): l = lax.ppermute(l, 'blk', left)  4.05 us
    ppermute x3, waiting for transfers between devices, exchange_channels(): part = lax.ppermute(part, 'grp', [(j, (j + d) % grp) for j in range(grp)])  3.85 us
  transfers between devices with their start and end apart: 10, of which 6 were waited for; matrix products, arithmetic and copies ran while one was open for 10% of the time, Pallas kernels for 0%

profile of v11, /device:TPU:0, one launch (start us, length us, event | category | flops | bytes accessed | tf_op | source)
XLA Modules:
  0.0 100.3 jit_solution(10607328550772084595)
XLA Ops:
  0.0 3.2 %cosine_convert_fusion = (bf16[16,8192]{1,0:T(8,128)(2,1)S(1)}, bf16[16,8192]{1,0:T(8,128)(2,1)S(1)}) fusion(s32[16]{0:T(128)} %param.6), kind=kLoop, calls=%fused_computation.17 | loop fusion | flops 2228224 | bytes 524352 | tf_op jit(solution)/shard_map/convert
  3.3 2.7 %multiply_convert_fusion = bf16[8,32,8192]{2,1,0:T(8,128)(2,1)} fusion(f32[32,8192]{1,0:T(8,128)S(1)} %maximum_convert_fusion, f32[8,8192]{1,0:T(8,128)S(1)} %copy-done), kind=kLoop, calls=%fused_computation.3 | loop fusion | flops 4194304 | bytes 5505024 | tf_op jit(solution)/shard_map/convert_element_type | solution.py:71
  5.9 23.7 %shard_map.46 = f32[16,128,32]{2,1,0:T(8,128)} custom-call(bf16[128,188416]{1,0:T(8,128)(2,1)} %v_ref.1, bf16[256,8192]{1,0:T(8,128)(2,1)} %bitcast.75), custom_call_target="tpu_custom_call" | custom-call | tf_op jit(solution)/shard_map/pallas_call | solution.py:51
  29.7 1.5 %copy.32 = f32[16,128,32]{1,2,0:T(8,128)S(1)} copy(f32[16,128,32]{2,1,0:T(8,128)} %shard_map.46) | data formatting | bytes 524288 | tf_op jit(solution)/shard_map/pallas_call | solution.py:51
  31.3 4.0 %collective-permute-start.2 = (f32[128,4,2,16]{0,3,2,1:T(8,128)S(1)}, f32[128,4,2,16]{0,3,2,1:T(8,128)S(1)}, u32[]{:S(2)}, u32[]{:S(2)}) collective-permute-start(f32[128,4,2,16]{0,3,2,1:T(8,128)S(1)} %bitcast.81), channel_id=1, source_target_pairs={{0,24},{8,0},{16,8},{24,16},{1,25},{9,1},{17,9},{25,17},{2,26},{10... | collective-permute-start | bytes 196616 | tf_op jit(solution)/shard_map/ppermute | solution.py:179
  35.4 1.1 %collective-permute-start.1 = (f32[128,4,2,16]{0,3,2,1:T(8,128)S(1)}, f32[128,4,2,16]{0,3,2,1:T(8,128)S(1)}, u32[]{:S(2)}, u32[]{:S(2)}) collective-permute-start(f32[128,4,2,16]{0,3,2,1:T(8,128)S(1)} %bitcast.83), channel_id=1, source_target_pairs={{0,16},{8,24},{16,0},{24,8},{1,17},{9,25},{17,1},{25,9},{2,18},{10... | collective-permute-start | bytes 196616 | tf_op jit(solution)/shard_map/ppermute | solution.py:179
  36.7 0.7 collective-permute-done.2
  37.3 3.2 %collective-permute-done = f32[128,4,2,16]{0,3,2,1:T(8,128)S(1)} collective-permute-done((f32[128,4,2,16]{0,3,2,1:T(8,128)S(1)}, f32[128,4,2,16]{0,3,2,1:T(8,128)S(1)}, u32[]{:S(2)}, u32[]{:S(2)}) %collective-permute-start) | collective-permute-done | bytes 65568 | tf_op jit(solution)/shard_map/ppermute | solution.py:179
  40.6 0.6 gather_fusion
  41.6 3.5 %collective-permute-start.3 = (f32[512,128]{1,0:T(8,128)S(1)}, f32[512,128]{1,0:T(8,128)S(1)}, u32[]{:S(2)}, u32[]{:S(2)}) collective-permute-start(f32[512,128]{1,0:T(8,128)S(1)} %broadcast_select_fusion), channel_id=1, source_target_pairs={{0,2},{1,3},{2,4},{3,5},{4,6},{5,7},{8,10},{9,11},{10,12},{11,13},... | collective-permute-start | bytes 786440 | tf_op jit(solution)/shard_map/ppermute | solution.py:198
  45.1 1.3 %collective-permute-start.6 = (f32[512,128]{1,0:T(8,128)S(1)}, f32[512,128]{1,0:T(8,128)S(1)}, u32[]{:S(2)}, u32[]{:S(2)}) collective-permute-start(f32[512,128]{1,0:T(8,128)S(1)} %broadcast_select_fusion), channel_id=1, source_target_pairs={{2,0},{3,1},{4,2},{5,3},{6,4},{7,5},{10,8},{11,9},{12,10},{13,11},... | collective-permute-start | bytes 786440 | tf_op jit(solution)/shard_map/ppermute | solution.py:199
  46.4 2.8 %collective-permute-done.3 = f32[512,128]{1,0:T(8,128)S(1)} collective-permute-done((f32[512,128]{1,0:T(8,128)S(1)}, f32[512,128]{1,0:T(8,128)S(1)}, u32[]{:S(2)}, u32[]{:S(2)}) %collective-permute-start.3) | collective-permute-done | bytes 262176 | tf_op jit(solution)/shard_map/ppermute | solution.py:198
  49.2 4.4 %collective-permute-start.4 = (f32[512,128]{1,0:T(8,128)S(1)}, f32[512,128]{1,0:T(8,128)S(1)}, u32[]{:S(2)}, u32[]{:S(2)}) collective-permute-start(f32[512,128]{1,0:T(8,128)S(1)} %collective-permute-done.3), channel_id=1, source_target_pairs={{0,2},{1,3},{2,4},{3,5},{4,6},{5,7},{8,10},{9,11},{10,12},{11,13},... | collective-permute-start | bytes 786440 | tf_op jit(solution)/shard_map/ppermute | solution.py:198
  53.9 1.3 %collective-permute-start.7 = (f32[512,128]{1,0:T(8,128)S(1)}, f32[512,128]{1,0:T(8,128)S(1)}, u32[]{:S(2)}, u32[]{:S(2)}) collective-permute-start(f32[512,128]{1,0:T(8,128)S(1)} %collective-permute-done.6), channel_id=1, source_target_pairs={{2,0},{3,1},{4,2},{5,3},{6,4},{7,5},{10,8},{11,9},{12,10},{13,11},... | collective-permute-start | bytes 786440 | tf_op jit(solution)/shard_map/ppermute | solution.py:199
  55.2 0.9 select_dynamic-update-slice_fusion
  56.0 1.4 %collective-permute-done.4 = f32[512,128]{1,0:T(8,128)S(1)} collective-permute-done((f32[512,128]{1,0:T(8,128)S(1)}, f32[512,128]{1,0:T(8,128)S(1)}, u32[]{:S(2)}, u32[]{:S(2)}) %collective-permute-start.4) | collective-permute-done | bytes 262176 | tf_op jit(solution)/shard_map/ppermute | solution.py:198
  57.5 4.4 %collective-permute-start.5 = (f32[512,128]{1,0:T(8,128)S(1)}, f32[512,128]{1,0:T(8,128)S(1)}, u32[]{:S(2)}, u32[]{:S(2)}) collective-permute-start(f32[512,128]{1,0:T(8,128)S(1)} %collective-permute-done.4), channel_id=1, source_target_pairs={{0,2},{1,3},{2,4},{3,5},{4,6},{5,7},{8,10},{9,11},{10,12},{11,13},... | collective-permute-start | bytes 786440 | tf_op jit(solution)/shard_map/ppermute | solution.py:198
  61.9 0.7 bitcast_dynamic-update-slice_fusion.5
  62.6 1.5 %collective-permute-start.8 = (f32[512,128]{1,0:T(8,128)S(1)}, f32[512,128]{1,0:T(8,128)S(1)}, u32[]{:S(2)}, u32[]{:S(2)}) collective-permute-start(f32[512,128]{1,0:T(8,128)S(1)} %collective-permute-done.7), channel_id=1, source_target_pairs={{2,0},{3,1},{4,2},{5,3},{6,4},{7,5},{10,8},{11,9},{12,10},{13,11},... | collective-permute-start | bytes 786440 | tf_op jit(solution)/shard_map/ppermute | solution.py:199
  64.1 0.7 bitcast_dynamic-update-slice_fusion.4
  64.8 0.9 collective-permute-done.5
  65.7 0.7 bitcast_dynamic-update-slice_fusion.3
  66.5 0.7 bitcast_dynamic-update-slice_fusion.2
  67.2 0.7 bitcast_dynamic-update-slice_fusion.1
  67.9 3.0 %collective-permute-done.8 = f32[512,128]{1,0:T(8,128)S(1)} collective-permute-done((f32[512,128]{1,0:T(8,128)S(1)}, f32[512,128]{1,0:T(8,128)S(1)}, u32[]{:S(2)}, u32[]{:S(2)}) %collective-permute-start.8) | collective-permute-done | bytes 262176 | tf_op jit(solution)/shard_map/ppermute | solution.py:199
  70.9 0.7 bitcast_dynamic-update-slice_fusion.mine_hbm
  71.6 2.3 %select_reduce_fusion.inv_ref = s32[2048]{0:T(1024)} fusion(s32[2048]{0:T(1024)S(1)} %copy-done.1), kind=kLoop, calls=%fused_computation.1 | loop fusion | flops 12580864 | bytes 16384 | tf_op jit(solution)/shard_map/reduce_sum | solution.py:79
  74.1 1.0 %copy.39 = f32[4,512,2,32]{3,2,1,0:T(2,128)S(1)} copy(f32[4,512,2,32]{1,3,0,2:T(8,128)S(1)} %pad_maximum_fusion.1) | data formatting | bytes 1048576 | tf_op jit(solution)/shard_map/stack | solution.py:227
  75.5 1.0 pad_maximum_fusion.l_ref
  76.5 6.5 %shard_map.47 = f32[4096,128]{1,0:T(8,128)} custom-call(s32[2048]{0:T(1024)} %select_reduce_fusion.inv_ref, f32[7,512,128]{2,1,0:T(8,128)} %bitcast_dynamic-update-slice_fusion.mine_hbm, f32[7,512,128]{2,1,0:T(8,128)} %collective-permute-done.9.other_hbm), custom_call_target="tpu_custom_call" | custom-call | tf_op jit(solution)/shard_map/pallas_call | solution.py:129
  83.0 1.9 %copy.44 = f32[4096,128]{0,1:T(8,128)S(1)} copy(f32[4096,128]{1,0:T(8,128)} %shard_map.47) | data formatting | bytes 4194304 | tf_op jit(solution)/shard_map/pallas_call | solution.py:129
  85.6 14.7 %shard_map.48 = bf16[4,512,2,4096]{3,2,1,0:T(2,128)(2,1)} custom-call(bf16[4,1024,96]{2,1,0:T(8,128)(2,1)S(1)} %pad_maximum_fusion.l_ref, bf16[4,96,4096]{2,1,0:T(8,128)(2,1)S(1)} %maximum_bitcast_fusion.o_ref), custom_call_target="tpu_custom_call" | custom-call | tf_op jit(solution)/shard_map/pallas_call | solution.py:160
  (36 shorter events, 2.2 us)
Async XLA Ops:
  0.0 3.3 %copy-start = (f32[8,8192]{1,0:T(8,128)S(1)}, f32[8,8192]{1,0:T(8,128)}, u32[]{:S(2)}) copy-start(f32[8,8192]{1,0:T(8,128)} %param.5) | copy-start | bytes 786436
  31.3 6.0 %collective-permute-start.2 = (f32[128,4,2,16]{0,3,2,1:T(8,128)S(1)}, f32[128,4,2,16]{0,3,2,1:T(8,128)S(1)}, u32[]{:S(2)}, u32[]{:S(2)}) collective-permute-start(f32[128,4,2,16]{0,3,2,1:T(8,128)S(1)} %bitcast.81), channel_id=1, source_target_pairs={{0,24},{8,0},{16,8},{24,16},{1,25},{9,1},{17,9},{25,17},{2,26},{10... | collective-permute-start | bytes 196616 | tf_op jit(solution)/shard_map/ppermute | solution.py:179
  35.3 5.2 %collective-permute-start = (f32[128,4,2,16]{0,3,2,1:T(8,128)S(1)}, f32[128,4,2,16]{0,3,2,1:T(8,128)S(1)}, u32[]{:S(2)}, u32[]{:S(2)}) collective-permute-start(f32[128,4,2,16]{0,3,2,1:T(8,128)S(1)} %bitcast.82), channel_id=1, source_target_pairs={{0,8},{8,16},{16,24},{24,0},{1,9},{9,17},{17,25},{25,1},{2,10},{10... | collective-permute-start | bytes 196616 | tf_op jit(solution)/shard_map/ppermute | solution.py:179
  35.4 5.1 %collective-permute-start.1 = (f32[128,4,2,16]{0,3,2,1:T(8,128)S(1)}, f32[128,4,2,16]{0,3,2,1:T(8,128)S(1)}, u32[]{:S(2)}, u32[]{:S(2)}) collective-permute-start(f32[128,4,2,16]{0,3,2,1:T(8,128)S(1)} %bitcast.83), channel_id=1, source_target_pairs={{0,16},{8,24},{16,0},{24,8},{1,17},{9,25},{17,1},{25,9},{2,18},{10... | collective-permute-start | bytes 196616 | tf_op jit(solution)/shard_map/ppermute | solution.py:179
  41.6 7.6 %collective-permute-start.3 = (f32[512,128]{1,0:T(8,128)S(1)}, f32[512,128]{1,0:T(8,128)S(1)}, u32[]{:S(2)}, u32[]{:S(2)}) collective-permute-start(f32[512,128]{1,0:T(8,128)S(1)} %broadcast_select_fusion), channel_id=1, source_target_pairs={{0,2},{1,3},{2,4},{3,5},{4,6},{5,7},{8,10},{9,11},{10,12},{11,13},... | collective-permute-start | bytes 786440 | tf_op jit(solution)/shard_map/ppermute | solution.py:198
  45.1 8.8 %collective-permute-start.6 = (f32[512,128]{1,0:T(8,128)S(1)}, f32[512,128]{1,0:T(8,128)S(1)}, u32[]{:S(2)}, u32[]{:S(2)}) collective-permute-start(f32[512,128]{1,0:T(8,128)S(1)} %broadcast_select_fusion), channel_id=1, source_target_pairs={{2,0},{3,1},{4,2},{5,3},{6,4},{7,5},{10,8},{11,9},{12,10},{13,11},... | collective-permute-start | bytes 786440 | tf_op jit(solution)/shard_map/ppermute | solution.py:199
  49.2 8.3 %collective-permute-start.4 = (f32[512,128]{1,0:T(8,128)S(1)}, f32[512,128]{1,0:T(8,128)S(1)}, u32[]{:S(2)}, u32[]{:S(2)}) collective-permute-start(f32[512,128]{1,0:T(8,128)S(1)} %collective-permute-done.3), channel_id=1, source_target_pairs={{0,2},{1,3},{2,4},{3,5},{4,6},{5,7},{8,10},{9,11},{10,12},{11,13},... | collective-permute-start | bytes 786440 | tf_op jit(solution)/shard_map/ppermute | solution.py:198
  53.7 17.9 %copy-start.1 = (s32[2048]{0:T(1024)S(1)}, s32[2048]{0:T(1024)}, u32[]{:S(2)}) copy-start(s32[2048]{0:T(1024)} %param.7) | copy-start | bytes 24580
  53.9 8.7 %collective-permute-start.7 = (f32[512,128]{1,0:T(8,128)S(1)}, f32[512,128]{1,0:T(8,128)S(1)}, u32[]{:S(2)}, u32[]{:S(2)}) collective-permute-start(f32[512,128]{1,0:T(8,128)S(1)} %collective-permute-done.6), channel_id=1, source_target_pairs={{2,0},{3,1},{4,2},{5,3},{6,4},{7,5},{10,8},{11,9},{12,10},{13,11},... | collective-permute-start | bytes 786440 | tf_op jit(solution)/shard_map/ppermute | solution.py:199
  57.5 8.3 %collective-permute-start.5 = (f32[512,128]{1,0:T(8,128)S(1)}, f32[512,128]{1,0:T(8,128)S(1)}, u32[]{:S(2)}, u32[]{:S(2)}) collective-permute-start(f32[512,128]{1,0:T(8,128)S(1)} %collective-permute-done.4), channel_id=1, source_target_pairs={{0,2},{1,3},{2,4},{3,5},{4,6},{5,7},{8,10},{9,11},{10,12},{11,13},... | collective-permute-start | bytes 786440 | tf_op jit(solution)/shard_map/ppermute | solution.py:198
  62.6 8.3 %collective-permute-start.8 = (f32[512,128]{1,0:T(8,128)S(1)}, f32[512,128]{1,0:T(8,128)S(1)}, u32[]{:S(2)}, u32[]{:S(2)}) collective-permute-start(f32[512,128]{1,0:T(8,128)S(1)} %collective-permute-done.7), channel_id=1, source_target_pairs={{2,0},{3,1},{4,2},{5,3},{6,4},{7,5},{10,8},{11,9},{12,10},{13,11},... | collective-permute-start | bytes 786440 | tf_op jit(solution)/shard_map/ppermute | solution.py:199
  71.6 4.9 %collective-permute-start.9 = (f32[7,512,128]{2,1,0:T(8,128)}, f32[7,512,128]{2,1,0:T(8,128)}, u32[]{:S(2)}, u32[]{:S(2)}) collective-permute-start(f32[7,512,128]{2,1,0:T(8,128)} %bitcast_dynamic-update-slice_fusion.mine_hbm), channel_id=1, source_target_pairs={{0,1},{1,0},{2,3},{3,2},{4,5},{5,4},{6,7},{7,6},{8,9},{9,8},{10,11... | collective-permute-start | bytes 5505032 | tf_op jit(solution)/shard_map/ppermute | solution.py:203

commit v12 on v11

--- a/solution.py
+++ b/solution.py
@@ -70,7 +70,7 @@
     cols = twiddle.shape[0]
     weights = (filter_taps[:, None, :] * twiddle[None, :, :]).astype(jnp.bfloat16)
     weights = weights.reshape(tap_count * cols, fft_length)
-    return frame_products(voltages, weights, fft_length, 4, spectra)
+    return frame_products(voltages, weights, fft_length, 6, spectra)
 
 
 def slot_index(antenna_slot_order):

time: 101 us -> 101 us (level)
  no operation moved by 1% of the time
where the time goes in v12:
time: 101 us; the launch traced here: 100 us
  Pallas kernels  44.8 us (44%)
  starting transfers between devices  21.5 us (21%)
  waiting for transfers between devices  12 us (12%)
  other arithmetic  11.4 us (11%)
  local copies, waits for them, and re-layouts  10.2 us (10%)
    pallas_call x1, Pallas kernels, frame_products(): pl.pallas_call(_frame_kernel, grid=(steps,), in_specs=[pl.BlockSpec((rows...  23.6 us
    pallas_call x1, Pallas kernels, correlate(): pl.pallas_call(_corr_kernel, grid=(chans, slots // block_rows), in_specs=...  14.7 us
    ppermute x3, starting transfers between devices, gather_blocks(): r = lax.ppermute(r, 'blk', right)  12.3 us
    pallas_call x1, Pallas kernels, permute_pairs(): pl.pallas_call(_perm_kernel, grid_spec=pltpu.PrefetchScalarGridSpec(num_s...  6.51 us
    ppermute x3, starting transfers between devices, exchange_channels(): part = lax.ppermute(part, 'grp', [(j, (j + d) % grp) for j in range(grp)])  5.18 us
    ppermute x3, waiting for transfers between devices, gather_blocks(): r = lax.ppermute(r, 'blk', right)  5.17 us
    ppermute x3, starting transfers between devices, gather_blocks(): l = lax.ppermute(l, 'blk', left)  4.05 us
    ppermute x3, waiting for transfers between devices, exchange_channels(): part = lax.ppermute(part, 'grp', [(j, (j + d) % grp) for j in range(grp)])  3.85 us
  transfers between devices with their start and end apart: 10, of which 6 were waited for; matrix products, arithmetic and copies ran while one was open for 10% of the time, Pallas kernels for 0%

profile of v12, /device:TPU:0, one launch (start us, length us, event | category | flops | bytes accessed | tf_op | source)
XLA Modules:
  0.0 100.1 jit_solution(17248534114503488559)
XLA Ops:
  0.0 3.2 %cosine_convert_fusion = (bf16[16,8192]{1,0:T(8,128)(2,1)S(1)}, bf16[16,8192]{1,0:T(8,128)(2,1)S(1)}) fusion(s32[16]{0:T(128)} %param.6), kind=kLoop, calls=%fused_computation.17 | loop fusion | flops 2228224 | bytes 524352 | tf_op jit(solution)/shard_map/convert
  3.3 2.7 %multiply_convert_fusion = bf16[8,32,8192]{2,1,0:T(8,128)(2,1)} fusion(f32[32,8192]{1,0:T(8,128)S(1)} %maximum_convert_fusion, f32[8,8192]{1,0:T(8,128)S(1)} %copy-done), kind=kLoop, calls=%fused_computation.3 | loop fusion | flops 4194304 | bytes 5505024 | tf_op jit(solution)/shard_map/convert_element_type | solution.py:71
  5.9 23.6 %shard_map.46 = f32[16,128,32]{2,1,0:T(8,128)} custom-call(bf16[128,188416]{1,0:T(8,128)(2,1)} %v_ref.1, bf16[256,8192]{1,0:T(8,128)(2,1)} %bitcast.75), custom_call_target="tpu_custom_call" | custom-call | tf_op jit(solution)/shard_map/pallas_call | solution.py:51
  29.5 1.5 %copy.32 = f32[16,128,32]{1,2,0:T(8,128)S(1)} copy(f32[16,128,32]{2,1,0:T(8,128)} %shard_map.46) | data formatting | bytes 524288 | tf_op jit(solution)/shard_map/pallas_call | solution.py:51
  31.2 4.0 %collective-permute-start.2 = (f32[128,4,2,16]{0,3,2,1:T(8,128)S(1)}, f32[128,4,2,16]{0,3,2,1:T(8,128)S(1)}, u32[]{:S(2)}, u32[]{:S(2)}) collective-permute-start(f32[128,4,2,16]{0,3,2,1:T(8,128)S(1)} %bitcast.81), channel_id=1, source_target_pairs={{0,24},{8,0},{16,8},{24,16},{1,25},{9,1},{17,9},{25,17},{2,26},{10... | collective-permute-start | bytes 196616 | tf_op jit(solution)/shard_map/ppermute | solution.py:179
  35.2 1.1 %collective-permute-start.1 = (f32[128,4,2,16]{0,3,2,1:T(8,128)S(1)}, f32[128,4,2,16]{0,3,2,1:T(8,128)S(1)}, u32[]{:S(2)}, u32[]{:S(2)}) collective-permute-start(f32[128,4,2,16]{0,3,2,1:T(8,128)S(1)} %bitcast.83), channel_id=1, source_target_pairs={{0,16},{8,24},{16,0},{24,8},{1,17},{9,25},{17,1},{25,9},{2,18},{10... | collective-permute-start | bytes 196616 | tf_op jit(solution)/shard_map/ppermute | solution.py:179
  36.5 0.7 collective-permute-done.2
  37.2 3.2 %collective-permute-done = f32[128,4,2,16]{0,3,2,1:T(8,128)S(1)} collective-permute-done((f32[128,4,2,16]{0,3,2,1:T(8,128)S(1)}, f32[128,4,2,16]{0,3,2,1:T(8,128)S(1)}, u32[]{:S(2)}, u32[]{:S(2)}) %collective-permute-start) | collective-permute-done | bytes 65568 | tf_op jit(solution)/shard_map/ppermute | solution.py:179
  40.4 0.6 gather_fusion
  41.4 3.5 %collective-permute-start.3 = (f32[512,128]{1,0:T(8,128)S(1)}, f32[512,128]{1,0:T(8,128)S(1)}, u32[]{:S(2)}, u32[]{:S(2)}) collective-permute-start(f32[512,128]{1,0:T(8,128)S(1)} %broadcast_select_fusion), channel_id=1, source_target_pairs={{0,2},{1,3},{2,4},{3,5},{4,6},{5,7},{8,10},{9,11},{10,12},{11,13},... | collective-permute-start | bytes 786440 | tf_op jit(solution)/shard_map/ppermute | solution.py:198
  45.0 1.3 %collective-permute-start.6 = (f32[512,128]{1,0:T(8,128)S(1)}, f32[512,128]{1,0:T(8,128)S(1)}, u32[]{:S(2)}, u32[]{:S(2)}) collective-permute-start(f32[512,128]{1,0:T(8,128)S(1)} %broadcast_select_fusion), channel_id=1, source_target_pairs={{2,0},{3,1},{4,2},{5,3},{6,4},{7,5},{10,8},{11,9},{12,10},{13,11},... | collective-permute-start | bytes 786440 | tf_op jit(solution)/shard_map/ppermute | solution.py:199
  46.3 2.8 %collective-permute-done.3 = f32[512,128]{1,0:T(8,128)S(1)} collective-permute-done((f32[512,128]{1,0:T(8,128)S(1)}, f32[512,128]{1,0:T(8,128)S(1)}, u32[]{:S(2)}, u32[]{:S(2)}) %collective-permute-start.3) | collective-permute-done | bytes 262176 | tf_op jit(solution)/shard_map/ppermute | solution.py:198
  49.1 4.4 %collective-permute-start.4 = (f32[512,128]{1,0:T(8,128)S(1)}, f32[512,128]{1,0:T(8,128)S(1)}, u32[]{:S(2)}, u32[]{:S(2)}) collective-permute-start(f32[512,128]{1,0:T(8,128)S(1)} %collective-permute-done.3), channel_id=1, source_target_pairs={{0,2},{1,3},{2,4},{3,5},{4,6},{5,7},{8,10},{9,11},{10,12},{11,13},... | collective-permute-start | bytes 786440 | tf_op jit(solution)/shard_map/ppermute | solution.py:198
  53.7 1.3 %collective-permute-start.7 = (f32[512,128]{1,0:T(8,128)S(1)}, f32[512,128]{1,0:T(8,128)S(1)}, u32[]{:S(2)}, u32[]{:S(2)}) collective-permute-start(f32[512,128]{1,0:T(8,128)S(1)} %collective-permute-done.6), channel_id=1, source_target_pairs={{2,0},{3,1},{4,2},{5,3},{6,4},{7,5},{10,8},{11,9},{12,10},{13,11},... | collective-permute-start | bytes 786440 | tf_op jit(solution)/shard_map/ppermute | solution.py:199
  55.0 0.9 select_dynamic-update-slice_fusion
  55.9 1.4 %collective-permute-done.4 = f32[512,128]{1,0:T(8,128)S(1)} collective-permute-done((f32[512,128]{1,0:T(8,128)S(1)}, f32[512,128]{1,0:T(8,128)S(1)}, u32[]{:S(2)}, u32[]{:S(2)}) %collective-permute-start.4) | collective-permute-done | bytes 262176 | tf_op jit(solution)/shard_map/ppermute | solution.py:198
  57.3 4.4 %collective-permute-start.5 = (f32[512,128]{1,0:T(8,128)S(1)}, f32[512,128]{1,0:T(8,128)S(1)}, u32[]{:S(2)}, u32[]{:S(2)}) collective-permute-start(f32[512,128]{1,0:T(8,128)S(1)} %collective-permute-done.4), channel_id=1, source_target_pairs={{0,2},{1,3},{2,4},{3,5},{4,6},{5,7},{8,10},{9,11},{10,12},{11,13},... | collective-permute-start | bytes 786440 | tf_op jit(solution)/shard_map/ppermute | solution.py:198
  61.7 0.7 bitcast_dynamic-update-slice_fusion.5
  62.4 1.5 %collective-permute-start.8 = (f32[512,128]{1,0:T(8,128)S(1)}, f32[512,128]{1,0:T(8,128)S(1)}, u32[]{:S(2)}, u32[]{:S(2)}) collective-permute-start(f32[512,128]{1,0:T(8,128)S(1)} %collective-permute-done.7), channel_id=1, source_target_pairs={{2,0},{3,1},{4,2},{5,3},{6,4},{7,5},{10,8},{11,9},{12,10},{13,11},... | collective-permute-start | bytes 786440 | tf_op jit(solution)/shard_map/ppermute | solution.py:199
  63.9 0.7 bitcast_dynamic-update-slice_fusion.4
  64.6 0.9 collective-permute-done.5
  65.6 0.7 bitcast_dynamic-update-slice_fusion.3
  66.3 0.7 bitcast_dynamic-update-slice_fusion.2
  67.0 0.7 bitcast_dynamic-update-slice_fusion.1
  67.7 3.0 %collective-permute-done.8 = f32[512,128]{1,0:T(8,128)S(1)} collective-permute-done((f32[512,128]{1,0:T(8,128)S(1)}, f32[512,128]{1,0:T(8,128)S(1)}, u32[]{:S(2)}, u32[]{:S(2)}) %collective-permute-start.8) | collective-permute-done | bytes 262176 | tf_op jit(solution)/shard_map/ppermute | solution.py:199
  70.7 0.7 bitcast_dynamic-update-slice_fusion.mine_hbm
  71.4 2.3 %select_reduce_fusion.inv_ref = s32[2048]{0:T(1024)} fusion(s32[2048]{0:T(1024)S(1)} %copy-done.1), kind=kLoop, calls=%fused_computation.1 | loop fusion | flops 12580864 | bytes 16384 | tf_op jit(solution)/shard_map/reduce_sum | solution.py:79
  74.0 1.0 %copy.39 = f32[4,512,2,32]{3,2,1,0:T(2,128)S(1)} copy(f32[4,512,2,32]{1,3,0,2:T(8,128)S(1)} %pad_maximum_fusion.1) | data formatting | bytes 1048576 | tf_op jit(solution)/shard_map/stack | solution.py:227
  75.3 1.0 pad_maximum_fusion.l_ref
  76.3 6.5 %shard_map.47 = f32[4096,128]{1,0:T(8,128)} custom-call(s32[2048]{0:T(1024)} %select_reduce_fusion.inv_ref, f32[7,512,128]{2,1,0:T(8,128)} %bitcast_dynamic-update-slice_fusion.mine_hbm, f32[7,512,128]{2,1,0:T(8,128)} %collective-permute-done.9.other_hbm), custom_call_target="tpu_custom_call" | custom-call | tf_op jit(solution)/shard_map/pallas_call | solution.py:129
  82.8 1.9 %copy.44 = f32[4096,128]{0,1:T(8,128)S(1)} copy(f32[4096,128]{1,0:T(8,128)} %shard_map.47) | data formatting | bytes 4194304 | tf_op jit(solution)/shard_map/pallas_call | solution.py:129
  85.5 14.7 %shard_map.48 = bf16[4,512,2,4096]{3,2,1,0:T(2,128)(2,1)} custom-call(bf16[4,1024,96]{2,1,0:T(8,128)(2,1)S(1)} %pad_maximum_fusion.l_ref, bf16[4,96,4096]{2,1,0:T(8,128)(2,1)S(1)} %maximum_bitcast_fusion.o_ref), custom_call_target="tpu_custom_call" | custom-call | tf_op jit(solution)/shard_map/pallas_call | solution.py:160
  (36 shorter events, 2.2 us)
Async XLA Ops:
  0.0 3.3 %copy-start = (f32[8,8192]{1,0:T(8,128)S(1)}, f32[8,8192]{1,0:T(8,128)}, u32[]{:S(2)}) copy-start(f32[8,8192]{1,0:T(8,128)} %param.5) | copy-start | bytes 786436
  31.2 6.0 %collective-permute-start.2 = (f32[128,4,2,16]{0,3,2,1:T(8,128)S(1)}, f32[128,4,2,16]{0,3,2,1:T(8,128)S(1)}, u32[]{:S(2)}, u32[]{:S(2)}) collective-permute-start(f32[128,4,2,16]{0,3,2,1:T(8,128)S(1)} %bitcast.81), channel_id=1, source_target_pairs={{0,24},{8,0},{16,8},{24,16},{1,25},{9,1},{17,9},{25,17},{2,26},{10... | collective-permute-start | bytes 196616 | tf_op jit(solution)/shard_map/ppermute | solution.py:179
  35.2 5.2 %collective-permute-start = (f32[128,4,2,16]{0,3,2,1:T(8,128)S(1)}, f32[128,4,2,16]{0,3,2,1:T(8,128)S(1)}, u32[]{:S(2)}, u32[]{:S(2)}) collective-permute-start(f32[128,4,2,16]{0,3,2,1:T(8,128)S(1)} %bitcast.82), channel_id=1, source_target_pairs={{0,8},{8,16},{16,24},{24,0},{1,9},{9,17},{17,25},{25,1},{2,10},{10... | collective-permute-start | bytes 196616 | tf_op jit(solution)/shard_map/ppermute | solution.py:179
  35.2 5.1 %collective-permute-start.1 = (f32[128,4,2,16]{0,3,2,1:T(8,128)S(1)}, f32[128,4,2,16]{0,3,2,1:T(8,128)S(1)}, u32[]{:S(2)}, u32[]{:S(2)}) collective-permute-start(f32[128,4,2,16]{0,3,2,1:T(8,128)S(1)} %bitcast.83), channel_id=1, source_target_pairs={{0,16},{8,24},{16,0},{24,8},{1,17},{9,25},{17,1},{25,9},{2,18},{10... | collective-permute-start | bytes 196616 | tf_op jit(solution)/shard_map/ppermute | solution.py:179
  41.4 7.6 %collective-permute-start.3 = (f32[512,128]{1,0:T(8,128)S(1)}, f32[512,128]{1,0:T(8,128)S(1)}, u32[]{:S(2)}, u32[]{:S(2)}) collective-permute-start(f32[512,128]{1,0:T(8,128)S(1)} %broadcast_select_fusion), channel_id=1, source_target_pairs={{0,2},{1,3},{2,4},{3,5},{4,6},{5,7},{8,10},{9,11},{10,12},{11,13},... | collective-permute-start | bytes 786440 | tf_op jit(solution)/shard_map/ppermute | solution.py:198
  45.0 8.8 %collective-permute-start.6 = (f32[512,128]{1,0:T(8,128)S(1)}, f32[512,128]{1,0:T(8,128)S(1)}, u32[]{:S(2)}, u32[]{:S(2)}) collective-permute-start(f32[512,128]{1,0:T(8,128)S(1)} %broadcast_select_fusion), channel_id=1, source_target_pairs={{2,0},{3,1},{4,2},{5,3},{6,4},{7,5},{10,8},{11,9},{12,10},{13,11},... | collective-permute-start | bytes 786440 | tf_op jit(solution)/shard_map/ppermute | solution.py:199
  49.1 8.3 %collective-permute-start.4 = (f32[512,128]{1,0:T(8,128)S(1)}, f32[512,128]{1,0:T(8,128)S(1)}, u32[]{:S(2)}, u32[]{:S(2)}) collective-permute-start(f32[512,128]{1,0:T(8,128)S(1)} %collective-permute-done.3), channel_id=1, source_target_pairs={{0,2},{1,3},{2,4},{3,5},{4,6},{5,7},{8,10},{9,11},{10,12},{11,13},... | collective-permute-start | bytes 786440 | tf_op jit(solution)/shard_map/ppermute | solution.py:198
  53.6 17.9 %copy-start.1 = (s32[2048]{0:T(1024)S(1)}, s32[2048]{0:T(1024)}, u32[]{:S(2)}) copy-start(s32[2048]{0:T(1024)} %param.7) | copy-start | bytes 24580
  53.7 8.7 %collective-permute-start.7 = (f32[512,128]{1,0:T(8,128)S(1)}, f32[512,128]{1,0:T(8,128)S(1)}, u32[]{:S(2)}, u32[]{:S(2)}) collective-permute-start(f32[512,128]{1,0:T(8,128)S(1)} %collective-permute-done.6), channel_id=1, source_target_pairs={{2,0},{3,1},{4,2},{5,3},{6,4},{7,5},{10,8},{11,9},{12,10},{13,11},... | collective-permute-start | bytes 786440 | tf_op jit(solution)/shard_map/ppermute | solution.py:199
  57.3 8.3 %collective-permute-start.5 = (f32[512,128]{1,0:T(8,128)S(1)}, f32[512,128]{1,0:T(8,128)S(1)}, u32[]{:S(2)}, u32[]{:S(2)}) collective-permute-start(f32[512,128]{1,0:T(8,128)S(1)} %collective-permute-done.4), channel_id=1, source_target_pairs={{0,2},{1,3},{2,4},{3,5},{4,6},{5,7},{8,10},{9,11},{10,12},{11,13},... | collective-permute-start | bytes 786440 | tf_op jit(solution)/shard_map/ppermute | solution.py:198
  62.4 8.3 %collective-permute-start.8 = (f32[512,128]{1,0:T(8,128)S(1)}, f32[512,128]{1,0:T(8,128)S(1)}, u32[]{:S(2)}, u32[]{:S(2)}) collective-permute-start(f32[512,128]{1,0:T(8,128)S(1)} %collective-permute-done.7), channel_id=1, source_target_pairs={{2,0},{3,1},{4,2},{5,3},{6,4},{7,5},{10,8},{11,9},{12,10},{13,11},... | collective-permute-start | bytes 786440 | tf_op jit(solution)/shard_map/ppermute | solution.py:199
  71.4 4.9 %collective-permute-start.9 = (f32[7,512,128]{2,1,0:T(8,128)}, f32[7,512,128]{2,1,0:T(8,128)}, u32[]{:S(2)}, u32[]{:S(2)}) collective-permute-start(f32[7,512,128]{2,1,0:T(8,128)} %bitcast_dynamic-update-slice_fusion.mine_hbm), channel_id=1, source_target_pairs={{0,1},{1,0},{2,3},{3,2},{4,5},{5,4},{6,7},{7,6},{8,9},{9,8},{10,11... | collective-permute-start | bytes 5505032 | tf_op jit(solution)/shard_map/ppermute | solution.py:203
